TPU v7x, 128 devices: a whole 4x4x4 slice. The times are simulated.
128 devices in a mesh: slab: 8 (over z_lo, x), tile: 16 (over y, z_hi, core).
Axes of the slice: x: 4, y: 4, z: 4 (z_hi: 2, z_lo: 2; z = z_hi * 2 + z_lo), core: 2. Of those that a mesh axis runs over, the one named last changes fastest.
Arguments:
- base_flow: float32 [2, 64, 1024, 128], P(None, 'slab', 'tile'), may hold values from -0.4 to 0.8
- forcing: float32 [64, 4, 1024, 128], P('slab', None, 'tile'), may hold values from -6 to 6
- damping: float32 [1024, 128], P('tile'), may hold values from 0.005 to 0.2
- harmonics: int32 [8], replicated, may hold values from 1 to 31, as said below
Outputs:
- sketch: float32 [8, 2, 4, 1024, 128], P('slab', None, None, 'tile')
Inputs may be any that keep to these rules, and one draw needn't show every extreme that they name: `harmonics`: distinct harmonic indices.
All inputs are finite; a program needn't handle non-finite values.
Results may differ from a plain program's by a relative error of at most 0.0003.
Values sent between devices are 32-bit elements; how exact they have to be, the bound alone decides.
No kernel may reach another device: no remote copies, remote signals or barrier semaphores. Data moves between devices by JAX's collectives and lax.ppermute only.
A program may use at most 64 MiB of HBM per device.

v0:
```python
import math

import jax
import jax.numpy as jnp
from jax import lax
from jax.sharding import PartitionSpec as P

SWEEPS = 2
H = 8


DIFFUSE = 0.15


def passed_along(block, axis, distance):
    devices = range(lax.axis_size(axis))
    route = [((i - distance) % len(devices), i) for i in devices]
    return lax.ppermute(block, axis, route)


def with_neighbours(block, axis, dim):
    count = lax.axis_size(axis)
    before = lax.ppermute(block, axis, [(i, i + 1) for i in range(count - 1)])
    after = lax.ppermute(block, axis, [(i + 1, i) for i in range(count - 1)])
    return jnp.concatenate([before, block, after], axis=dim)


def pad_grid(field):
    widths = [(0, 0)] * (field.ndim - 2) + [(1, 1), (1, 1)]
    return jnp.pad(field, widths)


def laplace(padded, center):
    return (
        padded[..., 2:, 1:-1]
        + padded[..., :-2, 1:-1]
        + padded[..., 1:-1, 2:]
        + padded[..., 1:-1, :-2]
        - 4.0 * center
    )


def forward_rate(state, speed_x, speed_y, damping, source, mask):
    padded = pad_grid(state)
    grad_x = 0.5 * (padded[..., 2:, 1:-1] - padded[..., :-2, 1:-1])
    grad_y = 0.5 * (padded[..., 1:-1, 2:] - padded[..., 1:-1, :-2])
    rate = source - (speed_x * grad_x + speed_y * grad_y) + DIFFUSE * laplace(padded, state) - damping * state
    return rate * mask


def adjoint_rate(state, speed_x, speed_y, damping, source, mask):
    padded = pad_grid(state)
    flux_x = pad_grid(speed_x * state)
    flux_y = pad_grid(speed_y * state)
    div_x = 0.5 * (flux_x[..., 2:, 1:-1] - flux_x[..., :-2, 1:-1])
    div_y = 0.5 * (flux_y[..., 1:-1, 2:] - flux_y[..., 1:-1, :-2])
    rate = source + div_x + div_y + DIFFUSE * laplace(padded, state) - damping * state
    return rate * mask


def coefficient_table(chosen, phase, periods):
    turns = chosen[:, None] * phase[None, :] % periods
    angle = 2.0 * math.pi / periods * turns.astype(jnp.float32)
    table = jnp.stack([jnp.cos(angle), -jnp.sin(angle)], axis=1) * (1.0 / math.sqrt(periods))
    return table.reshape(2 * chosen.shape[0], phase.shape[0])


def on_device(base_flow, forcing, damping, harmonics):
    steps = forcing.shape[0]
    count_f, rows, columns = (forcing.shape[1], forcing.shape[2], forcing.shape[3])
    slabs = lax.axis_size("slab")
    tiles = lax.axis_size("tile")
    periods = steps * slabs

    packed = jnp.concatenate(
        [base_flow.reshape(2 * steps, rows, columns), forcing.reshape(steps * count_f, rows, columns), damping[None]],
        axis=0,
    )
    wide = with_neighbours(packed, "tile", 1)
    ext = 3 * rows
    flow = wide[: 2 * steps].reshape(2, steps, ext, columns)
    drive = wide[2 * steps : 2 * steps + steps * count_f].reshape(steps, count_f, ext, columns)
    damp = wide[-1]
    row = lax.axis_index("tile") * rows - rows + jnp.arange(ext, dtype=jnp.int32)
    mask = ((row >= 0) & (row < tiles * rows)).astype(jnp.float32)[:, None]

    def band(depth):
        return min(rows, -(-depth // 8) * 8)

    def cut(field, have, want):
        return lax.slice_in_dim(field, have - want, have + rows + want, axis=field.ndim - 2)

    def full(field, want):
        return cut(field, rows, want)

    tail = 2 * steps
    fwd_need = [tail + 4 * steps - 3 - 2 * m for m in range(steps)]
    fwd_need = [max(need, tail + 2 * m + 2) for m, need in enumerate(fwd_need)]
    sweep_bands = [
        [band(fwd_need[0] + 2 * (steps - m)) for m in range(steps)],
        [band(need) for need in fwd_need],
    ]
    sends = [band(fwd_need[0])]

    have = band(fwd_need[0] + 2 * steps)
    start = jnp.zeros((count_f, rows + 2 * have, columns), jnp.float32)
    for sweep in range(SWEEPS):
        state = start
        record = []
        for step in range(steps):
            want = sweep_bands[min(sweep, 1)][step]
            state = cut(state, have, want)
            have = want
            record.append((state, have))
            speed_x = full(flow[0, step], want)
            speed_y = full(flow[1, step], want)
            damp_here, mask_here = full(damp, want), full(mask, want)
            source = full(drive[step], want)
            first = forward_rate(state, speed_x, speed_y, damp_here, source, mask_here)
            second = forward_rate(state + first, speed_x, speed_y, damp_here, source, mask_here)
            state = state + 0.5 * (first + second)
        if sweep + 1 < SWEEPS:
            start = passed_along(cut(state, have, sends[0]), "slab", 1)
            have = sends[0]
    response = record
    adj_bands = [
        [band(tail + 2 * m + 2) for m in range(steps)],
        [band(2 * m + 2) for m in range(steps)],
    ]
    have = adj_bands[0][steps - 1]
    start = jnp.zeros((count_f, rows + 2 * have, columns), jnp.float32)
    for sweep in range(SWEEPS):
        state = start
        record = [None] * steps
        for step in range(steps - 1, -1, -1):
            want = adj_bands[min(sweep, 1)][step]
            state = cut(state, have, want)
            have = want
            speed_x = full(flow[0, step], want)
            speed_y = full(flow[1, step], want)
            damp_here, mask_here = full(damp, want), full(mask, want)
            source = cut(response[step][0], response[step][1], want)
            first = adjoint_rate(state, speed_x, speed_y, damp_here, source, mask_here)
            second = adjoint_rate(state + first, speed_x, speed_y, damp_here, source, mask_here)
            state = state + 0.5 * (first + second)
            record[step] = cut(state, have, 0)
        if sweep + 1 < SWEEPS:
            start = passed_along(cut(state, have, tail), "slab", -1)
            have = tail
    adjoint = jnp.stack(record, axis=0)
    phase = lax.axis_index("slab") * steps + jnp.arange(steps, dtype=jnp.int32)
    flat = adjoint.reshape(steps, count_f * rows * columns)
    table = coefficient_table(harmonics, phase, periods)
    terms = jnp.dot(table, flat, precision=lax.Precision.HIGHEST)
    parts = lax.all_to_all(terms.reshape(slabs, 2 * H // slabs, count_f, rows, columns), "slab", 0, 0, tiled=True)
    return jnp.sum(parts, axis=0, keepdims=True)


def solution(mesh):
    return jax.shard_map(
        on_device,
        mesh=mesh,
        in_specs=(
            P(None, "slab", "tile", None),
            P("slab", None, "tile", None),
            P("tile", None),
            P(),
        ),
        out_specs=P("slab", None, None, "tile", None),
        check_vma=False,
    )
```

profile of v0, /device:TPU:64, one launch (start us, length us, event | category | flops | bytes accessed | tf_op | source)
XLA Modules:
  0.0 118.7 jit_solution(14903671096282991661)
XLA Ops:
  0.0 2.8 %pad_maximum_fusion.1 = f32[49,64,128]{2,1,0:T(8,128)} fusion(f32[1,64,128]{2,1,0:T(8,128)} %bitcast.210, f32[32,64,128]{2,1,0:T(8,128)} %bitcast.178, f32[16,64,128]{2,1,0:T(8,128)} %bitcast.188), kind=kLoop, calls=%fused_computation.1 | loop fusion | flops 802816 | bytes 3211264 | tf_op jit(solution)/shard_map/concatenate | solution.py:75
  2.8 1.9 %collective-permute-start.1 = (f32[49,64,128]{2,1,0:T(8,128)}, f32[49,64,128]{2,1,0:T(8,128)S(1)}, u32[]{:S(2)}, u32[]{:S(2)}) collective-permute-start(f32[49,64,128]{2,1,0:T(8,128)} %pad_maximum_fusion.1), channel_id=1, source_target_pairs={{1,0},{2,1},{3,2},{4,3},{5,4},{6,5},{7,6},{8,7},{9,8},{10,9},{11,1... | collective-permute-start | bytes 4816904 | tf_op jit(solution)/shard_map/ppermute | solution.py:24
  4.7 2.4 %collective-permute-start = (f32[49,64,128]{2,1,0:T(8,128)}, f32[49,64,128]{2,1,0:T(8,128)S(1)}, u32[]{:S(2)}, u32[]{:S(2)}) collective-permute-start(f32[49,64,128]{2,1,0:T(8,128)} %pad_maximum_fusion.1), channel_id=1, source_target_pairs={{0,1},{1,2},{2,3},{3,4},{4,5},{5,6},{6,7},{7,8},{8,9},{9,10},{10,1... | collective-permute-start | bytes 4816904 | tf_op jit(solution)/shard_map/ppermute | solution.py:23
  8.0 15.3 %collective-permute-done.1 = f32[49,64,128]{2,1,0:T(8,128)S(1)} collective-permute-done((f32[49,64,128]{2,1,0:T(8,128)}, f32[49,64,128]{2,1,0:T(8,128)S(1)}, u32[]{:S(2)}, u32[]{:S(2)}) %collective-permute-start.1) | collective-permute-done | bytes 1605664 | tf_op jit(solution)/shard_map/ppermute | solution.py:24
  23.3 24.9 %collective-permute-done = f32[49,64,128]{2,1,0:T(8,128)S(1)} collective-permute-done((f32[49,64,128]{2,1,0:T(8,128)}, f32[49,64,128]{2,1,0:T(8,128)S(1)}, u32[]{:S(2)}, u32[]{:S(2)}) %collective-permute-start) | collective-permute-done | bytes 1605664 | tf_op jit(solution)/shard_map/ppermute | solution.py:23
  48.2 0.5 pad_maximum_fusion
  50.5 0.4 multiply_add_fusion
  51.2 0.5 add_subtract_fusion
  51.9 0.5 fusion.5
  52.4 0.4 multiply_add_fusion.6
  52.8 0.5 fusion.4
  53.3 0.4 multiply_add_fusion.4
  53.7 0.5 fusion.3
  54.2 0.4 multiply_add_fusion.2
  55.0 0.4 add_subtract_fusion.1
  55.7 0.4 fusion.12
  56.9 9.0 %collective-permute-done.2 = f32[4,160,128]{2,1,0:T(8,128)S(1)} collective-permute-done((f32[4,160,128]{2,1,0:T(8,128)S(1)}, f32[4,160,128]{2,1,0:T(8,128)S(1)}, u32[]{:S(2)}, u32[]{:S(2)}) %collective-permute-start.2) | collective-permute-done | bytes 327712 | tf_op jit(solution)/shard_map/ppermute | solution.py:18
  65.9 0.4 fusion.11
  66.8 0.4 fusion.10
  67.6 0.4 fusion.9
  68.5 0.4 fusion.16
  69.2 0.4 fusion.15
  70.0 0.4 fusion.14
  70.7 0.4 fusion.13
  72.1 0.4 broadcast_multiply_fusion.9
  72.5 0.4 broadcast_multiply_fusion.6
  78.2 7.7 %collective-permute-done.3 = f32[4,96,128]{2,1,0:T(8,128)S(1)} collective-permute-done((f32[4,96,128]{2,1,0:T(8,128)S(1)}, f32[4,96,128]{2,1,0:T(8,128)S(1)}, u32[]{:S(2)}, u32[]{:S(2)}) %collective-permute-start.3) | collective-permute-done | bytes 196640 | tf_op jit(solution)/shard_map/ppermute | solution.py:18
  91.4 1.6 %stack.41 = f32[8,32768]{1,0:T(8,128)S(1)} concatenate(f32[1,32768]{1,0:T(1,128)S(1)} %bitcast.221, f32[1,32768]{1,0:T(1,128)S(1)} %bitcast.220, f32[1,32768]{1,0:T(1,128)S(1)} %bitcast.226, f32[1,32768]{1,0:T(1,128)S(1)} %bitcast.225, f32[1,32768]{1,0:T(1,128)S(1)} %bitcast.209, f32[1,32768]{1,0:T(1,128)S(1)} %bitcast.224, f32[1,32768]{1,0:T(1,128)S(1)} %bitcast.223, ...), dimensions={0} | concatenate | bytes 2097152 | tf_op jit(solution)/shard_map/stack | solution.py:150
  93.1 1.8 %fusion.537 = f32[8,2,4,64,128]{4,0,3,2,1:T(8,128)S(1)} fusion(f32[4,64,128,8,1]{2,3,1,0,4:T(8,128)S(1)} %bitcast.208, f32[8,1,8]{2,0,1:T(8,128)S(1)} %get-tuple-element.211, f32[8,1,8]{2,0,1:T(8,128)S(1)} %get-tuple-element.210), kind=kOutput, calls=%fused_computation.1143 | convolution fusion | flops 50331904 | bytes 3146240 | tf_op jit(solution)/shard_map/dot_general | solution.py:154
  94.8 0.4 copy.5
  95.3 22.6 %all_to_all.5 = f32[8,2,4,64,128]{4,3,2,1,0:T(8,128)S(1)} all-to-all(f32[8,2,4,64,128]{4,3,2,1,0:T(8,128)S(1)} %copy.5), channel_id=1, replica_groups=mesh['slab'=8,'tile'=16] {'slab'}, dimensions={0} | all-to-all | bytes 4194304 | tf_op jit(solution)/shard_map/all_to_all | solution.py:155
  117.8 0.8 reduce_sum.9
  (139 shorter events, 17.8 us)
Async XLA Ops:
  0.0 48.2 %copy-start.3 = (f32[64,128]{1,0:T(8,128)S(1)}, f32[64,128]{1,0:T(8,128)}, u32[]{:S(2)}) copy-start(f32[64,128]{1,0:T(8,128)} %param.6) | copy-start | bytes 98308
  0.0 7.8 %copy-start.4 = (s32[8]{0:T(128)S(1)}, s32[8]{0:T(128)}, u32[]{:S(2)}) copy-start(s32[8]{0:T(128)} %param.7) | copy-start | bytes 100
  2.8 20.5 %collective-permute-start.1 = (f32[49,64,128]{2,1,0:T(8,128)}, f32[49,64,128]{2,1,0:T(8,128)S(1)}, u32[]{:S(2)}, u32[]{:S(2)}) collective-permute-start(f32[49,64,128]{2,1,0:T(8,128)} %pad_maximum_fusion.1), channel_id=1, source_target_pairs={{1,0},{2,1},{3,2},{4,3},{5,4},{6,5},{7,6},{8,7},{9,8},{10,9},{11,1... | collective-permute-start | bytes 4816904 | tf_op jit(solution)/shard_map/ppermute | solution.py:24
  4.7 43.5 %collective-permute-start = (f32[49,64,128]{2,1,0:T(8,128)}, f32[49,64,128]{2,1,0:T(8,128)S(1)}, u32[]{:S(2)}, u32[]{:S(2)}) collective-permute-start(f32[49,64,128]{2,1,0:T(8,128)} %pad_maximum_fusion.1), channel_id=1, source_target_pairs={{0,1},{1,2},{2,3},{3,4},{4,5},{5,6},{6,7},{7,8},{8,9},{9,10},{10,1... | collective-permute-start | bytes 4816904 | tf_op jit(solution)/shard_map/ppermute | solution.py:23
  7.9 40.3 %copy-start = (f32[8,4,64,128]{3,2,1,0:T(8,128)S(1)}, f32[8,4,64,128]{3,2,1,0:T(8,128)}, u32[]{:S(2)}) copy-start(f32[8,4,64,128]{3,2,1,0:T(8,128)} %param.5) | copy-start | bytes 3145732
  7.9 40.3 %copy-start.1 = (f32[2,8,64,128]{3,2,1,0:T(8,128)S(1)}, f32[2,8,64,128]{3,2,1,0:T(8,128)}, u32[]{:S(2)}) copy-start(f32[2,8,64,128]{3,2,1,0:T(8,128)} %param.4) | copy-start | bytes 1572868
  56.5 9.4 %collective-permute-start.2 = (f32[4,160,128]{2,1,0:T(8,128)S(1)}, f32[4,160,128]{2,1,0:T(8,128)S(1)}, u32[]{:S(2)}, u32[]{:S(2)}) collective-permute-start(f32[4,160,128]{2,1,0:T(8,128)S(1)} %multiply_add_fusion.14), channel_id=1, source_target_pairs={{112,0},{0,16},{16,32},{32,48},{48,64},{64,80},{80,96},{96,112},{1... | collective-permute-start | bytes 983048 | tf_op jit(solution)/shard_map/ppermute | solution.py:18
  77.9 8.1 %collective-permute-start.3 = (f32[4,96,128]{2,1,0:T(8,128)S(1)}, f32[4,96,128]{2,1,0:T(8,128)S(1)}, u32[]{:S(2)}, u32[]{:S(2)}) collective-permute-start(f32[4,96,128]{2,1,0:T(8,128)S(1)} %slice_add_fusion.9), channel_id=1, source_target_pairs={{16,0},{32,16},{48,32},{64,48},{80,64},{96,80},{112,96},{0,112},{1... | collective-permute-start | bytes 589832 | tf_op jit(solution)/shard_map/ppermute | solution.py:18
  88.7 0.7 copy-start.2
  90.5 0.9 slice-start
where the time goes:
time: 119 us
  waiting for transfers between devices  56.9 us (48%)
  other arithmetic  28.3 us (24%)
  blocking collectives  22.6 us (19%)
  starting transfers between devices  4.87 us (4%)
  local copies, waits for them, and re-layouts  3.24 us (3%)
  matrix products  1.77 us (1%)
    ppermute x1, waiting for transfers between devices, with_neighbours(): before = lax.ppermute(block, axis, [(i, i + 1) for i in range(count - 1)])  24.9 us
    all_to_all x1, blocking collectives, on_device(): lax.all_to_all(terms.reshape(slabs, 2 * H // slabs, count_f, rows, column...  22.6 us
    ppermute x2, waiting for transfers between devices, passed_along(): return lax.ppermute(block, axis, route)  16.7 us
    ppermute x1, waiting for transfers between devices, with_neighbours(): after = lax.ppermute(block, axis, [(i + 1, i) for i in range(count - 1)])  15.3 us
    mul x28, other arithmetic, adjoint_rate(): flux_y = pad_grid(speed_y * state)  8.48 us
    add x14, other arithmetic, on_device(): state + first  5.84 us
    add x16, other arithmetic, on_device(): state = state + 0.5 * (first + second)  5.41 us
    concatenate x1, other arithmetic, on_device(): jnp.concatenate([base_flow.reshape(2 * steps, rows, columns), forcing.res...  2.75 us
  transfers between devices with their start and end apart: 4, of which 4 were waited for; matrix products, arithmetic and copies ran while one was open for 1% of the time, Pallas kernels for 0%

commit v1 on v0

--- a/solution.py
+++ b/solution.py
@@ -76,13 +76,6 @@
         [base_flow.reshape(2 * steps, rows, columns), forcing.reshape(steps * count_f, rows, columns), damping[None]],
         axis=0,
     )
-    wide = with_neighbours(packed, "tile", 1)
-    ext = 3 * rows
-    flow = wide[: 2 * steps].reshape(2, steps, ext, columns)
-    drive = wide[2 * steps : 2 * steps + steps * count_f].reshape(steps, count_f, ext, columns)
-    damp = wide[-1]
-    row = lax.axis_index("tile") * rows - rows + jnp.arange(ext, dtype=jnp.int32)
-    mask = ((row >= 0) & (row < tiles * rows)).astype(jnp.float32)[:, None]
 
     def band(depth):
         return min(rows, -(-depth // 8) * 8)
@@ -90,21 +83,37 @@
     def cut(field, have, want):
         return lax.slice_in_dim(field, have - want, have + rows + want, axis=field.ndim - 2)
 
-    def full(field, want):
-        return cut(field, rows, want)
-
     tail = 2 * steps
     fwd_need = [tail + 4 * steps - 3 - 2 * m for m in range(steps)]
     fwd_need = [max(need, tail + 2 * m + 2) for m, need in enumerate(fwd_need)]
+    near = band(2 * steps)
+    far = band(fwd_need[0])
+
+    before = lax.ppermute(packed[:, rows - near :], "tile", [(i, i + 1) for i in range(tiles - 1)])
+    after = lax.ppermute(packed[:, :near], "tile", [(i + 1, i) for i in range(tiles - 1)])
+    before_far = lax.ppermute(packed[:, rows - far : rows - near], "tile", [(i, i + 1) for i in range(tiles - 1)])
+    after_far = lax.ppermute(packed[:, near:far], "tile", [(i + 1, i) for i in range(tiles - 1)])
+    narrow = jnp.concatenate([before, packed, after], axis=1)
+    wide = jnp.concatenate([before_far, before, packed, after, after_far], axis=1)
+
+    def fields(block, have):
+        ext = rows + 2 * have
+        flow = block[: 2 * steps].reshape(2, steps, ext, columns)
+        drive = block[2 * steps : 2 * steps + steps * count_f].reshape(steps, count_f, ext, columns)
+        row = lax.axis_index("tile") * rows - have + jnp.arange(ext, dtype=jnp.int32)
+        mask = ((row >= 0) & (row < tiles * rows)).astype(jnp.float32)[:, None]
+        return flow, drive, block[-1], mask, have
+
+    sweep_fields = [fields(narrow, near), fields(wide, far)]
     sweep_bands = [
-        [band(fwd_need[0] + 2 * (steps - m)) for m in range(steps)],
+        [band(2 * (steps - m)) for m in range(steps)],
         [band(need) for need in fwd_need],
     ]
-    sends = [band(fwd_need[0])]
 
-    have = band(fwd_need[0] + 2 * steps)
+    have = sweep_bands[0][0]
     start = jnp.zeros((count_f, rows + 2 * have, columns), jnp.float32)
     for sweep in range(SWEEPS):
+        flow, drive, damp, mask, held = sweep_fields[min(sweep, 1)]
         state = start
         record = []
         for step in range(steps):
@@ -112,21 +121,28 @@
             state = cut(state, have, want)
             have = want
             record.append((state, have))
-            speed_x = full(flow[0, step], want)
-            speed_y = full(flow[1, step], want)
-            damp_here, mask_here = full(damp, want), full(mask, want)
-            source = full(drive[step], want)
+            speed_x = cut(flow[0, step], held, want)
+            speed_y = cut(flow[1, step], held, want)
+            damp_here, mask_here = cut(damp, held, want), cut(mask, held, want)
+            source = cut(drive[step], held, want)
             first = forward_rate(state, speed_x, speed_y, damp_here, source, mask_here)
             second = forward_rate(state + first, speed_x, speed_y, damp_here, source, mask_here)
             state = state + 0.5 * (first + second)
         if sweep + 1 < SWEEPS:
-            start = passed_along(cut(state, have, sends[0]), "slab", 1)
-            have = sends[0]
+            own = cut(state, have, 0)
+            ahead = lambda j, t: ((j + 1) % slabs) * tiles + t
+            up = lax.ppermute(own[:, rows - far :], ("slab", "tile"),
+                              [(j * tiles + t, ahead(j, t + 1)) for j in range(slabs) for t in range(tiles - 1)])
+            down = lax.ppermute(own[:, :far], ("slab", "tile"),
+                                [(j * tiles + t + 1, ahead(j, t)) for j in range(slabs) for t in range(tiles - 1)])
+            start = jnp.concatenate([up, passed_along(own, "slab", 1), down], axis=1)
+            have = far
     response = record
     adj_bands = [
         [band(tail + 2 * m + 2) for m in range(steps)],
         [band(2 * m + 2) for m in range(steps)],
     ]
+    flow, drive, damp, mask, held = sweep_fields[1]
     have = adj_bands[0][steps - 1]
     start = jnp.zeros((count_f, rows + 2 * have, columns), jnp.float32)
     for sweep in range(SWEEPS):
@@ -136,9 +152,9 @@
             want = adj_bands[min(sweep, 1)][step]
             state = cut(state, have, want)
             have = want
-            speed_x = full(flow[0, step], want)
-            speed_y = full(flow[1, step], want)
-            damp_here, mask_here = full(damp, want), full(mask, want)
+            speed_x = cut(flow[0, step], held, want)
+            speed_y = cut(flow[1, step], held, want)
+            damp_here, mask_here = cut(damp, held, want), cut(mask, held, want)
             source = cut(response[step][0], response[step][1], want)
             first = adjoint_rate(state, speed_x, speed_y, damp_here, source, mask_here)
             second = adjoint_rate(state + first, speed_x, speed_y, damp_here, source, mask_here)

time: 119 us -> 119 us (level)
  the two profiles are of different devices: /device:TPU:64 before, /device:TPU:16 now
where the time goes in v1:
time: 119 us; the launch traced here: 117 us
  blocking collectives  31.3 us (26%)
  starting transfers between devices  30.3 us (25%)
  other arithmetic  24.2 us (20%)
  waiting for transfers between devices  22.2 us (19%)
  local copies, waits for them, and re-layouts  6.27 us (5%)
  matrix products  1.77 us (1%)
    all_to_all x1, blocking collectives, on_device(): lax.all_to_all(terms.reshape(slabs, 2 * H // slabs, count_f, rows, column...  31.3 us
    ppermute x1, starting transfers between devices, on_device(): lax.ppermute(own[:, rows - far:], ('slab', 'tile'), [(j * tiles + t, ahea...  10.6 us
    ppermute x2, waiting for transfers between devices, passed_along(): return lax.ppermute(block, axis, route)  8.95 us
    mul x28, other arithmetic, adjoint_rate(): flux_y = pad_grid(speed_y * state)  8.49 us
    ppermute x1, waiting for transfers between devices, on_device(): lax.ppermute(packed[:, rows - near:], 'tile', [(i, i + 1) for i in range(...  6.12 us
    ppermute x1, starting transfers between devices, on_device(): lax.ppermute(packed[:, :near], 'tile', [(i + 1, i) for i in range(tiles -...  6.03 us
    ppermute x1, starting transfers between devices, on_device(): lax.ppermute(packed[:, near:far], 'tile', [(i + 1, i) for i in range(tile...  5.1 us
    add x14, other arithmetic, on_device(): state + first  4.68 us
  transfers between devices with their start and end apart: 8, of which 5 were waited for; matrix products, arithmetic and copies ran while one was open for 6% of the time, Pallas kernels for 0%

profile of v1, /device:TPU:16, one launch (start us, length us, event | category | flops | bytes accessed | tf_op | source)
XLA Modules:
  0.0 117.1 jit_solution(3932184559408484352)
XLA Ops:
  0.0 1.7 %pad_maximum_fusion.1 = f32[49,64,128]{2,1,0:T(8,128)S(1)} fusion(f32[1,64,128]{2,1,0:T(8,128)} %bitcast.211, f32[32,64,128]{2,1,0:T(8,128)} %bitcast.178, f32[16,64,128]{2,1,0:T(8,128)} %bitcast.191), kind=kLoop, calls=%fused_computation.1 | loop fusion | flops 802816 | bytes 3211264 | tf_op jit(solution)/shard_map/concatenate | solution.py:75
  1.7 1.0 slice.2425
  2.7 5.1 %collective-permute-start.6 = (f32[49,32,128]{2,1,0:T(8,128)}, f32[49,32,128]{2,1,0:T(8,128)S(1)}, u32[]{:S(2)}, u32[]{:S(2)}) collective-permute-start(f32[49,32,128]{2,1,0:T(8,128)} %slice.2425), channel_id=1, source_target_pairs={{1,0},{2,1},{3,2},{4,3},{5,4},{6,5},{7,6},{8,7},{9,8},{10,9},{11,1... | collective-permute-start | bytes 2408456 | tf_op jit(solution)/shard_map/ppermute | solution.py:95
  7.8 1.9 %collective-permute-start.5 = (f32[49,32,128]{2,1,0:T(8,128)}, f32[49,32,128]{2,1,0:T(8,128)}, u32[]{:S(2)}, u32[]{:S(2)}) collective-permute-start(f32[49,32,128]{2,1,0:T(8,128)} %slice.2425), channel_id=1, source_target_pairs={{0,1},{1,2},{2,3},{3,4},{4,5},{5,6},{6,7},{7,8},{8,9},{9,10},{10,1... | collective-permute-start | bytes 2408456 | tf_op jit(solution)/shard_map/ppermute | solution.py:94
  9.7 0.9 fusion.577
  10.7 6.0 %collective-permute-start.1 = (f32[49,16,128]{2,1,0:T(8,128)}, f32[49,16,128]{2,1,0:T(8,128)S(1)}, u32[]{:S(2)}, u32[]{:S(2)}) collective-permute-start(f32[49,16,128]{2,1,0:T(8,128)} %get-tuple-element.133), channel_id=1, source_target_pairs={{1,0},{2,1},{3,2},{4,3},{5,4},{6,5},{7,6},{8,7},{9,8},{10,9},{11,1... | collective-permute-start | bytes 1204232 | tf_op jit(solution)/shard_map/ppermute | solution.py:93
  16.7 1.9 %collective-permute-start = (f32[49,16,128]{2,1,0:T(8,128)}, f32[49,16,128]{2,1,0:T(8,128)S(1)}, u32[]{:S(2)}, u32[]{:S(2)}) collective-permute-start(f32[49,16,128]{2,1,0:T(8,128)} %get-tuple-element.134), channel_id=1, source_target_pairs={{0,1},{1,2},{2,3},{3,4},{4,5},{5,6},{6,7},{7,8},{8,9},{9,10},{10,1... | collective-permute-start | bytes 1204232 | tf_op jit(solution)/shard_map/ppermute | solution.py:92
  19.0 3.4 %collective-permute-done.1 = f32[49,16,128]{2,1,0:T(8,128)S(1)} collective-permute-done((f32[49,16,128]{2,1,0:T(8,128)}, f32[49,16,128]{2,1,0:T(8,128)S(1)}, u32[]{:S(2)}, u32[]{:S(2)}) %collective-permute-start.1) | collective-permute-done | bytes 401440 | tf_op jit(solution)/shard_map/ppermute | solution.py:93
  22.4 6.1 %collective-permute-done = f32[49,16,128]{2,1,0:T(8,128)S(1)} collective-permute-done((f32[49,16,128]{2,1,0:T(8,128)}, f32[49,16,128]{2,1,0:T(8,128)S(1)}, u32[]{:S(2)}, u32[]{:S(2)}) %collective-permute-start) | collective-permute-done | bytes 401440 | tf_op jit(solution)/shard_map/ppermute | solution.py:92
  33.0 10.6 %collective-permute-start.2 = (f32[4,48,128]{2,1,0:T(8,128)S(1)}, f32[4,48,128]{2,1,0:T(8,128)S(1)}, u32[]{:S(2)}, u32[]{:S(2)}) collective-permute-start(f32[4,48,128]{2,1,0:T(8,128)S(1)} %get-tuple-element.219), channel_id=1, source_target_pairs={{0,17},{1,18},{2,19},{3,20},{4,21},{5,22},{6,23},{7,24},{8,25},{9,... | collective-permute-start | bytes 294920 | tf_op jit(solution)/shard_map/ppermute | solution.py:134
  43.7 1.6 %collective-permute-start.3 = (f32[4,64,128]{2,1,0:T(8,128)S(1)}, f32[4,64,128]{2,1,0:T(8,128)S(1)}, u32[]{:S(2)}, u32[]{:S(2)}) collective-permute-start(f32[4,64,128]{2,1,0:T(8,128)S(1)} %slice.2423), channel_id=1, source_target_pairs={{112,0},{0,16},{16,32},{32,48},{48,64},{64,80},{80,96},{96,112},{1... | collective-permute-start | bytes 393224 | tf_op jit(solution)/shard_map/ppermute | solution.py:18
  45.7 2.1 %collective-permute-start.4 = (f32[4,48,128]{2,1,0:T(8,128)S(1)}, f32[4,48,128]{2,1,0:T(8,128)S(1)}, u32[]{:S(2)}, u32[]{:S(2)}) collective-permute-start(f32[4,48,128]{2,1,0:T(8,128)S(1)} %get-tuple-element.218), channel_id=1, source_target_pairs={{1,16},{2,17},{3,18},{4,19},{5,20},{6,21},{7,22},{8,23},{9,24},{10... | collective-permute-start | bytes 294920 | tf_op jit(solution)/shard_map/ppermute | solution.py:136
  47.8 4.0 %collective-permute-done.3 = f32[4,64,128]{2,1,0:T(8,128)S(1)} collective-permute-done((f32[4,64,128]{2,1,0:T(8,128)S(1)}, f32[4,64,128]{2,1,0:T(8,128)S(1)}, u32[]{:S(2)}, u32[]{:S(2)}) %collective-permute-start.3) | collective-permute-done | bytes 131104 | tf_op jit(solution)/shard_map/ppermute | solution.py:18
  51.8 3.7 %collective-permute-done.4 = f32[4,48,128]{2,1,0:T(8,128)S(1)} collective-permute-done((f32[4,48,128]{2,1,0:T(8,128)S(1)}, f32[4,48,128]{2,1,0:T(8,128)S(1)}, u32[]{:S(2)}, u32[]{:S(2)}) %collective-permute-start.4) | collective-permute-done | bytes 98336 | tf_op jit(solution)/shard_map/ppermute | solution.py:136
  55.6 1.2 %constant_dynamic-update-slice_fusion.7 = f32[49,160,128]{2,1,0:T(8,128)S(1)} fusion(f32[49,32,128]{2,1,0:T(8,128)} %collective-permute-done.5), kind=kLoop, calls=%fused_computation.1150 | loop fusion | bytes 1605632
  57.5 0.4 fusion.2
  58.3 0.4 fusion.1
  59.2 0.4 fusion
  60.1 0.4 fusion.6
  60.9 0.4 fusion.5
  61.7 0.4 fusion.4
  62.5 0.4 fusion.3
  63.8 0.4 broadcast_multiply_fusion.8
  64.3 0.4 broadcast_multiply_fusion.5
  69.3 0.4 fusion.184
  69.8 1.0 collective-permute-start.7
  70.9 4.9 %collective-permute-done.7 = f32[4,96,128]{2,1,0:T(8,128)S(1)} collective-permute-done((f32[4,96,128]{2,1,0:T(8,128)S(1)}, f32[4,96,128]{2,1,0:T(8,128)S(1)}, u32[]{:S(2)}, u32[]{:S(2)}) %collective-permute-start.7) | collective-permute-done | bytes 196640 | tf_op jit(solution)/shard_map/ppermute | solution.py:18
  81.2 1.6 %stack.41 = f32[8,32768]{1,0:T(8,128)S(1)} concatenate(f32[1,32768]{1,0:T(1,128)S(1)} %bitcast.230, f32[1,32768]{1,0:T(1,128)S(1)} %bitcast.229, f32[1,32768]{1,0:T(1,128)S(1)} %bitcast.235, f32[1,32768]{1,0:T(1,128)S(1)} %bitcast.234, f32[1,32768]{1,0:T(1,128)S(1)} %bitcast.225, f32[1,32768]{1,0:T(1,128)S(1)} %bitcast.233, f32[1,32768]{1,0:T(1,128)S(1)} %bitcast.232, ...), dimensions={0} | concatenate | bytes 2097152 | tf_op jit(solution)/shard_map/stack | solution.py:166
  82.8 1.8 %fusion.535 = f32[8,2,4,64,128]{4,0,3,2,1:T(8,128)S(1)} fusion(f32[4,64,128,8,1]{2,3,1,0,4:T(8,128)S(1)} %bitcast.224, f32[8,1,8]{2,0,1:T(8,128)S(1)} %get-tuple-element.223, f32[8,1,8]{2,0,1:T(8,128)S(1)} %get-tuple-element.222), kind=kOutput, calls=%fused_computation.1153 | convolution fusion | flops 50331904 | bytes 3146240 | tf_op jit(solution)/shard_map/dot_general | solution.py:170
  84.6 0.4 copy.5
  85.0 31.3 %all_to_all.5 = f32[8,2,4,64,128]{4,3,2,1,0:T(8,128)S(1)} all-to-all(f32[8,2,4,64,128]{4,3,2,1,0:T(8,128)S(1)} %copy.5), channel_id=1, replica_groups=mesh['slab'=8,'tile'=16] {'slab'}, dimensions={0} | all-to-all | bytes 4194304 | tf_op jit(solution)/shard_map/all_to_all | solution.py:171
  116.2 0.8 reduce_sum.9
  (156 shorter events, 18.7 us)
Async XLA Ops:
  0.0 28.5 %copy-start.2 = (f32[64,128]{1,0:T(8,128)S(1)}, f32[64,128]{1,0:T(8,128)}, u32[]{:S(2)}) copy-start(f32[64,128]{1,0:T(8,128)} %param.6) | copy-start | bytes 98308
  0.0 28.5 %copy-start = (f32[8,4,64,128]{3,2,1,0:T(8,128)S(1)}, f32[8,4,64,128]{3,2,1,0:T(8,128)}, u32[]{:S(2)}) copy-start(f32[8,4,64,128]{3,2,1,0:T(8,128)} %param.5) | copy-start | bytes 3145732
  0.0 28.5 %copy-start.1 = (f32[2,8,64,128]{3,2,1,0:T(8,128)S(1)}, f32[2,8,64,128]{3,2,1,0:T(8,128)}, u32[]{:S(2)}) copy-start(f32[2,8,64,128]{3,2,1,0:T(8,128)} %param.4) | copy-start | bytes 1572868
  0.0 18.8 %copy-start.4 = (s32[8]{0:T(128)S(1)}, s32[8]{0:T(128)}, u32[]{:S(2)}) copy-start(s32[8]{0:T(128)} %param.7) | copy-start | bytes 100
  2.7 54.3 %collective-permute-start.6 = (f32[49,32,128]{2,1,0:T(8,128)}, f32[49,32,128]{2,1,0:T(8,128)S(1)}, u32[]{:S(2)}, u32[]{:S(2)}) collective-permute-start(f32[49,32,128]{2,1,0:T(8,128)} %slice.2425), channel_id=1, source_target_pairs={{1,0},{2,1},{3,2},{4,3},{5,4},{6,5},{7,6},{8,7},{9,8},{10,9},{11,1... | collective-permute-start | bytes 2408456 | tf_op jit(solution)/shard_map/ppermute | solution.py:95
  7.8 47.7 %collective-permute-start.5 = (f32[49,32,128]{2,1,0:T(8,128)}, f32[49,32,128]{2,1,0:T(8,128)}, u32[]{:S(2)}, u32[]{:S(2)}) collective-permute-start(f32[49,32,128]{2,1,0:T(8,128)} %slice.2425), channel_id=1, source_target_pairs={{0,1},{1,2},{2,3},{3,4},{4,5},{5,6},{6,7},{7,8},{8,9},{9,10},{10,1... | collective-permute-start | bytes 2408456 | tf_op jit(solution)/shard_map/ppermute | solution.py:94
  10.7 11.7 %collective-permute-start.1 = (f32[49,16,128]{2,1,0:T(8,128)}, f32[49,16,128]{2,1,0:T(8,128)S(1)}, u32[]{:S(2)}, u32[]{:S(2)}) collective-permute-start(f32[49,16,128]{2,1,0:T(8,128)} %get-tuple-element.133), channel_id=1, source_target_pairs={{1,0},{2,1},{3,2},{4,3},{5,4},{6,5},{7,6},{8,7},{9,8},{10,9},{11,1... | collective-permute-start | bytes 1204232 | tf_op jit(solution)/shard_map/ppermute | solution.py:93
  16.7 11.8 %collective-permute-start = (f32[49,16,128]{2,1,0:T(8,128)}, f32[49,16,128]{2,1,0:T(8,128)S(1)}, u32[]{:S(2)}, u32[]{:S(2)}) collective-permute-start(f32[49,16,128]{2,1,0:T(8,128)} %get-tuple-element.134), channel_id=1, source_target_pairs={{0,1},{1,2},{2,3},{3,4},{4,5},{5,6},{6,7},{7,8},{8,9},{9,10},{10,1... | collective-permute-start | bytes 1204232 | tf_op jit(solution)/shard_map/ppermute | solution.py:92
  33.0 14.7 %collective-permute-start.2 = (f32[4,48,128]{2,1,0:T(8,128)S(1)}, f32[4,48,128]{2,1,0:T(8,128)S(1)}, u32[]{:S(2)}, u32[]{:S(2)}) collective-permute-start(f32[4,48,128]{2,1,0:T(8,128)S(1)} %get-tuple-element.219), channel_id=1, source_target_pairs={{0,17},{1,18},{2,19},{3,20},{4,21},{5,22},{6,23},{7,24},{8,25},{9,... | collective-permute-start | bytes 294920 | tf_op jit(solution)/shard_map/ppermute | solution.py:134
  43.7 8.1 %collective-permute-start.3 = (f32[4,64,128]{2,1,0:T(8,128)S(1)}, f32[4,64,128]{2,1,0:T(8,128)S(1)}, u32[]{:S(2)}, u32[]{:S(2)}) collective-permute-start(f32[4,64,128]{2,1,0:T(8,128)S(1)} %slice.2423), channel_id=1, source_target_pairs={{112,0},{0,16},{16,32},{32,48},{48,64},{64,80},{80,96},{96,112},{1... | collective-permute-start | bytes 393224 | tf_op jit(solution)/shard_map/ppermute | solution.py:18
  45.7 9.9 %collective-permute-start.4 = (f32[4,48,128]{2,1,0:T(8,128)S(1)}, f32[4,48,128]{2,1,0:T(8,128)S(1)}, u32[]{:S(2)}, u32[]{:S(2)}) collective-permute-start(f32[4,48,128]{2,1,0:T(8,128)S(1)} %get-tuple-element.218), channel_id=1, source_target_pairs={{1,16},{2,17},{3,18},{4,19},{5,20},{6,21},{7,22},{8,23},{9,24},{10... | collective-permute-start | bytes 294920 | tf_op jit(solution)/shard_map/ppermute | solution.py:136
  69.8 6.0 %collective-permute-start.7 = (f32[4,96,128]{2,1,0:T(8,128)S(1)}, f32[4,96,128]{2,1,0:T(8,128)S(1)}, u32[]{:S(2)}, u32[]{:S(2)}) collective-permute-start(f32[4,96,128]{2,1,0:T(8,128)S(1)} %slice_add_fusion.3), channel_id=1, source_target_pairs={{16,0},{32,16},{48,32},{64,48},{80,64},{96,80},{112,96},{0,112},{1... | collective-permute-start | bytes 589832 | tf_op jit(solution)/shard_map/ppermute | solution.py:18
  78.6 1.3 %copy-start.3 = (f32[4,96,128]{2,1,0:T(8,128)}, f32[4,96,128]{2,1,0:T(8,128)S(1)}, u32[]{:S(2)}) copy-start(f32[4,96,128]{2,1,0:T(8,128)S(1)} %fusion.311) | copy-start | bytes 589828
  79.8 1.3 %slice-start = ((f32[4,96,128]{2,1,0:T(8,128)}), f32[4,64,128]{2,1,0:T(8,128)S(1)}, s32[]{:S(2)}) async-start(f32[4,96,128]{2,1,0:T(8,128)} %copy-done.3), calls=%async_computation.1 | async-start | bytes 262144 | tf_op jit(solution)/shard_map/slice | solution.py:84

commit v2 on v1

--- a/solution.py
+++ b/solution.py
@@ -89,12 +89,9 @@
     near = band(2 * steps)
     far = band(fwd_need[0])
 
-    before = lax.ppermute(packed[:, rows - near :], "tile", [(i, i + 1) for i in range(tiles - 1)])
-    after = lax.ppermute(packed[:, :near], "tile", [(i + 1, i) for i in range(tiles - 1)])
-    before_far = lax.ppermute(packed[:, rows - far : rows - near], "tile", [(i, i + 1) for i in range(tiles - 1)])
-    after_far = lax.ppermute(packed[:, near:far], "tile", [(i + 1, i) for i in range(tiles - 1)])
-    narrow = jnp.concatenate([before, packed, after], axis=1)
-    wide = jnp.concatenate([before_far, before, packed, after, after_far], axis=1)
+    before = lax.ppermute(packed[:, rows - far :], "tile", [(i, i + 1) for i in range(tiles - 1)])
+    after = lax.ppermute(packed[:, :far], "tile", [(i + 1, i) for i in range(tiles - 1)])
+    wide = jnp.concatenate([before, packed, after], axis=1)
 
     def fields(block, have):
         ext = rows + 2 * have
@@ -104,7 +101,7 @@
         mask = ((row >= 0) & (row < tiles * rows)).astype(jnp.float32)[:, None]
         return flow, drive, block[-1], mask, have
 
-    sweep_fields = [fields(narrow, near), fields(wide, far)]
+    sweep_fields = [fields(wide, far)] * 2
     sweep_bands = [
         [band(2 * (steps - m)) for m in range(steps)],
         [band(need) for need in fwd_need],
@@ -168,8 +165,18 @@
     flat = adjoint.reshape(steps, count_f * rows * columns)
     table = coefficient_table(harmonics, phase, periods)
     terms = jnp.dot(table, flat, precision=lax.Precision.HIGHEST)
-    parts = lax.all_to_all(terms.reshape(slabs, 2 * H // slabs, count_f, rows, columns), "slab", 0, 0, tiled=True)
-    return jnp.sum(parts, axis=0, keepdims=True)
+    ring = 4
+    rings = slabs // ring
+    here = lax.axis_index("slab")
+    split = terms.reshape(rings, ring, 2 * H // slabs, count_f, rows, columns).swapaxes(0, 1)
+    groups = [list(range(g * ring, (g + 1) * ring)) for g in range(rings)]
+    parts = lax.all_to_all(split, "slab", 0, 0, tiled=True, axis_index_groups=groups)
+    partial = jnp.sum(parts, axis=0)
+    total = lax.dynamic_index_in_dim(partial, here // ring, 0, keepdims=False)
+    for shift in range(1, rings):
+        away = lax.dynamic_index_in_dim(partial, (here // ring + shift) % rings, 0, keepdims=False)
+        total = total + passed_along(away, "slab", shift * ring)
+    return total[None]
 
 
 def solution(mesh):

time: 119 us -> 130 us (1.092); the launches traced: 117 us -> 129 us
  waiting for transfers between devices: 22.2 us -> 59.8 us
  blocking collectives: 31.3 us -> 0 us
  starting transfers between devices: 30.3 us -> 34 us
    all_to_all x1 -> x0, blocking collectives: 31.3 us -> none  [on_device(): lax.all_to_all(terms.reshape(slabs, 2 * H // slabs, count_f, rows, column...]
    all_to_all x0 -> x1, waiting for transfers between devices: none -> 27.6 us  [on_device(): lax.all_to_all(split, 'slab', 0, 0, tiled=True, axis_index_groups=groups)]
    ppermute x4 -> x2, starting transfers between devices: 15 us -> 7.95 us  [the longest x1 6.04 us: on_device(): lax.ppermute(packed[:, :far], 'tile', [(i + 1, i) for i in range(tiles -...]
    ppermute x2 -> x3, waiting for transfers between devices: 8.95 us -> 15.1 us  [passed_along(): return lax.ppermute(block, axis, route)]
    all_to_all x0 -> x1, starting transfers between devices: none -> 5.13 us  [on_device(): lax.all_to_all(split, 'slab', 0, 0, tiled=True, axis_index_groups=groups)]
    ppermute x4 -> x2, waiting for transfers between devices: 9.54 us -> 13.7 us  [the longest x1 11.9 us: on_device(): lax.ppermute(packed[:, rows - far:], 'tile', [(i, i + 1) for i in range(t...]
    ppermute x1, starting transfers between devices: 10.6 us -> 13.8 us  [on_device(): lax.ppermute(own[:, rows - far:], ('slab', 'tile'), [(j * tiles + t, ahea...]
    ppermute x2 -> x3, starting transfers between devices: 2.6 us -> 4.98 us  [passed_along(): return lax.ppermute(block, axis, route)]
  transfers between devices with their start and end apart: 8 -> 8, of which waited for: 5 -> 7; matrix products, arithmetic and copies ran while one was open for 6% -> 1% of each run, Pallas kernels for 0% -> 0%
where the time goes in v2:
time: 130 us; the launch traced here: 129 us
  waiting for transfers between devices  59.8 us (46%)
  starting transfers between devices  34 us (26%)
  other arithmetic  25.1 us (19%)
  local copies, waits for them, and re-layouts  7.25 us (6%)
  matrix products  2.33 us (2%)
    all_to_all x1, waiting for transfers between devices, on_device(): lax.all_to_all(split, 'slab', 0, 0, tiled=True, axis_index_groups=groups)  27.6 us
    ppermute x3, waiting for transfers between devices, passed_along(): return lax.ppermute(block, axis, route)  15.1 us
    ppermute x1, starting transfers between devices, on_device(): lax.ppermute(own[:, rows - far:], ('slab', 'tile'), [(j * tiles + t, ahea...  13.8 us
    ppermute x1, waiting for transfers between devices, on_device(): lax.ppermute(packed[:, rows - far:], 'tile', [(i, i + 1) for i in range(t...  11.9 us
    mul x28, other arithmetic, adjoint_rate(): flux_y = pad_grid(speed_y * state)  8.5 us
    ppermute x1, starting transfers between devices, on_device(): lax.ppermute(packed[:, :far], 'tile', [(i + 1, i) for i in range(tiles -...  6.04 us
    all_to_all x1, starting transfers between devices, on_device(): lax.all_to_all(split, 'slab', 0, 0, tiled=True, axis_index_groups=groups)  5.13 us
    ppermute x3, starting transfers between devices, passed_along(): return lax.ppermute(block, axis, route)  4.98 us
  transfers between devices with their start and end apart: 8, of which 7 were waited for; matrix products, arithmetic and copies ran while one was open for 1% of the time, Pallas kernels for 0%

profile of v2, /device:TPU:16, one launch (start us, length us, event | category | flops | bytes accessed | tf_op | source)
XLA Modules:
  0.0 129.5 jit_solution(18043670376332361900)
XLA Ops:
  0.0 1.5 %pad_maximum_fusion.1 = f32[49,64,128]{2,1,0:T(8,128)S(1)} fusion(f32[1,64,128]{2,1,0:T(8,128)} %bitcast.217, f32[32,64,128]{2,1,0:T(8,128)} %bitcast.185, f32[16,64,128]{2,1,0:T(8,128)} %bitcast.197), kind=kLoop, calls=%fused_computation.2 | loop fusion | flops 802816 | bytes 3211264 | tf_op jit(solution)/shard_map/concatenate | solution.py:75
  1.5 1.6 %fusion.577 = (f32[49,48,128]{2,1,0:T(8,128)}, f32[49,48,128]{2,1,0:T(8,128)}) fusion(f32[49,64,128]{2,1,0:T(8,128)S(1)} %pad_maximum_fusion.1), kind=kLoop, calls=%fused_computation.1169 | loop fusion | bytes 4816896 | tf_op jit(solution)/shard_map/slice | solution.py:92
  3.1 1.9 %collective-permute-start = (f32[49,48,128]{2,1,0:T(8,128)}, f32[49,48,128]{2,1,0:T(8,128)S(1)}, u32[]{:S(2)}, u32[]{:S(2)}) collective-permute-start(f32[49,48,128]{2,1,0:T(8,128)} %get-tuple-element.128), channel_id=1, source_target_pairs={{0,1},{1,2},{2,3},{3,4},{4,5},{5,6},{6,7},{7,8},{8,9},{9,10},{10,1... | collective-permute-start | bytes 3612680 | tf_op jit(solution)/shard_map/ppermute | solution.py:92
  5.0 6.0 %collective-permute-start.1 = (f32[49,48,128]{2,1,0:T(8,128)}, f32[49,48,128]{2,1,0:T(8,128)S(1)}, u32[]{:S(2)}, u32[]{:S(2)}) collective-permute-start(f32[49,48,128]{2,1,0:T(8,128)} %get-tuple-element.129), channel_id=1, source_target_pairs={{1,0},{2,1},{3,2},{4,3},{5,4},{6,5},{7,6},{8,7},{9,8},{10,9},{11,1... | collective-permute-start | bytes 3612680 | tf_op jit(solution)/shard_map/ppermute | solution.py:93
  11.8 11.9 %collective-permute-done = f32[49,48,128]{2,1,0:T(8,128)S(1)} collective-permute-done((f32[49,48,128]{2,1,0:T(8,128)}, f32[49,48,128]{2,1,0:T(8,128)S(1)}, u32[]{:S(2)}, u32[]{:S(2)}) %collective-permute-start) | collective-permute-done | bytes 1204256 | tf_op jit(solution)/shard_map/ppermute | solution.py:92
  23.6 1.8 %collective-permute-done.1 = f32[49,48,128]{2,1,0:T(8,128)S(1)} collective-permute-done((f32[49,48,128]{2,1,0:T(8,128)}, f32[49,48,128]{2,1,0:T(8,128)S(1)}, u32[]{:S(2)}, u32[]{:S(2)}) %collective-permute-start.1) | collective-permute-done | bytes 1204256 | tf_op jit(solution)/shard_map/ppermute | solution.py:93
  25.4 1.5 %pad_maximum_fusion = f32[49,160,128]{2,1,0:T(8,128)S(1)} fusion(f32[49,48,128]{2,1,0:T(8,128)S(1)} %collective-permute-done.1, f32[1,64,128]{2,1,0:T(8,128)S(1)} %bitcast.218, f32[32,64,128]{2,1,0:T(8,128)S(1)} %bitcast.186, f32[16,64,128]{2,1,0:T(8,128)} %bitcast.198, f32[49,48,128]{2,1,0:T(8,128)S(1)} %collective-permute-done), kind=kLoop, calls=%fused_computation | loop fusion | flops 4014080 | bytes 8028160 | tf_op jit(solution)/shard_map/concatenate | solution.py:94
  27.1 0.9 copy-done.1
  32.4 13.8 %collective-permute-start.2 = (f32[4,48,128]{2,1,0:T(8,128)S(1)}, f32[4,48,128]{2,1,0:T(8,128)S(1)}, u32[]{:S(2)}, u32[]{:S(2)}) collective-permute-start(f32[4,48,128]{2,1,0:T(8,128)S(1)} %get-tuple-element.214), channel_id=1, source_target_pairs={{0,17},{1,18},{2,19},{3,20},{4,21},{5,22},{6,23},{7,24},{8,25},{9,... | collective-permute-start | bytes 294920 | tf_op jit(solution)/shard_map/ppermute | solution.py:131
  46.3 1.6 %collective-permute-start.3 = (f32[4,64,128]{2,1,0:T(8,128)S(1)}, f32[4,64,128]{2,1,0:T(8,128)S(1)}, u32[]{:S(2)}, u32[]{:S(2)}) collective-permute-start(f32[4,64,128]{2,1,0:T(8,128)S(1)} %slice.2434), channel_id=1, source_target_pairs={{112,0},{0,16},{16,32},{32,48},{48,64},{64,80},{80,96},{96,112},{1... | collective-permute-start | bytes 393224 | tf_op jit(solution)/shard_map/ppermute | solution.py:18
  47.8 2.1 %collective-permute-start.4 = (f32[4,48,128]{2,1,0:T(8,128)S(1)}, f32[4,48,128]{2,1,0:T(8,128)S(1)}, u32[]{:S(2)}, u32[]{:S(2)}) collective-permute-start(f32[4,48,128]{2,1,0:T(8,128)S(1)} %get-tuple-element.213), channel_id=1, source_target_pairs={{1,16},{2,17},{3,18},{4,19},{5,20},{6,21},{7,22},{8,23},{9,24},{10... | collective-permute-start | bytes 294920 | tf_op jit(solution)/shard_map/ppermute | solution.py:133
  50.1 3.8 %collective-permute-done.3 = f32[4,64,128]{2,1,0:T(8,128)S(1)} collective-permute-done((f32[4,64,128]{2,1,0:T(8,128)S(1)}, f32[4,64,128]{2,1,0:T(8,128)S(1)}, u32[]{:S(2)}, u32[]{:S(2)}) %collective-permute-start.3) | collective-permute-done | bytes 131104 | tf_op jit(solution)/shard_map/ppermute | solution.py:18
  53.9 3.5 %collective-permute-done.4 = f32[4,48,128]{2,1,0:T(8,128)S(1)} collective-permute-done((f32[4,48,128]{2,1,0:T(8,128)S(1)}, f32[4,48,128]{2,1,0:T(8,128)S(1)}, u32[]{:S(2)}, u32[]{:S(2)}) %collective-permute-start.4) | collective-permute-done | bytes 98336 | tf_op jit(solution)/shard_map/ppermute | solution.py:133
  57.5 0.4 fusion.2
  58.3 0.4 fusion.1
  59.1 0.4 fusion
  60.0 0.4 fusion.6
  60.8 0.4 fusion.5
  61.6 0.4 fusion.4
  62.3 0.4 fusion.3
  63.7 0.4 broadcast_multiply_fusion.8
  64.1 0.4 broadcast_multiply_fusion.5
  69.9 2.3 %collective-permute-start.5 = (f32[4,96,128]{2,1,0:T(8,128)S(1)}, f32[4,96,128]{2,1,0:T(8,128)S(1)}, u32[]{:S(2)}, u32[]{:S(2)}) collective-permute-start(f32[4,96,128]{2,1,0:T(8,128)S(1)} %slice_add_fusion.3), channel_id=1, source_target_pairs={{16,0},{32,16},{48,32},{64,48},{80,64},{96,80},{112,96},{0,112},{1... | collective-permute-start | bytes 589832 | tf_op jit(solution)/shard_map/ppermute | solution.py:18
  72.3 4.1 %collective-permute-done.5 = f32[4,96,128]{2,1,0:T(8,128)S(1)} collective-permute-done((f32[4,96,128]{2,1,0:T(8,128)S(1)}, f32[4,96,128]{2,1,0:T(8,128)S(1)}, u32[]{:S(2)}, u32[]{:S(2)}) %collective-permute-start.5) | collective-permute-done | bytes 196640 | tf_op jit(solution)/shard_map/ppermute | solution.py:18
  82.0 1.6 %stack.41 = f32[8,32768]{1,0:T(8,128)S(1)} concatenate(f32[1,32768]{1,0:T(1,128)S(1)} %bitcast.232, f32[1,32768]{1,0:T(1,128)S(1)} %bitcast.231, f32[1,32768]{1,0:T(1,128)S(1)} %bitcast.237, f32[1,32768]{1,0:T(1,128)S(1)} %bitcast.236, f32[1,32768]{1,0:T(1,128)S(1)} %bitcast.230, f32[1,32768]{1,0:T(1,128)S(1)} %bitcast.235, f32[1,32768]{1,0:T(1,128)S(1)} %bitcast.234, ...), dimensions={0} | concatenate | bytes 2097152 | tf_op jit(solution)/shard_map/stack | solution.py:163
  83.7 2.3 %convolution_bitcast_fusion = f32[4,2,2,4,64,128]{5,0,4,3,2,1:T(4,128)S(1)} fusion(f32[4,64,128,8,1,1]{2,3,1,0,5,4:T(8,128)S(1)} %bitcast.229, f32[2,4,1,8]{3,1,2,0:T(4,128)S(1)} %get-tuple-element.218, f32[2,4,1,8]{3,1,2,0:T(4,128)S(1)} %get-tuple-element.217), kind=kOutput, calls=%fused_computation.1 | convolution fusion | flops 50331904 | bytes 3146240 | tf_op jit(solution)/shard_map/dot_general | solution.py:167
  86.0 1.6 %copy.5 = f32[4,2,2,4,64,128]{5,4,3,2,1,0:T(8,128)} copy(f32[4,2,2,4,64,128]{5,0,4,3,2,1:T(4,128)S(1)} %convolution_bitcast_fusion) | data formatting | bytes 4194304 | tf_op jit(solution)/shard_map/transpose | solution.py:171
  87.6 5.1 %all-to-all-start = ((f32[4,2,2,4,64,128]{5,4,3,2,1,0:T(8,128)}), f32[4,2,2,4,64,128]{5,4,3,2,1,0:T(8,128)S(1)}, u32[]{:S(2)}, u32[]{:S(2)}) async-start(f32[4,2,2,4,64,128]{5,4,3,2,1,0:T(8,128)} %copy.5), calls=%async_computation | async-start | bytes 4194304 | tf_op jit(solution)/shard_map/all_to_all | solution.py:173
  92.7 27.6 %all-to-all-done = f32[4,2,2,4,64,128]{5,4,3,2,1,0:T(8,128)S(1)} async-done(((f32[4,2,2,4,64,128]{5,4,3,2,1,0:T(8,128)}), f32[4,2,2,4,64,128]{5,4,3,2,1,0:T(8,128)S(1)}, u32[]{:S(2)}, u32[]{:S(2)}) %all-to-all-start) | async-done | bytes 2097184 | tf_op jit(solution)/shard_map/all_to_all | solution.py:173
  120.5 1.1 collective-permute-start.6
  121.6 7.1 %collective-permute-done.6 = f32[2,4,64,128]{3,2,1,0:T(8,128)S(1)} collective-permute-done((f32[2,4,64,128]{3,2,1,0:T(8,128)S(1)}, f32[2,4,64,128]{3,2,1,0:T(8,128)S(1)}, u32[]{:S(2)}, u32[]{:S(2)}) %collective-permute-start.6) | collective-permute-done | bytes 262176 | tf_op jit(solution)/shard_map/ppermute | solution.py:18
  128.8 0.7 fusion.109
  (150 shorter events, 19.3 us)
Async XLA Ops:
  1.5 10.1 %copy-start.5 = (s32[8]{0:T(128)S(1)}, s32[8]{0:T(128)}, u32[]{:S(2)}) copy-start(s32[8]{0:T(128)} %param.7) | copy-start | bytes 100
  1.5 23.9 %copy-start = (f32[8,4,64,128]{3,2,1,0:T(8,128)S(1)}, f32[8,4,64,128]{3,2,1,0:T(8,128)}, u32[]{:S(2)}) copy-start(f32[8,4,64,128]{3,2,1,0:T(8,128)} %param.5) | copy-start | bytes 3145732
  1.5 23.9 %copy-start.2 = (f32[64,128]{1,0:T(8,128)S(1)}, f32[64,128]{1,0:T(8,128)}, u32[]{:S(2)}) copy-start(f32[64,128]{1,0:T(8,128)} %param.6) | copy-start | bytes 98308
  3.1 20.5 %collective-permute-start = (f32[49,48,128]{2,1,0:T(8,128)}, f32[49,48,128]{2,1,0:T(8,128)S(1)}, u32[]{:S(2)}, u32[]{:S(2)}) collective-permute-start(f32[49,48,128]{2,1,0:T(8,128)} %get-tuple-element.128), channel_id=1, source_target_pairs={{0,1},{1,2},{2,3},{3,4},{4,5},{5,6},{6,7},{7,8},{8,9},{9,10},{10,1... | collective-permute-start | bytes 3612680 | tf_op jit(solution)/shard_map/ppermute | solution.py:92
  5.0 20.4 %collective-permute-start.1 = (f32[49,48,128]{2,1,0:T(8,128)}, f32[49,48,128]{2,1,0:T(8,128)S(1)}, u32[]{:S(2)}, u32[]{:S(2)}) collective-permute-start(f32[49,48,128]{2,1,0:T(8,128)} %get-tuple-element.129), channel_id=1, source_target_pairs={{1,0},{2,1},{3,2},{4,3},{5,4},{6,5},{7,6},{8,7},{9,8},{10,9},{11,1... | collective-permute-start | bytes 3612680 | tf_op jit(solution)/shard_map/ppermute | solution.py:93
  27.0 1.0 copy-start.1
  32.4 17.7 %collective-permute-start.2 = (f32[4,48,128]{2,1,0:T(8,128)S(1)}, f32[4,48,128]{2,1,0:T(8,128)S(1)}, u32[]{:S(2)}, u32[]{:S(2)}) collective-permute-start(f32[4,48,128]{2,1,0:T(8,128)S(1)} %get-tuple-element.214), channel_id=1, source_target_pairs={{0,17},{1,18},{2,19},{3,20},{4,21},{5,22},{6,23},{7,24},{8,25},{9,... | collective-permute-start | bytes 294920 | tf_op jit(solution)/shard_map/ppermute | solution.py:131
  46.3 7.7 %collective-permute-start.3 = (f32[4,64,128]{2,1,0:T(8,128)S(1)}, f32[4,64,128]{2,1,0:T(8,128)S(1)}, u32[]{:S(2)}, u32[]{:S(2)}) collective-permute-start(f32[4,64,128]{2,1,0:T(8,128)S(1)} %slice.2434), channel_id=1, source_target_pairs={{112,0},{0,16},{16,32},{32,48},{48,64},{64,80},{80,96},{96,112},{1... | collective-permute-start | bytes 393224 | tf_op jit(solution)/shard_map/ppermute | solution.py:18
  47.8 9.6 %collective-permute-start.4 = (f32[4,48,128]{2,1,0:T(8,128)S(1)}, f32[4,48,128]{2,1,0:T(8,128)S(1)}, u32[]{:S(2)}, u32[]{:S(2)}) collective-permute-start(f32[4,48,128]{2,1,0:T(8,128)S(1)} %get-tuple-element.213), channel_id=1, source_target_pairs={{1,16},{2,17},{3,18},{4,19},{5,20},{6,21},{7,22},{8,23},{9,24},{10... | collective-permute-start | bytes 294920 | tf_op jit(solution)/shard_map/ppermute | solution.py:133
  50.1 18.6 %copy-start.3 = (f32[112,128]{1,0:T(8,128)}, f32[112,128]{1,0:T(8,128)S(1)}, u32[]{:S(2)}) copy-start(f32[112,128]{1,0:T(8,128)S(1)} %maximum_bitcast_fusion.3) | copy-start | bytes 172036
  69.0 0.8 slice-start
  69.9 6.6 %collective-permute-start.5 = (f32[4,96,128]{2,1,0:T(8,128)S(1)}, f32[4,96,128]{2,1,0:T(8,128)S(1)}, u32[]{:S(2)}, u32[]{:S(2)}) collective-permute-start(f32[4,96,128]{2,1,0:T(8,128)S(1)} %slice_add_fusion.3), channel_id=1, source_target_pairs={{16,0},{32,16},{48,32},{64,48},{80,64},{96,80},{112,96},{0,112},{1... | collective-permute-start | bytes 589832 | tf_op jit(solution)/shard_map/ppermute | solution.py:18
  79.2 0.7 copy-start.4
  81.1 0.9 slice-start.1
  87.6 32.7 %all-to-all-start = ((f32[4,2,2,4,64,128]{5,4,3,2,1,0:T(8,128)}), f32[4,2,2,4,64,128]{5,4,3,2,1,0:T(8,128)S(1)}, u32[]{:S(2)}, u32[]{:S(2)}) async-start(f32[4,2,2,4,64,128]{5,4,3,2,1,0:T(8,128)} %copy.5), calls=%async_computation | async-start | bytes 4194304 | tf_op jit(solution)/shard_map/all_to_all | solution.py:173
  120.5 8.2 %collective-permute-start.6 = (f32[2,4,64,128]{3,2,1,0:T(8,128)S(1)}, f32[2,4,64,128]{3,2,1,0:T(8,128)S(1)}, u32[]{:S(2)}, u32[]{:S(2)}) collective-permute-start(f32[2,4,64,128]{3,2,1,0:T(8,128)S(1)} %dynamic-slice_bitcast_fusion), channel_id=1, source_target_pairs={{64,0},{80,16},{96,32},{112,48},{0,64},{16,80},{32,96},{48,112},{6... | collective-permute-start | bytes 786440 | tf_op jit(solution)/shard_map/ppermute | solution.py:18

commit v3 on v1

--- a/solution.py
+++ b/solution.py
@@ -86,15 +86,11 @@
     tail = 2 * steps
     fwd_need = [tail + 4 * steps - 3 - 2 * m for m in range(steps)]
     fwd_need = [max(need, tail + 2 * m + 2) for m, need in enumerate(fwd_need)]
-    near = band(2 * steps)
     far = band(fwd_need[0])
 
-    before = lax.ppermute(packed[:, rows - near :], "tile", [(i, i + 1) for i in range(tiles - 1)])
-    after = lax.ppermute(packed[:, :near], "tile", [(i + 1, i) for i in range(tiles - 1)])
-    before_far = lax.ppermute(packed[:, rows - far : rows - near], "tile", [(i, i + 1) for i in range(tiles - 1)])
-    after_far = lax.ppermute(packed[:, near:far], "tile", [(i + 1, i) for i in range(tiles - 1)])
-    narrow = jnp.concatenate([before, packed, after], axis=1)
-    wide = jnp.concatenate([before_far, before, packed, after, after_far], axis=1)
+    before = lax.ppermute(packed[:, rows - far :], "tile", [(i, i + 1) for i in range(tiles - 1)])
+    after = lax.ppermute(packed[:, :far], "tile", [(i + 1, i) for i in range(tiles - 1)])
+    wide = jnp.concatenate([before, packed, after], axis=1)
 
     def fields(block, have):
         ext = rows + 2 * have
@@ -104,7 +100,7 @@
         mask = ((row >= 0) & (row < tiles * rows)).astype(jnp.float32)[:, None]
         return flow, drive, block[-1], mask, have
 
-    sweep_fields = [fields(narrow, near), fields(wide, far)]
+    sweep_fields = [fields(wide, far)] * 2
     sweep_bands = [
         [band(2 * (steps - m)) for m in range(steps)],
         [band(need) for need in fwd_need],

time: 119 us -> 122 us (1.025); the launches traced: 117 us -> 122 us
  waiting for transfers between devices: 22.2 us -> 25.2 us
  starting transfers between devices: 30.3 us -> 27.7 us
  blocking collectives: 31.3 us -> 33.6 us
    ppermute x4 -> x2, starting transfers between devices: 15 us -> 7.95 us  [the longest x1 6.04 us: on_device(): lax.ppermute(packed[:, :far], 'tile', [(i + 1, i) for i in range(tiles -...]
    ppermute x4 -> x2, waiting for transfers between devices: 9.54 us -> 13.8 us  [the longest x1 11.9 us: on_device(): lax.ppermute(packed[:, rows - far:], 'tile', [(i, i + 1) for i in range(t...]
    ppermute x1, starting transfers between devices: 10.6 us -> 13.8 us  [on_device(): lax.ppermute(own[:, rows - far:], ('slab', 'tile'), [(j * tiles + t, ahea...]
    all_to_all x1, blocking collectives: 31.3 us -> 33.6 us  [on_device(): lax.all_to_all(terms.reshape(slabs, 2 * H // slabs, count_f, rows, column...]
    slice x20, local copies, waits for them, and re-layouts: 0.61 us -> 2.41 us  [cut(): lax.slice_in_dim(field, have - want, have + rows + want, axis=field.ndim...]
    ppermute x2, starting transfers between devices: 2.6 us -> 3.85 us  [passed_along(): return lax.ppermute(block, axis, route)]
    concatenate x1, other arithmetic: 0.23 us -> 1.46 us  [on_device(): wide = jnp.concatenate([before, packed, after], axis=1)]
  transfers between devices with their start and end apart: 8 -> 6, of which waited for: 5 -> 5; matrix products, arithmetic and copies ran while one was open for 6% -> 1% of each run, Pallas kernels for 0% -> 0%
where the time goes in v3:
time: 122 us
  blocking collectives  33.6 us (28%)
  starting transfers between devices  27.7 us (23%)
  waiting for transfers between devices  25.2 us (21%)
  other arithmetic  25 us (20%)
  local copies, waits for them, and re-layouts  7.37 us (6%)
  matrix products  1.77 us (1%)
    all_to_all x1, blocking collectives, on_device(): lax.all_to_all(terms.reshape(slabs, 2 * H // slabs, count_f, rows, column...  33.6 us
    ppermute x1, starting transfers between devices, on_device(): lax.ppermute(own[:, rows - far:], ('slab', 'tile'), [(j * tiles + t, ahea...  13.8 us
    ppermute x1, waiting for transfers between devices, on_device(): lax.ppermute(packed[:, rows - far:], 'tile', [(i, i + 1) for i in range(t...  11.9 us
    mul x28, other arithmetic, adjoint_rate(): flux_y = pad_grid(speed_y * state)  8.49 us
    ppermute x2, waiting for transfers between devices, passed_along(): return lax.ppermute(block, axis, route)  7.97 us
    ppermute x1, starting transfers between devices, on_device(): lax.ppermute(packed[:, :far], 'tile', [(i + 1, i) for i in range(tiles -...  6.04 us
    add x14, other arithmetic, on_device(): state + first  4.68 us
    add x16, other arithmetic, on_device(): state = state + 0.5 * (first + second)  4.53 us
  transfers between devices with their start and end apart: 6, of which 5 were waited for; matrix products, arithmetic and copies ran while one was open for 1% of the time, Pallas kernels for 0%

profile of v3, /device:TPU:16, one launch (start us, length us, event | category | flops | bytes accessed | tf_op | source)
XLA Modules:
  0.0 121.7 jit_solution(13908626758904120075)
XLA Ops:
  0.0 1.5 %pad_maximum_fusion.1 = f32[49,64,128]{2,1,0:T(8,128)S(1)} fusion(f32[1,64,128]{2,1,0:T(8,128)} %bitcast.206, f32[32,64,128]{2,1,0:T(8,128)} %bitcast.174, f32[16,64,128]{2,1,0:T(8,128)} %bitcast.186), kind=kLoop, calls=%fused_computation.1 | loop fusion | flops 802816 | bytes 3211264 | tf_op jit(solution)/shard_map/concatenate | solution.py:75
  1.5 1.6 %fusion.577 = (f32[49,48,128]{2,1,0:T(8,128)}, f32[49,48,128]{2,1,0:T(8,128)}) fusion(f32[49,64,128]{2,1,0:T(8,128)S(1)} %pad_maximum_fusion.1), kind=kLoop, calls=%fused_computation.1166 | loop fusion | bytes 4816896 | tf_op jit(solution)/shard_map/slice | solution.py:91
  3.1 1.9 %collective-permute-start = (f32[49,48,128]{2,1,0:T(8,128)}, f32[49,48,128]{2,1,0:T(8,128)S(1)}, u32[]{:S(2)}, u32[]{:S(2)}) collective-permute-start(f32[49,48,128]{2,1,0:T(8,128)} %get-tuple-element.128), channel_id=1, source_target_pairs={{0,1},{1,2},{2,3},{3,4},{4,5},{5,6},{6,7},{7,8},{8,9},{9,10},{10,1... | collective-permute-start | bytes 3612680 | tf_op jit(solution)/shard_map/ppermute | solution.py:91
  5.0 6.0 %collective-permute-start.1 = (f32[49,48,128]{2,1,0:T(8,128)}, f32[49,48,128]{2,1,0:T(8,128)S(1)}, u32[]{:S(2)}, u32[]{:S(2)}) collective-permute-start(f32[49,48,128]{2,1,0:T(8,128)} %get-tuple-element.129), channel_id=1, source_target_pairs={{1,0},{2,1},{3,2},{4,3},{5,4},{6,5},{7,6},{8,7},{9,8},{10,9},{11,1... | collective-permute-start | bytes 3612680 | tf_op jit(solution)/shard_map/ppermute | solution.py:92
  11.7 11.9 %collective-permute-done = f32[49,48,128]{2,1,0:T(8,128)S(1)} collective-permute-done((f32[49,48,128]{2,1,0:T(8,128)}, f32[49,48,128]{2,1,0:T(8,128)S(1)}, u32[]{:S(2)}, u32[]{:S(2)}) %collective-permute-start) | collective-permute-done | bytes 1204256 | tf_op jit(solution)/shard_map/ppermute | solution.py:91
  23.6 1.8 %collective-permute-done.1 = f32[49,48,128]{2,1,0:T(8,128)S(1)} collective-permute-done((f32[49,48,128]{2,1,0:T(8,128)}, f32[49,48,128]{2,1,0:T(8,128)S(1)}, u32[]{:S(2)}, u32[]{:S(2)}) %collective-permute-start.1) | collective-permute-done | bytes 1204256 | tf_op jit(solution)/shard_map/ppermute | solution.py:92
  25.4 1.5 %pad_maximum_fusion = f32[49,160,128]{2,1,0:T(8,128)S(1)} fusion(f32[49,48,128]{2,1,0:T(8,128)S(1)} %collective-permute-done.1, f32[1,64,128]{2,1,0:T(8,128)S(1)} %bitcast.207, f32[32,64,128]{2,1,0:T(8,128)S(1)} %bitcast.175, f32[16,64,128]{2,1,0:T(8,128)} %bitcast.187, f32[49,48,128]{2,1,0:T(8,128)S(1)} %collective-permute-done), kind=kLoop, calls=%fused_computation | loop fusion | flops 4014080 | bytes 8028160 | tf_op jit(solution)/shard_map/concatenate | solution.py:93
  27.1 0.9 copy-done.1
  32.4 13.8 %collective-permute-start.2 = (f32[4,48,128]{2,1,0:T(8,128)S(1)}, f32[4,48,128]{2,1,0:T(8,128)S(1)}, u32[]{:S(2)}, u32[]{:S(2)}) collective-permute-start(f32[4,48,128]{2,1,0:T(8,128)S(1)} %get-tuple-element.214), channel_id=1, source_target_pairs={{0,17},{1,18},{2,19},{3,20},{4,21},{5,22},{6,23},{7,24},{8,25},{9,... | collective-permute-start | bytes 294920 | tf_op jit(solution)/shard_map/ppermute | solution.py:130
  46.2 1.6 %collective-permute-start.3 = (f32[4,64,128]{2,1,0:T(8,128)S(1)}, f32[4,64,128]{2,1,0:T(8,128)S(1)}, u32[]{:S(2)}, u32[]{:S(2)}) collective-permute-start(f32[4,64,128]{2,1,0:T(8,128)S(1)} %slice.2434), channel_id=1, source_target_pairs={{112,0},{0,16},{16,32},{32,48},{48,64},{64,80},{80,96},{96,112},{1... | collective-permute-start | bytes 393224 | tf_op jit(solution)/shard_map/ppermute | solution.py:18
  47.8 2.1 %collective-permute-start.4 = (f32[4,48,128]{2,1,0:T(8,128)S(1)}, f32[4,48,128]{2,1,0:T(8,128)S(1)}, u32[]{:S(2)}, u32[]{:S(2)}) collective-permute-start(f32[4,48,128]{2,1,0:T(8,128)S(1)} %get-tuple-element.213), channel_id=1, source_target_pairs={{1,16},{2,17},{3,18},{4,19},{5,20},{6,21},{7,22},{8,23},{9,24},{10... | collective-permute-start | bytes 294920 | tf_op jit(solution)/shard_map/ppermute | solution.py:132
  50.1 3.8 %collective-permute-done.3 = f32[4,64,128]{2,1,0:T(8,128)S(1)} collective-permute-done((f32[4,64,128]{2,1,0:T(8,128)S(1)}, f32[4,64,128]{2,1,0:T(8,128)S(1)}, u32[]{:S(2)}, u32[]{:S(2)}) %collective-permute-start.3) | collective-permute-done | bytes 131104 | tf_op jit(solution)/shard_map/ppermute | solution.py:18
  53.9 3.5 %collective-permute-done.4 = f32[4,48,128]{2,1,0:T(8,128)S(1)} collective-permute-done((f32[4,48,128]{2,1,0:T(8,128)S(1)}, f32[4,48,128]{2,1,0:T(8,128)S(1)}, u32[]{:S(2)}, u32[]{:S(2)}) %collective-permute-start.4) | collective-permute-done | bytes 98336 | tf_op jit(solution)/shard_map/ppermute | solution.py:132
  57.4 0.4 fusion.2
  57.9 0.4 multiply_add_fusion.4
  58.3 0.4 fusion.1
  58.7 0.4 multiply_add_fusion.2
  59.1 0.4 fusion
  60.0 0.4 fusion.6
  60.8 0.4 fusion.5
  61.5 0.4 fusion.4
  62.3 0.4 fusion.3
  64.1 0.4 broadcast_multiply_fusion.5
  69.9 2.3 %collective-permute-start.5 = (f32[4,96,128]{2,1,0:T(8,128)S(1)}, f32[4,96,128]{2,1,0:T(8,128)S(1)}, u32[]{:S(2)}, u32[]{:S(2)}) collective-permute-start(f32[4,96,128]{2,1,0:T(8,128)S(1)} %slice_add_fusion.3), channel_id=1, source_target_pairs={{16,0},{32,16},{48,32},{64,48},{80,64},{96,80},{112,96},{0,112},{1... | collective-permute-start | bytes 589832 | tf_op jit(solution)/shard_map/ppermute | solution.py:18
  72.3 4.1 %collective-permute-done.5 = f32[4,96,128]{2,1,0:T(8,128)S(1)} collective-permute-done((f32[4,96,128]{2,1,0:T(8,128)S(1)}, f32[4,96,128]{2,1,0:T(8,128)S(1)}, u32[]{:S(2)}, u32[]{:S(2)}) %collective-permute-start.5) | collective-permute-done | bytes 196640 | tf_op jit(solution)/shard_map/ppermute | solution.py:18
  77.1 0.7 slice.2534
  78.4 0.7 slice.2533
  83.4 1.6 %stack.41 = f32[8,32768]{1,0:T(8,128)S(1)} concatenate(f32[1,32768]{1,0:T(1,128)S(1)} %bitcast.221, f32[1,32768]{1,0:T(1,128)S(1)} %bitcast.220, f32[1,32768]{1,0:T(1,128)S(1)} %bitcast.226, f32[1,32768]{1,0:T(1,128)S(1)} %bitcast.225, f32[1,32768]{1,0:T(1,128)S(1)} %bitcast.219, f32[1,32768]{1,0:T(1,128)S(1)} %bitcast.224, f32[1,32768]{1,0:T(1,128)S(1)} %bitcast.223, ...), dimensions={0} | concatenate | bytes 2097152 | tf_op jit(solution)/shard_map/stack | solution.py:162
  85.0 1.8 %fusion.535 = f32[8,2,4,64,128]{4,0,3,2,1:T(8,128)S(1)} fusion(f32[4,64,128,8,1]{2,3,1,0,4:T(8,128)S(1)} %bitcast.218, f32[8,1,8]{2,0,1:T(8,128)S(1)} %get-tuple-element.218, f32[8,1,8]{2,0,1:T(8,128)S(1)} %get-tuple-element.217), kind=kOutput, calls=%fused_computation.1141 | convolution fusion | flops 50331904 | bytes 3146240 | tf_op jit(solution)/shard_map/dot_general | solution.py:166
  86.8 0.4 copy.5
  87.2 33.6 %all_to_all.5 = f32[8,2,4,64,128]{4,3,2,1,0:T(8,128)S(1)} all-to-all(f32[8,2,4,64,128]{4,3,2,1,0:T(8,128)S(1)} %copy.5), channel_id=1, replica_groups=mesh['slab'=8,'tile'=16] {'slab'}, dimensions={0} | all-to-all | bytes 4194304 | tf_op jit(solution)/shard_map/all_to_all | solution.py:167
  120.8 0.8 reduce_sum.9
  (148 shorter events, 18.6 us)
Async XLA Ops:
  1.5 23.9 %copy-start = (f32[8,4,64,128]{3,2,1,0:T(8,128)S(1)}, f32[8,4,64,128]{3,2,1,0:T(8,128)}, u32[]{:S(2)}) copy-start(f32[8,4,64,128]{3,2,1,0:T(8,128)} %param.5) | copy-start | bytes 3145732
  1.5 23.9 %copy-start.2 = (f32[64,128]{1,0:T(8,128)S(1)}, f32[64,128]{1,0:T(8,128)}, u32[]{:S(2)}) copy-start(f32[64,128]{1,0:T(8,128)} %param.6) | copy-start | bytes 98308
  3.1 20.5 %collective-permute-start = (f32[49,48,128]{2,1,0:T(8,128)}, f32[49,48,128]{2,1,0:T(8,128)S(1)}, u32[]{:S(2)}, u32[]{:S(2)}) collective-permute-start(f32[49,48,128]{2,1,0:T(8,128)} %get-tuple-element.128), channel_id=1, source_target_pairs={{0,1},{1,2},{2,3},{3,4},{4,5},{5,6},{6,7},{7,8},{8,9},{9,10},{10,1... | collective-permute-start | bytes 3612680 | tf_op jit(solution)/shard_map/ppermute | solution.py:91
  5.0 20.4 %collective-permute-start.1 = (f32[49,48,128]{2,1,0:T(8,128)}, f32[49,48,128]{2,1,0:T(8,128)S(1)}, u32[]{:S(2)}, u32[]{:S(2)}) collective-permute-start(f32[49,48,128]{2,1,0:T(8,128)} %get-tuple-element.129), channel_id=1, source_target_pairs={{1,0},{2,1},{3,2},{4,3},{5,4},{6,5},{7,6},{8,7},{9,8},{10,9},{11,1... | collective-permute-start | bytes 3612680 | tf_op jit(solution)/shard_map/ppermute | solution.py:92
  27.0 1.0 copy-start.1
  32.4 17.7 %collective-permute-start.2 = (f32[4,48,128]{2,1,0:T(8,128)S(1)}, f32[4,48,128]{2,1,0:T(8,128)S(1)}, u32[]{:S(2)}, u32[]{:S(2)}) collective-permute-start(f32[4,48,128]{2,1,0:T(8,128)S(1)} %get-tuple-element.214), channel_id=1, source_target_pairs={{0,17},{1,18},{2,19},{3,20},{4,21},{5,22},{6,23},{7,24},{8,25},{9,... | collective-permute-start | bytes 294920 | tf_op jit(solution)/shard_map/ppermute | solution.py:130
  46.2 7.7 %collective-permute-start.3 = (f32[4,64,128]{2,1,0:T(8,128)S(1)}, f32[4,64,128]{2,1,0:T(8,128)S(1)}, u32[]{:S(2)}, u32[]{:S(2)}) collective-permute-start(f32[4,64,128]{2,1,0:T(8,128)S(1)} %slice.2434), channel_id=1, source_target_pairs={{112,0},{0,16},{16,32},{32,48},{48,64},{64,80},{80,96},{96,112},{1... | collective-permute-start | bytes 393224 | tf_op jit(solution)/shard_map/ppermute | solution.py:18
  47.8 9.6 %collective-permute-start.4 = (f32[4,48,128]{2,1,0:T(8,128)S(1)}, f32[4,48,128]{2,1,0:T(8,128)S(1)}, u32[]{:S(2)}, u32[]{:S(2)}) collective-permute-start(f32[4,48,128]{2,1,0:T(8,128)S(1)} %get-tuple-element.213), channel_id=1, source_target_pairs={{1,16},{2,17},{3,18},{4,19},{5,20},{6,21},{7,22},{8,23},{9,24},{10... | collective-permute-start | bytes 294920 | tf_op jit(solution)/shard_map/ppermute | solution.py:132
  50.1 18.6 %copy-start.3 = (f32[112,128]{1,0:T(8,128)}, f32[112,128]{1,0:T(8,128)S(1)}, u32[]{:S(2)}) copy-start(f32[112,128]{1,0:T(8,128)S(1)} %maximum_bitcast_fusion.3) | copy-start | bytes 172036
  69.0 0.8 slice-start
  69.0 3.2 %copy-start.7 = (s32[8]{0:T(128)S(1)}, s32[8]{0:T(128)}, u32[]{:S(2)}) copy-start(s32[8]{0:T(128)} %param.7) | copy-start | bytes 100
  69.9 6.6 %collective-permute-start.5 = (f32[4,96,128]{2,1,0:T(8,128)S(1)}, f32[4,96,128]{2,1,0:T(8,128)S(1)}, u32[]{:S(2)}, u32[]{:S(2)}) collective-permute-start(f32[4,96,128]{2,1,0:T(8,128)S(1)} %slice_add_fusion.3), channel_id=1, source_target_pairs={{16,0},{32,16},{48,32},{64,48},{80,64},{96,80},{112,96},{0,112},{1... | collective-permute-start | bytes 589832 | tf_op jit(solution)/shard_map/ppermute | solution.py:18
  80.5 0.7 copy-start.4
  82.4 0.9 slice-start.1
  82.4 1.0 copy-start.5
  82.4 1.0 copy-start.6

commit v4 on v0

--- a/solution.py
+++ b/solution.py
@@ -72,18 +72,6 @@
     tiles = lax.axis_size("tile")
     periods = steps * slabs
 
-    packed = jnp.concatenate(
-        [base_flow.reshape(2 * steps, rows, columns), forcing.reshape(steps * count_f, rows, columns), damping[None]],
-        axis=0,
-    )
-    wide = with_neighbours(packed, "tile", 1)
-    ext = 3 * rows
-    flow = wide[: 2 * steps].reshape(2, steps, ext, columns)
-    drive = wide[2 * steps : 2 * steps + steps * count_f].reshape(steps, count_f, ext, columns)
-    damp = wide[-1]
-    row = lax.axis_index("tile") * rows - rows + jnp.arange(ext, dtype=jnp.int32)
-    mask = ((row >= 0) & (row < tiles * rows)).astype(jnp.float32)[:, None]
-
     def band(depth):
         return min(rows, -(-depth // 8) * 8)
 
@@ -96,6 +84,45 @@
     tail = 2 * steps
     fwd_need = [tail + 4 * steps - 3 - 2 * m for m in range(steps)]
     fwd_need = [max(need, tail + 2 * m + 2) for m, need in enumerate(fwd_need)]
+    step_depth = [band(fwd_need[0] + 2 * (steps - m) - 1) for m in range(steps)]
+    assert max(step_depth) <= rows
+    per_step = jnp.concatenate([base_flow.swapaxes(0, 1), forcing], axis=1)
+    runs = []
+    for m, d in enumerate(step_depth):
+        if runs and runs[-1][2] == d:
+            runs[-1][1] = m + 1
+        else:
+            runs.append([m, m + 1, d])
+
+    def edges(take):
+        pieces = [take(per_step[lo:hi], d).reshape(-1, columns) for lo, hi, d in runs]
+        return jnp.concatenate(pieces + [take(damping, step_depth[0])], axis=0)
+
+    down = lax.ppermute(edges(lambda x, d: x[..., rows - d :, :]), "tile", [(i, i + 1) for i in range(tiles - 1)])
+    up = lax.ppermute(edges(lambda x, d: x[..., :d, :]), "tile", [(i + 1, i) for i in range(tiles - 1)])
+
+    def placed(got, top):
+        blocks, at = [], 0
+        for lo, hi, d in runs:
+            size = (hi - lo) * per_step.shape[1] * d
+            block = got[at : at + size].reshape(hi - lo, per_step.shape[1], d, columns)
+            gap = ((0, 0), (0, 0), (rows - d, 0) if top else (0, rows - d), (0, 0))
+            blocks.append(jnp.pad(block, gap))
+            at += size
+        d = step_depth[0]
+        damp_part = jnp.pad(got[at : at + d], ((rows - d, 0) if top else (0, rows - d), (0, 0)))
+        return jnp.concatenate(blocks, axis=0), damp_part
+
+    before, damp_before = placed(down, True)
+    after, damp_after = placed(up, False)
+    wide = jnp.concatenate([before, per_step, after], axis=2)
+    ext = 3 * rows
+    flow = wide[:, :2].swapaxes(0, 1)
+    drive = wide[:, 2:]
+    damp = jnp.concatenate([damp_before, damping, damp_after], axis=0)
+    row = lax.axis_index("tile") * rows - rows + jnp.arange(ext, dtype=jnp.int32)
+    mask = ((row >= 0) & (row < tiles * rows)).astype(jnp.float32)[:, None]
+
     sweep_bands = [
         [band(fwd_need[0] + 2 * (steps - m)) for m in range(steps)],
         [band(need) for need in fwd_need],

time: 119 us -> 121 us (1.017)
  local copies, waits for them, and re-layouts: 3.24 us -> 13 us
  waiting for transfers between devices: 56.9 us -> 50.6 us
  blocking collectives: 22.6 us -> 20.9 us
    slice x1 -> x8, local copies, waits for them, and re-layouts: 0.14 us -> 7.82 us  [the longest x6 6.3 us: placed(): block = got[at:at + size].reshape(hi - lo, per_step.shape[1], d, columns)]
    ppermute x2, waiting for transfers between devices: 40.2 us -> 34 us  [the longest x1 20.7 us: on_device(): lax.ppermute(edges(lambda x, d: x[..., rows - d:, :]), 'tile', [(i, i + 1...]
    unnamed x10 -> x9, local copies, waits for them, and re-layouts: 0.07 us -> 1.87 us
    all_to_all x1, blocking collectives: 22.6 us -> 20.9 us  [on_device(): lax.all_to_all(terms.reshape(slabs, 2 * H // slabs, count_f, rows, column...]
    concatenate x2 -> x5, other arithmetic: 3.29 us -> 3.41 us  [the longest x3 1.33 us: on_device(): per_step = jnp.concatenate([base_flow.swapaxes(0, 1), forcing], axis=1)]
  transfers between devices with their start and end apart: 4 -> 4, of which waited for: 4 -> 4; matrix products, arithmetic and copies ran while one was open for 1% -> 3% of each run, Pallas kernels for 0% -> 0%
where the time goes in v4:
time: 121 us
  waiting for transfers between devices  50.6 us (42%)
  other arithmetic  28.6 us (24%)
  blocking collectives  20.9 us (17%)
  local copies, waits for them, and re-layouts  13 us (11%)
  starting transfers between devices  4.87 us (4%)
  matrix products  1.77 us (1%)
    all_to_all x1, blocking collectives, on_device(): lax.all_to_all(terms.reshape(slabs, 2 * H // slabs, count_f, rows, column...  20.9 us
    ppermute x1, waiting for transfers between devices, on_device(): lax.ppermute(edges(lambda x, d: x[..., rows - d:, :]), 'tile', [(i, i + 1...  20.7 us
    ppermute x2, waiting for transfers between devices, passed_along(): return lax.ppermute(block, axis, route)  16.7 us
    ppermute x1, waiting for transfers between devices, on_device(): lax.ppermute(edges(lambda x, d: x[..., :d, :]), 'tile', [(i + 1, i) for i...  13.2 us
    mul x28, other arithmetic, adjoint_rate(): flux_y = pad_grid(speed_y * state)  8.55 us
    slice x6, local copies, waits for them, and re-layouts, placed(): block = got[at:at + size].reshape(hi - lo, per_step.shape[1], d, columns)  6.3 us
    add x14, other arithmetic, on_device(): state + first  5.87 us
    add x16, other arithmetic, on_device(): state = state + 0.5 * (first + second)  5.53 us
  transfers between devices with their start and end apart: 4, of which 4 were waited for; matrix products, arithmetic and copies ran while one was open for 3% of the time, Pallas kernels for 0%

profile of v4, /device:TPU:64, one launch (start us, length us, event | category | flops | bytes accessed | tf_op | source)
XLA Modules:
  0.0 120.8 jit_solution(11797806144966020282)
XLA Ops:
  0.0 1.2 copy.45
  1.2 1.3 %fusion.10 = (f32[4,6,56,128]{3,2,1,0:T(8,128)S(1)}, f32[4,6,56,128]{3,2,1,0:T(8,128)S(1)}) fusion(f32[8,4,64,128]{3,2,1,0:T(8,128)} %param.5, f32[8,2,64,128]{3,2,1,0:T(8,128)S(1)} %bitcast.249), kind=kLoop, calls=%fused_computation.240 | loop fusion | flops 344064 | bytes 2949120 | tf_op jit(solution)/shard_map/concatenate | solution.py:89
  2.5 0.7 copy-done.2
  3.2 1.3 %pad_maximum_fusion.1 = (f32[2752,128]{1,0:T(8,128)S(1)}, f32[2752,128]{1,0:T(8,128)}) fusion(f32[64,128]{1,0:T(8,128)S(1)} %copy-done.2, f32[768,128]{1,0:T(8,128)S(1)} %bitcast.261, f32[576,128]{1,0:T(8,128)S(1)} %bitcast.264, f32[1344,128]{1,0:T(8,128)S(1)} %bitcast.255, f32[576,128]{1,0:T(8,128)S(1)} %bitcast.265, f32[1344,128]{1,0:T(8,128)S(1)} %bitcast.256), kind=kLoop, calls=%fused_computation.25 | loop fusion | flops 2113536 | bytes 5210112 | tf_op jit(solution)/shard_map/concatenate | solution.py:99
  4.5 1.9 %collective-permute-start.1 = (f32[2752,128]{1,0:T(8,128)}, f32[2752,128]{1,0:T(8,128)}, u32[]{:S(2)}, u32[]{:S(2)}) collective-permute-start(f32[2752,128]{1,0:T(8,128)} %get-tuple-element.198), channel_id=1, source_target_pairs={{1,0},{2,1},{3,2},{4,3},{5,4},{6,5},{7,6},{8,7},{9,8},{10,9},{11,1... | collective-permute-start | bytes 4227080 | tf_op jit(solution)/shard_map/ppermute | solution.py:102
  6.4 2.4 %collective-permute-start = (f32[2752,128]{1,0:T(8,128)S(1)}, f32[2752,128]{1,0:T(8,128)}, u32[]{:S(2)}, u32[]{:S(2)}) collective-permute-start(f32[2752,128]{1,0:T(8,128)S(1)} %get-tuple-element.197), channel_id=1, source_target_pairs={{0,1},{1,2},{2,3},{3,4},{4,5},{5,6},{6,7},{7,8},{8,9},{9,10},{10,1... | collective-permute-start | bytes 4227080 | tf_op jit(solution)/shard_map/ppermute | solution.py:101
  9.7 13.2 %collective-permute-done.1 = f32[2752,128]{1,0:T(8,128)} collective-permute-done((f32[2752,128]{1,0:T(8,128)}, f32[2752,128]{1,0:T(8,128)}, u32[]{:S(2)}, u32[]{:S(2)}) %collective-permute-start.1) | collective-permute-done | bytes 1409056 | tf_op jit(solution)/shard_map/ppermute | solution.py:102
  22.9 1.1 slice.2453
  24.0 1.0 slice.2452
  25.0 20.7 %collective-permute-done = f32[2752,128]{1,0:T(8,128)} collective-permute-done((f32[2752,128]{1,0:T(8,128)S(1)}, f32[2752,128]{1,0:T(8,128)}, u32[]{:S(2)}, u32[]{:S(2)}) %collective-permute-start) | collective-permute-done | bytes 1409056 | tf_op jit(solution)/shard_map/ppermute | solution.py:101
  45.8 1.1 slice.2448
  46.9 1.0 slice.2447
  48.0 1.0 slice.2454
  49.0 1.0 slice.2449
  49.9 0.8 fusion
  51.2 0.8 slice.2459
  52.0 0.8 slice.2460
  54.9 0.5 add_subtract_fusion
  55.6 0.5 fusion.17
  56.5 0.5 fusion.16
  57.0 0.4 multiply_add_fusion.4
  57.4 0.5 fusion.15
  58.7 0.5 add_subtract_fusion.1
  59.3 0.4 fusion.24
  60.6 9.0 %collective-permute-done.2 = f32[4,160,128]{2,1,0:T(8,128)S(1)} collective-permute-done((f32[4,160,128]{2,1,0:T(8,128)S(1)}, f32[4,160,128]{2,1,0:T(8,128)S(1)}, u32[]{:S(2)}, u32[]{:S(2)}) %collective-permute-start.2) | collective-permute-done | bytes 327712 | tf_op jit(solution)/shard_map/ppermute | solution.py:18
  70.4 0.4 fusion.22
  71.3 0.4 fusion.21
  82.0 7.6 %collective-permute-done.3 = f32[4,96,128]{2,1,0:T(8,128)S(1)} collective-permute-done((f32[4,96,128]{2,1,0:T(8,128)S(1)}, f32[4,96,128]{2,1,0:T(8,128)S(1)}, u32[]{:S(2)}, u32[]{:S(2)}) %collective-permute-start.3) | collective-permute-done | bytes 196640 | tf_op jit(solution)/shard_map/ppermute | solution.py:18
  95.2 1.6 %stack.41 = f32[8,32768]{1,0:T(8,128)S(1)} concatenate(f32[1,32768]{1,0:T(1,128)S(1)} %bitcast.267, f32[1,32768]{1,0:T(1,128)S(1)} %bitcast.266, f32[1,32768]{1,0:T(1,128)S(1)} %bitcast.272, f32[1,32768]{1,0:T(1,128)S(1)} %bitcast.271, f32[1,32768]{1,0:T(1,128)S(1)} %bitcast.254, f32[1,32768]{1,0:T(1,128)S(1)} %bitcast.270, f32[1,32768]{1,0:T(1,128)S(1)} %bitcast.269, ...), dimensions={0} | concatenate | bytes 2097152 | tf_op jit(solution)/shard_map/stack | solution.py:177
  96.8 1.8 %fusion.556 = f32[8,2,4,64,128]{4,0,3,2,1:T(8,128)S(1)} fusion(f32[4,64,128,8,1]{2,3,1,0,4:T(8,128)S(1)} %bitcast.253, f32[8,1,8]{2,0,1:T(8,128)S(1)} %get-tuple-element.227, f32[8,1,8]{2,0,1:T(8,128)S(1)} %get-tuple-element.226), kind=kOutput, calls=%fused_computation.1185 | convolution fusion | flops 50331904 | bytes 3146240 | tf_op jit(solution)/shard_map/dot_general | solution.py:181
  99.0 20.9 %all_to_all.5 = f32[8,2,4,64,128]{4,3,2,1,0:T(8,128)S(1)} all-to-all(f32[8,2,4,64,128]{4,3,2,1,0:T(8,128)S(1)} %copy.33), channel_id=1, replica_groups=mesh['slab'=8,'tile'=16] {'slab'}, dimensions={0} | all-to-all | bytes 4194304 | tf_op jit(solution)/shard_map/all_to_all | solution.py:182
  119.9 0.8 reduce_sum.9
  (144 shorter events, 22.6 us)
Async XLA Ops:
  0.0 2.4 %copy-start = (f32[8,4,64,128]{3,2,1,0:T(8,128)S(1)}, f32[8,4,64,128]{3,2,1,0:T(8,128)}, u32[]{:S(2)}) copy-start(f32[8,4,64,128]{3,2,1,0:T(8,128)} %param.5) | copy-start | bytes 3145732
  2.4 0.8 copy-start.2
  3.2 6.3 %copy-start.3 = (s32[8]{0:T(128)S(1)}, s32[8]{0:T(128)}, u32[]{:S(2)}) copy-start(s32[8]{0:T(128)} %param.7) | copy-start | bytes 100
  4.5 18.4 %collective-permute-start.1 = (f32[2752,128]{1,0:T(8,128)}, f32[2752,128]{1,0:T(8,128)}, u32[]{:S(2)}, u32[]{:S(2)}) collective-permute-start(f32[2752,128]{1,0:T(8,128)} %get-tuple-element.198), channel_id=1, source_target_pairs={{1,0},{2,1},{3,2},{4,3},{5,4},{6,5},{7,6},{8,7},{9,8},{10,9},{11,1... | collective-permute-start | bytes 4227080 | tf_op jit(solution)/shard_map/ppermute | solution.py:102
  6.4 39.4 %collective-permute-start = (f32[2752,128]{1,0:T(8,128)S(1)}, f32[2752,128]{1,0:T(8,128)}, u32[]{:S(2)}, u32[]{:S(2)}) collective-permute-start(f32[2752,128]{1,0:T(8,128)S(1)} %get-tuple-element.197), channel_id=1, source_target_pairs={{0,1},{1,2},{2,3},{3,4},{4,5},{5,6},{6,7},{7,8},{8,9},{9,10},{10,1... | collective-permute-start | bytes 4227080 | tf_op jit(solution)/shard_map/ppermute | solution.py:101
  60.2 9.4 %collective-permute-start.2 = (f32[4,160,128]{2,1,0:T(8,128)S(1)}, f32[4,160,128]{2,1,0:T(8,128)S(1)}, u32[]{:S(2)}, u32[]{:S(2)}) collective-permute-start(f32[4,160,128]{2,1,0:T(8,128)S(1)} %multiply_add_fusion.14), channel_id=1, source_target_pairs={{112,0},{0,16},{16,32},{32,48},{48,64},{64,80},{80,96},{96,112},{1... | collective-permute-start | bytes 983048 | tf_op jit(solution)/shard_map/ppermute | solution.py:18
  81.7 8.0 %collective-permute-start.3 = (f32[4,96,128]{2,1,0:T(8,128)S(1)}, f32[4,96,128]{2,1,0:T(8,128)S(1)}, u32[]{:S(2)}, u32[]{:S(2)}) collective-permute-start(f32[4,96,128]{2,1,0:T(8,128)S(1)} %slice_add_fusion.9), channel_id=1, source_target_pairs={{16,0},{32,16},{48,32},{64,48},{80,64},{96,80},{112,96},{0,112},{1... | collective-permute-start | bytes 589832 | tf_op jit(solution)/shard_map/ppermute | solution.py:18
  92.4 0.7 copy-start.1
  94.3 0.9 slice-start

commit v5 on v3

--- a/solution.py
+++ b/solution.py
@@ -84,9 +84,13 @@
         return lax.slice_in_dim(field, have - want, have + rows + want, axis=field.ndim - 2)
 
     tail = 2 * steps
-    fwd_need = [tail + 4 * steps - 3 - 2 * m for m in range(steps)]
-    fwd_need = [max(need, tail + 2 * m + 2) for m, need in enumerate(fwd_need)]
+    fwd_need = [0] * steps
+    fwd_need[-1] = 2 * steps - 1
+    for m in range(steps - 2, -1, -1):
+        fwd_need[m] = max(2 * m + 1, fwd_need[m + 1] + 2)
+    fwd_need = [max(need, 2 * m + 2) for m, need in enumerate(fwd_need)]
     far = band(fwd_need[0])
+    assert far <= rows
 
     before = lax.ppermute(packed[:, rows - far :], "tile", [(i, i + 1) for i in range(tiles - 1)])
     after = lax.ppermute(packed[:, :far], "tile", [(i + 1, i) for i in range(tiles - 1)])
@@ -101,6 +105,15 @@
         return flow, drive, block[-1], mask, have
 
     sweep_fields = [fields(wide, far)] * 2
+    def slab_start(own, shift, depth):
+        onward = lambda j, t: ((j + shift) % slabs) * tiles + t
+        both = ("slab", "tile")
+        up = lax.ppermute(own[:, rows - depth :], both,
+                          [(j * tiles + t, onward(j, t + 1)) for j in range(slabs) for t in range(tiles - 1)])
+        down = lax.ppermute(own[:, :depth], both,
+                            [(j * tiles + t + 1, onward(j, t)) for j in range(slabs) for t in range(tiles - 1)])
+        return jnp.concatenate([up, passed_along(own, "slab", shift), down], axis=1)
+
     sweep_bands = [
         [band(2 * (steps - m)) for m in range(steps)],
         [band(need) for need in fwd_need],
@@ -125,17 +138,11 @@
             second = forward_rate(state + first, speed_x, speed_y, damp_here, source, mask_here)
             state = state + 0.5 * (first + second)
         if sweep + 1 < SWEEPS:
-            own = cut(state, have, 0)
-            ahead = lambda j, t: ((j + 1) % slabs) * tiles + t
-            up = lax.ppermute(own[:, rows - far :], ("slab", "tile"),
-                              [(j * tiles + t, ahead(j, t + 1)) for j in range(slabs) for t in range(tiles - 1)])
-            down = lax.ppermute(own[:, :far], ("slab", "tile"),
-                                [(j * tiles + t + 1, ahead(j, t)) for j in range(slabs) for t in range(tiles - 1)])
-            start = jnp.concatenate([up, passed_along(own, "slab", 1), down], axis=1)
+            start = slab_start(cut(state, have, 0), 1, far)
             have = far
     response = record
     adj_bands = [
-        [band(tail + 2 * m + 2) for m in range(steps)],
+        [band(2 * m + 2) for m in range(steps)],
         [band(2 * m + 2) for m in range(steps)],
     ]
     flow, drive, damp, mask, held = sweep_fields[1]
@@ -157,7 +164,7 @@
             state = state + 0.5 * (first + second)
             record[step] = cut(state, have, 0)
         if sweep + 1 < SWEEPS:
-            start = passed_along(cut(state, have, tail), "slab", -1)
+            start = slab_start(cut(state, have, 0), -1, tail)
             have = tail
     adjoint = jnp.stack(record, axis=0)
     phase = lax.axis_index("slab") * steps + jnp.arange(steps, dtype=jnp.int32)

time: 122 us -> 111 us (0.910)
  waiting for transfers between devices: 25.2 us -> 18 us
  other arithmetic: 25 us -> 21.5 us
  local copies, waits for them, and re-layouts: 7.37 us -> 3.91 us
  starting transfers between devices: 27.7 us -> 31 us
  blocking collectives: 33.6 us -> 32.3 us
    ppermute x2 -> x4, starting transfers between devices: 15.9 us -> 21.4 us  [the longest x2 15.6 us: slab_start(): lax.ppermute(own[:, rows - depth:], both, [(j * tiles + t, onward(j, t +...]
    ppermute x1, waiting for transfers between devices: 11.9 us -> 7.98 us  [on_device(): lax.ppermute(packed[:, rows - far:], 'tile', [(i, i + 1) for i in range(t...]
    ppermute x2, waiting for transfers between devices: 7.97 us -> 4.33 us  [passed_along(): return lax.ppermute(block, axis, route)]
    ppermute x2, starting transfers between devices: 3.85 us -> 1.63 us  [passed_along(): return lax.ppermute(block, axis, route)]
    slice x20 -> x17, local copies, waits for them, and re-layouts: 2.41 us -> 0.4 us  [cut(): lax.slice_in_dim(field, have - want, have + rows + want, axis=field.ndim...]
    all_to_all x1, blocking collectives: 33.6 us -> 32.3 us  [on_device(): lax.all_to_all(terms.reshape(slabs, 2 * H // slabs, count_f, rows, column...]
    add x16 -> x15, other arithmetic: 4.53 us -> 3.99 us  [on_device(): state = state + 0.5 * (first + second)]
    ppermute x2 -> x4, waiting for transfers between devices: 3.5 us -> 3.9 us  [the longest x2 3.9 us: slab_start(): lax.ppermute(own[:, :depth], both, [(j * tiles + t + 1, onward(j, t)) for...]
  transfers between devices with their start and end apart: 6 -> 8, of which waited for: 5 -> 6; matrix products, arithmetic and copies ran while one was open for 1% -> 1% of each run, Pallas kernels for 0% -> 0%
where the time goes in v5:
time: 111 us; the launch traced here: 110 us
  blocking collectives  32.3 us (29%)
  starting transfers between devices  31 us (28%)
  other arithmetic  21.5 us (19%)
  waiting for transfers between devices  18 us (16%)
  local copies, waits for them, and re-layouts  3.91 us (4%)
  matrix products  1.77 us (2%)
    all_to_all x1, blocking collectives, on_device(): lax.all_to_all(terms.reshape(slabs, 2 * H // slabs, count_f, rows, column...  32.3 us
    ppermute x2, starting transfers between devices, slab_start(): lax.ppermute(own[:, rows - depth:], both, [(j * tiles + t, onward(j, t +...  15.6 us
    ppermute x1, waiting for transfers between devices, on_device(): lax.ppermute(packed[:, rows - far:], 'tile', [(i, i + 1) for i in range(t...  7.98 us
    mul x28, other arithmetic, adjoint_rate(): flux_y = pad_grid(speed_y * state)  7.64 us
    ppermute x1, starting transfers between devices, on_device(): lax.ppermute(packed[:, :far], 'tile', [(i + 1, i) for i in range(tiles -...  6.04 us
    ppermute x2, starting transfers between devices, slab_start(): lax.ppermute(own[:, :depth], both, [(j * tiles + t + 1, onward(j, t)) for...  5.84 us
    ppermute x2, waiting for transfers between devices, passed_along(): return lax.ppermute(block, axis, route)  4.33 us
    add x14, other arithmetic, on_device(): state + first  4.12 us
  transfers between devices with their start and end apart: 8, of which 6 were waited for; matrix products, arithmetic and copies ran while one was open for 1% of the time, Pallas kernels for 0%

profile of v5, /device:TPU:16, one launch (start us, length us, event | category | flops | bytes accessed | tf_op | source)
XLA Modules:
  0.0 109.6 jit_solution(16453718117727153904)
XLA Ops:
  0.0 1.6 %pad_maximum_fusion.1 = f32[49,64,128]{2,1,0:T(8,128)S(1)} fusion(f32[1,64,128]{2,1,0:T(8,128)} %bitcast.170, f32[32,64,128]{2,1,0:T(8,128)} %bitcast.137, f32[16,64,128]{2,1,0:T(8,128)} %bitcast.151), kind=kLoop, calls=%fused_computation.1 | loop fusion | flops 802816 | bytes 3211264 | tf_op jit(solution)/shard_map/concatenate | solution.py:75
  1.6 1.3 %fusion.581 = (f32[49,32,128]{2,1,0:T(8,128)}, f32[49,32,128]{2,1,0:T(8,128)}) fusion(f32[49,64,128]{2,1,0:T(8,128)S(1)} %pad_maximum_fusion.1), kind=kLoop, calls=%fused_computation.1149 | loop fusion | bytes 3211264 | tf_op jit(solution)/shard_map/slice | solution.py:95
  2.9 1.9 %collective-permute-start = (f32[49,32,128]{2,1,0:T(8,128)}, f32[49,32,128]{2,1,0:T(8,128)S(1)}, u32[]{:S(2)}, u32[]{:S(2)}) collective-permute-start(f32[49,32,128]{2,1,0:T(8,128)} %get-tuple-element.130), channel_id=1, source_target_pairs={{0,1},{1,2},{2,3},{3,4},{4,5},{5,6},{6,7},{7,8},{8,9},{9,10},{10,1... | collective-permute-start | bytes 2408456 | tf_op jit(solution)/shard_map/ppermute | solution.py:95
  4.9 6.0 %collective-permute-start.1 = (f32[49,32,128]{2,1,0:T(8,128)}, f32[49,32,128]{2,1,0:T(8,128)S(1)}, u32[]{:S(2)}, u32[]{:S(2)}) collective-permute-start(f32[49,32,128]{2,1,0:T(8,128)} %get-tuple-element.131), channel_id=1, source_target_pairs={{1,0},{2,1},{3,2},{4,3},{5,4},{6,5},{7,6},{8,7},{9,8},{10,9},{11,1... | collective-permute-start | bytes 2408456 | tf_op jit(solution)/shard_map/ppermute | solution.py:96
  11.1 8.0 %collective-permute-done = f32[49,32,128]{2,1,0:T(8,128)S(1)} collective-permute-done((f32[49,32,128]{2,1,0:T(8,128)}, f32[49,32,128]{2,1,0:T(8,128)S(1)}, u32[]{:S(2)}, u32[]{:S(2)}) %collective-permute-start) | collective-permute-done | bytes 802848 | tf_op jit(solution)/shard_map/ppermute | solution.py:95
  19.1 1.8 %collective-permute-done.1 = f32[49,32,128]{2,1,0:T(8,128)S(1)} collective-permute-done((f32[49,32,128]{2,1,0:T(8,128)}, f32[49,32,128]{2,1,0:T(8,128)S(1)}, u32[]{:S(2)}, u32[]{:S(2)}) %collective-permute-start.1) | collective-permute-done | bytes 802848 | tf_op jit(solution)/shard_map/ppermute | solution.py:96
  25.7 9.5 %collective-permute-start.2 = (f32[4,32,128]{2,1,0:T(8,128)S(1)}, f32[4,32,128]{2,1,0:T(8,128)S(1)}, u32[]{:S(2)}, u32[]{:S(2)}) collective-permute-start(f32[4,32,128]{2,1,0:T(8,128)S(1)} %get-tuple-element.203), channel_id=1, source_target_pairs={{0,17},{1,18},{2,19},{3,20},{4,21},{5,22},{6,23},{7,24},{8,25},{9,... | collective-permute-start | bytes 196616 | tf_op jit(solution)/shard_map/ppermute | solution.py:111
  35.2 1.6 %collective-permute-start.3 = (f32[4,64,128]{2,1,0:T(8,128)S(1)}, f32[4,64,128]{2,1,0:T(8,128)S(1)}, u32[]{:S(2)}, u32[]{:S(2)}) collective-permute-start(f32[4,64,128]{2,1,0:T(8,128)S(1)} %slice.2303), channel_id=1, source_target_pairs={{112,0},{0,16},{16,32},{32,48},{48,64},{64,80},{80,96},{96,112},{1... | collective-permute-start | bytes 393224 | tf_op jit(solution)/shard_map/ppermute | solution.py:18
  36.9 2.1 %collective-permute-start.4 = (f32[4,32,128]{2,1,0:T(8,128)S(1)}, f32[4,32,128]{2,1,0:T(8,128)S(1)}, u32[]{:S(2)}, u32[]{:S(2)}) collective-permute-start(f32[4,32,128]{2,1,0:T(8,128)S(1)} %get-tuple-element.202), channel_id=1, source_target_pairs={{1,16},{2,17},{3,18},{4,19},{5,20},{6,21},{7,22},{8,23},{9,24},{10... | collective-permute-start | bytes 196616 | tf_op jit(solution)/shard_map/ppermute | solution.py:113
  39.1 3.4 %collective-permute-done.3 = f32[4,64,128]{2,1,0:T(8,128)S(1)} collective-permute-done((f32[4,64,128]{2,1,0:T(8,128)S(1)}, f32[4,64,128]{2,1,0:T(8,128)S(1)}, u32[]{:S(2)}, u32[]{:S(2)}) %collective-permute-start.3) | collective-permute-done | bytes 131104 | tf_op jit(solution)/shard_map/ppermute | solution.py:18
  42.4 3.4 %collective-permute-done.4 = f32[4,32,128]{2,1,0:T(8,128)S(1)} collective-permute-done((f32[4,32,128]{2,1,0:T(8,128)S(1)}, f32[4,32,128]{2,1,0:T(8,128)S(1)}, u32[]{:S(2)}, u32[]{:S(2)}) %collective-permute-start.4) | collective-permute-done | bytes 65568 | tf_op jit(solution)/shard_map/ppermute | solution.py:113
  45.9 0.4 fusion.2
  46.2 0.3 multiply_add_fusion.4
  46.6 0.4 fusion.1
  46.9 0.3 multiply_add_fusion.2
  47.3 0.4 fusion
  47.6 0.3 multiply_add_fusion
  48.0 0.3 fusion.5
  48.6 0.3 fusion.4
  49.3 0.3 fusion.3
  51.4 0.3 broadcast_multiply_fusion.11
  52.1 0.3 broadcast_multiply_fusion.3
  55.6 6.0 %collective-permute-start.5 = (f32[4,16,128]{2,1,0:T(8,128)S(1)}, f32[4,16,128]{2,1,0:T(8,128)S(1)}, u32[]{:S(2)}, u32[]{:S(2)}) collective-permute-start(f32[4,16,128]{2,1,0:T(8,128)S(1)} %get-tuple-element.201), channel_id=1, source_target_pairs={{0,113},{1,114},{2,115},{3,116},{4,117},{5,118},{6,119},{7,120},{8... | collective-permute-start | bytes 98312 | tf_op jit(solution)/shard_map/ppermute | solution.py:111
  62.0 3.7 %collective-permute-start.7 = (f32[4,16,128]{2,1,0:T(8,128)S(1)}, f32[4,16,128]{2,1,0:T(8,128)S(1)}, u32[]{:S(2)}, u32[]{:S(2)}) collective-permute-start(f32[4,16,128]{2,1,0:T(8,128)S(1)} %get-tuple-element.200), channel_id=1, source_target_pairs={{1,112},{2,113},{3,114},{4,115},{5,116},{6,117},{7,118},{8,119},{9... | collective-permute-start | bytes 98312 | tf_op jit(solution)/shard_map/ppermute | solution.py:113
  65.7 1.0 collective-permute-done.6
  66.7 0.5 collective-permute-done.7
  68.3 0.3 broadcast_multiply_fusion.9
  72.6 1.6 %stack.41 = f32[8,32768]{1,0:T(8,128)S(1)} concatenate(f32[1,32768]{1,0:T(1,128)S(1)} %bitcast.187, f32[1,32768]{1,0:T(1,128)S(1)} %bitcast.186, f32[1,32768]{1,0:T(1,128)S(1)} %bitcast.192, f32[1,32768]{1,0:T(1,128)S(1)} %bitcast.191, f32[1,32768]{1,0:T(1,128)S(1)} %bitcast.185, f32[1,32768]{1,0:T(1,128)S(1)} %bitcast.190, f32[1,32768]{1,0:T(1,128)S(1)} %bitcast.189, ...), dimensions={0} | concatenate | bytes 2097152 | tf_op jit(solution)/shard_map/stack | solution.py:169
  74.2 1.8 %fusion.537 = f32[8,2,4,64,128]{4,0,3,2,1:T(8,128)S(1)} fusion(f32[4,64,128,8,1]{2,3,1,0,4:T(8,128)S(1)} %bitcast.184, f32[8,1,8]{2,0,1:T(8,128)S(1)} %get-tuple-element.206, f32[8,1,8]{2,0,1:T(8,128)S(1)} %get-tuple-element.205), kind=kOutput, calls=%fused_computation.1126 | convolution fusion | flops 50331904 | bytes 3146240 | tf_op jit(solution)/shard_map/dot_general | solution.py:173
  76.0 0.4 copy.5
  76.4 32.3 %all_to_all.5 = f32[8,2,4,64,128]{4,3,2,1,0:T(8,128)S(1)} all-to-all(f32[8,2,4,64,128]{4,3,2,1,0:T(8,128)S(1)} %copy.5), channel_id=1, replica_groups=mesh['slab'=8,'tile'=16] {'slab'}, dimensions={0} | all-to-all | bytes 4194304 | tf_op jit(solution)/shard_map/all_to_all | solution.py:174
  108.7 0.8 reduce_sum.9
  (139 shorter events, 15.7 us)
Async XLA Ops:
  0.0 20.9 %copy-start = (f32[8,4,64,128]{3,2,1,0:T(8,128)S(1)}, f32[8,4,64,128]{3,2,1,0:T(8,128)}, u32[]{:S(2)}) copy-start(f32[8,4,64,128]{3,2,1,0:T(8,128)} %param.5) | copy-start | bytes 3145732
  0.0 20.9 %copy-start.1 = (f32[2,8,64,128]{3,2,1,0:T(8,128)S(1)}, f32[2,8,64,128]{3,2,1,0:T(8,128)}, u32[]{:S(2)}) copy-start(f32[2,8,64,128]{3,2,1,0:T(8,128)} %param.4) | copy-start | bytes 1572868
  0.0 20.9 %copy-start.2 = (f32[64,128]{1,0:T(8,128)S(1)}, f32[64,128]{1,0:T(8,128)}, u32[]{:S(2)}) copy-start(f32[64,128]{1,0:T(8,128)} %param.6) | copy-start | bytes 98308
  2.9 16.2 %collective-permute-start = (f32[49,32,128]{2,1,0:T(8,128)}, f32[49,32,128]{2,1,0:T(8,128)S(1)}, u32[]{:S(2)}, u32[]{:S(2)}) collective-permute-start(f32[49,32,128]{2,1,0:T(8,128)} %get-tuple-element.130), channel_id=1, source_target_pairs={{0,1},{1,2},{2,3},{3,4},{4,5},{5,6},{6,7},{7,8},{8,9},{9,10},{10,1... | collective-permute-start | bytes 2408456 | tf_op jit(solution)/shard_map/ppermute | solution.py:95
  4.9 16.1 %collective-permute-start.1 = (f32[49,32,128]{2,1,0:T(8,128)}, f32[49,32,128]{2,1,0:T(8,128)S(1)}, u32[]{:S(2)}, u32[]{:S(2)}) collective-permute-start(f32[49,32,128]{2,1,0:T(8,128)} %get-tuple-element.131), channel_id=1, source_target_pairs={{1,0},{2,1},{3,2},{4,3},{5,4},{6,5},{7,6},{8,7},{9,8},{10,9},{11,1... | collective-permute-start | bytes 2408456 | tf_op jit(solution)/shard_map/ppermute | solution.py:96
  25.7 13.3 %collective-permute-start.2 = (f32[4,32,128]{2,1,0:T(8,128)S(1)}, f32[4,32,128]{2,1,0:T(8,128)S(1)}, u32[]{:S(2)}, u32[]{:S(2)}) collective-permute-start(f32[4,32,128]{2,1,0:T(8,128)S(1)} %get-tuple-element.203), channel_id=1, source_target_pairs={{0,17},{1,18},{2,19},{3,20},{4,21},{5,22},{6,23},{7,24},{8,25},{9,... | collective-permute-start | bytes 196616 | tf_op jit(solution)/shard_map/ppermute | solution.py:111
  35.2 7.2 %collective-permute-start.3 = (f32[4,64,128]{2,1,0:T(8,128)S(1)}, f32[4,64,128]{2,1,0:T(8,128)S(1)}, u32[]{:S(2)}, u32[]{:S(2)}) collective-permute-start(f32[4,64,128]{2,1,0:T(8,128)S(1)} %slice.2303), channel_id=1, source_target_pairs={{112,0},{0,16},{16,32},{32,48},{48,64},{64,80},{80,96},{96,112},{1... | collective-permute-start | bytes 393224 | tf_op jit(solution)/shard_map/ppermute | solution.py:18
  36.9 8.9 %collective-permute-start.4 = (f32[4,32,128]{2,1,0:T(8,128)S(1)}, f32[4,32,128]{2,1,0:T(8,128)S(1)}, u32[]{:S(2)}, u32[]{:S(2)}) collective-permute-start(f32[4,32,128]{2,1,0:T(8,128)S(1)} %get-tuple-element.202), channel_id=1, source_target_pairs={{1,16},{2,17},{3,18},{4,19},{5,20},{6,21},{7,22},{8,23},{9,24},{10... | collective-permute-start | bytes 196616 | tf_op jit(solution)/shard_map/ppermute | solution.py:113
  54.4 7.3 %copy-start.4 = (s32[8]{0:T(128)S(1)}, s32[8]{0:T(128)}, u32[]{:S(2)}) copy-start(s32[8]{0:T(128)} %param.7) | copy-start | bytes 100
  55.6 10.1 %collective-permute-start.5 = (f32[4,16,128]{2,1,0:T(8,128)S(1)}, f32[4,16,128]{2,1,0:T(8,128)S(1)}, u32[]{:S(2)}, u32[]{:S(2)}) collective-permute-start(f32[4,16,128]{2,1,0:T(8,128)S(1)} %get-tuple-element.201), channel_id=1, source_target_pairs={{0,113},{1,114},{2,115},{3,116},{4,117},{5,118},{6,119},{7,120},{8... | collective-permute-start | bytes 98312 | tf_op jit(solution)/shard_map/ppermute | solution.py:111
  61.7 5.0 %collective-permute-start.6 = (f32[4,64,128]{2,1,0:T(8,128)S(1)}, f32[4,64,128]{2,1,0:T(8,128)S(1)}, u32[]{:S(2)}, u32[]{:S(2)}) collective-permute-start(f32[4,64,128]{2,1,0:T(8,128)S(1)} %slice.2361), channel_id=1, source_target_pairs={{16,0},{32,16},{48,32},{64,48},{80,64},{96,80},{112,96},{0,112},{1... | collective-permute-start | bytes 393224 | tf_op jit(solution)/shard_map/ppermute | solution.py:18
  62.0 5.2 %collective-permute-start.7 = (f32[4,16,128]{2,1,0:T(8,128)S(1)}, f32[4,16,128]{2,1,0:T(8,128)S(1)}, u32[]{:S(2)}, u32[]{:S(2)}) collective-permute-start(f32[4,16,128]{2,1,0:T(8,128)S(1)} %get-tuple-element.200), channel_id=1, source_target_pairs={{1,112},{2,113},{3,114},{4,115},{5,116},{6,117},{7,118},{8,119},{9... | collective-permute-start | bytes 98312 | tf_op jit(solution)/shard_map/ppermute | solution.py:113
  70.0 1.2 %copy-start.3 = (f32[4,96,128]{2,1,0:T(8,128)}, f32[4,96,128]{2,1,0:T(8,128)S(1)}, u32[]{:S(2)}) copy-start(f32[4,96,128]{2,1,0:T(8,128)S(1)} %fusion.154) | copy-start | bytes 589828
  71.3 1.3 %slice-start = ((f32[4,96,128]{2,1,0:T(8,128)}), f32[4,64,128]{2,1,0:T(8,128)S(1)}, s32[]{:S(2)}) async-start(f32[4,96,128]{2,1,0:T(8,128)} %copy-done.3), calls=%async_computation.1 | async-start | bytes 262144 | tf_op jit(solution)/shard_map/slice | solution.py:84

commit v6 on v5

--- a/solution.py
+++ b/solution.py
@@ -166,11 +166,9 @@
         if sweep + 1 < SWEEPS:
             start = slab_start(cut(state, have, 0), -1, tail)
             have = tail
-    adjoint = jnp.stack(record, axis=0)
     phase = lax.axis_index("slab") * steps + jnp.arange(steps, dtype=jnp.int32)
-    flat = adjoint.reshape(steps, count_f * rows * columns)
     table = coefficient_table(harmonics, phase, periods)
-    terms = jnp.dot(table, flat, precision=lax.Precision.HIGHEST)
+    terms = sum(table[:, m, None, None, None] * record[m][None] for m in range(steps))
     parts = lax.all_to_all(terms.reshape(slabs, 2 * H // slabs, count_f, rows, columns), "slab", 0, 0, tiled=True)
     return jnp.sum(parts, axis=0, keepdims=True)
 

time: 111 us -> 111 us (level)
  matrix products: 1.77 us -> 0 us
  other arithmetic: 21.5 us -> 22.7 us
    dot_general x1 -> x0, matrix products: 1.77 us -> none  [on_device(): terms = jnp.dot(table, flat, precision=lax.Precision.HIGHEST)]
    another operation x2 -> x1, local copies, waits for them, and re-layouts: 1.63 us -> 0.01 us  [the longest x1 1.62 us: on_device(): adjoint = jnp.stack(record, axis=0)]
    unnamed x14 -> x104, local copies, waits for them, and re-layouts: 0.05 us -> 1.65 us
    add x0 -> x1, other arithmetic: none -> 1.32 us  [on_device(): sum((table[:, m, None, None, None] * record[m][None] for m in range(steps)))]
    add x15 -> x16, other arithmetic: 3.99 us -> 4.07 us  [on_device(): state = state + 0.5 * (first + second)]
where the time goes in v6:
time: 111 us; the launch traced here: 110 us
  blocking collectives  32.3 us (29%)
  starting transfers between devices  31.1 us (28%)
  other arithmetic  22.7 us (20%)
  waiting for transfers between devices  17.9 us (16%)
  local copies, waits for them, and re-layouts  4.4 us (4%)
  between operations  1.59 us (1%)
    all_to_all x1, blocking collectives, on_device(): lax.all_to_all(terms.reshape(slabs, 2 * H // slabs, count_f, rows, column...  32.3 us
    ppermute x2, starting transfers between devices, slab_start(): lax.ppermute(own[:, rows - depth:], both, [(j * tiles + t, onward(j, t +...  15.6 us
    ppermute x1, waiting for transfers between devices, on_device(): lax.ppermute(packed[:, rows - far:], 'tile', [(i, i + 1) for i in range(t...  7.83 us
    mul x28, other arithmetic, adjoint_rate(): flux_y = pad_grid(speed_y * state)  7.55 us
    ppermute x1, starting transfers between devices, on_device(): lax.ppermute(packed[:, :far], 'tile', [(i + 1, i) for i in range(tiles -...  6.04 us
    ppermute x2, starting transfers between devices, slab_start(): lax.ppermute(own[:, :depth], both, [(j * tiles + t + 1, onward(j, t)) for...  5.89 us
    ppermute x2, waiting for transfers between devices, slab_start(): lax.ppermute(own[:, :depth], both, [(j * tiles + t + 1, onward(j, t)) for...  4.72 us
    add x14, other arithmetic, on_device(): state + first  4.13 us
  transfers between devices with their start and end apart: 8, of which 6 were waited for; matrix products, arithmetic and copies ran while one was open for 1% of the time, Pallas kernels for 0%

profile of v6, /device:TPU:16, one launch (start us, length us, event | category | flops | bytes accessed | tf_op | source)
XLA Modules:
  0.0 109.9 jit_solution(10339848942693248875)
XLA Ops:
  0.0 1.5 %pad_maximum_fusion.1 = f32[49,64,128]{2,1,0:T(8,128)S(1)} fusion(f32[1,64,128]{2,1,0:T(8,128)} %bitcast.152, f32[32,64,128]{2,1,0:T(8,128)} %bitcast.119, f32[16,64,128]{2,1,0:T(8,128)} %bitcast.133), kind=kLoop, calls=%fused_computation.2 | loop fusion | flops 802816 | bytes 3211264 | tf_op jit(solution)/shard_map/concatenate | solution.py:75
  1.5 1.3 %fusion.573 = (f32[49,32,128]{2,1,0:T(8,128)}, f32[49,32,128]{2,1,0:T(8,128)}) fusion(f32[49,64,128]{2,1,0:T(8,128)S(1)} %pad_maximum_fusion.1), kind=kLoop, calls=%fused_computation.1151 | loop fusion | bytes 3211264 | tf_op jit(solution)/shard_map/slice | solution.py:95
  2.9 1.9 %collective-permute-start = (f32[49,32,128]{2,1,0:T(8,128)}, f32[49,32,128]{2,1,0:T(8,128)S(1)}, u32[]{:S(2)}, u32[]{:S(2)}) collective-permute-start(f32[49,32,128]{2,1,0:T(8,128)} %get-tuple-element.138), channel_id=1, source_target_pairs={{0,1},{1,2},{2,3},{3,4},{4,5},{5,6},{6,7},{7,8},{8,9},{9,10},{10,1... | collective-permute-start | bytes 2408456 | tf_op jit(solution)/shard_map/ppermute | solution.py:95
  4.8 6.0 %collective-permute-start.1 = (f32[49,32,128]{2,1,0:T(8,128)}, f32[49,32,128]{2,1,0:T(8,128)S(1)}, u32[]{:S(2)}, u32[]{:S(2)}) collective-permute-start(f32[49,32,128]{2,1,0:T(8,128)} %get-tuple-element.139), channel_id=1, source_target_pairs={{1,0},{2,1},{3,2},{4,3},{5,4},{6,5},{7,6},{8,7},{9,8},{10,9},{11,1... | collective-permute-start | bytes 2408456 | tf_op jit(solution)/shard_map/ppermute | solution.py:96
  11.2 7.8 %collective-permute-done = f32[49,32,128]{2,1,0:T(8,128)S(1)} collective-permute-done((f32[49,32,128]{2,1,0:T(8,128)}, f32[49,32,128]{2,1,0:T(8,128)S(1)}, u32[]{:S(2)}, u32[]{:S(2)}) %collective-permute-start) | collective-permute-done | bytes 802848 | tf_op jit(solution)/shard_map/ppermute | solution.py:95
  19.0 1.8 %collective-permute-done.1 = f32[49,32,128]{2,1,0:T(8,128)S(1)} collective-permute-done((f32[49,32,128]{2,1,0:T(8,128)}, f32[49,32,128]{2,1,0:T(8,128)S(1)}, u32[]{:S(2)}, u32[]{:S(2)}) %collective-permute-start.1) | collective-permute-done | bytes 802848 | tf_op jit(solution)/shard_map/ppermute | solution.py:96
  20.9 0.3 pad_maximum_fusion
  25.9 9.5 %collective-permute-start.2 = (f32[4,32,128]{2,1,0:T(8,128)S(1)}, f32[4,32,128]{2,1,0:T(8,128)S(1)}, u32[]{:S(2)}, u32[]{:S(2)}) collective-permute-start(f32[4,32,128]{2,1,0:T(8,128)S(1)} %get-tuple-element.211), channel_id=1, source_target_pairs={{0,17},{1,18},{2,19},{3,20},{4,21},{5,22},{6,23},{7,24},{8,25},{9,... | collective-permute-start | bytes 196616 | tf_op jit(solution)/shard_map/ppermute | solution.py:111
  35.4 1.6 %collective-permute-start.3 = (f32[4,64,128]{2,1,0:T(8,128)S(1)}, f32[4,64,128]{2,1,0:T(8,128)S(1)}, u32[]{:S(2)}, u32[]{:S(2)}) collective-permute-start(f32[4,64,128]{2,1,0:T(8,128)S(1)} %slice.2336), channel_id=1, source_target_pairs={{112,0},{0,16},{16,32},{32,48},{48,64},{64,80},{80,96},{96,112},{1... | collective-permute-start | bytes 393224 | tf_op jit(solution)/shard_map/ppermute | solution.py:18
  37.1 2.1 %collective-permute-start.4 = (f32[4,32,128]{2,1,0:T(8,128)S(1)}, f32[4,32,128]{2,1,0:T(8,128)S(1)}, u32[]{:S(2)}, u32[]{:S(2)}) collective-permute-start(f32[4,32,128]{2,1,0:T(8,128)S(1)} %get-tuple-element.210), channel_id=1, source_target_pairs={{1,16},{2,17},{3,18},{4,19},{5,20},{6,21},{7,22},{8,23},{9,24},{10... | collective-permute-start | bytes 196616 | tf_op jit(solution)/shard_map/ppermute | solution.py:113
  39.2 3.4 %collective-permute-done.3 = f32[4,64,128]{2,1,0:T(8,128)S(1)} collective-permute-done((f32[4,64,128]{2,1,0:T(8,128)S(1)}, f32[4,64,128]{2,1,0:T(8,128)S(1)}, u32[]{:S(2)}, u32[]{:S(2)}) %collective-permute-start.3) | collective-permute-done | bytes 131104 | tf_op jit(solution)/shard_map/ppermute | solution.py:18
  42.6 3.4 %collective-permute-done.4 = f32[4,32,128]{2,1,0:T(8,128)S(1)} collective-permute-done((f32[4,32,128]{2,1,0:T(8,128)S(1)}, f32[4,32,128]{2,1,0:T(8,128)S(1)}, u32[]{:S(2)}, u32[]{:S(2)}) %collective-permute-start.4) | collective-permute-done | bytes 65568 | tf_op jit(solution)/shard_map/ppermute | solution.py:113
  46.0 0.4 fusion.2
  46.4 0.3 multiply_add_fusion.5
  46.8 0.4 fusion.1
  47.1 0.3 multiply_add_fusion.3
  47.5 0.4 fusion
  47.9 0.3 multiply_add_fusion.1
  48.3 0.3 fusion.5
  48.6 0.3 multiply_add_fusion.11
  48.9 0.3 fusion.4
  49.6 0.3 fusion.3
  50.5 0.3 add_subtract_fusion.3
  51.4 0.3 broadcast_multiply_fusion.18
  51.7 0.3 broadcast_multiply_fusion.11
  52.4 0.3 broadcast_multiply_fusion.3
  56.1 6.0 %collective-permute-start.5 = (f32[4,16,128]{2,1,0:T(8,128)S(1)}, f32[4,16,128]{2,1,0:T(8,128)S(1)}, u32[]{:S(2)}, u32[]{:S(2)}) collective-permute-start(f32[4,16,128]{2,1,0:T(8,128)S(1)} %get-tuple-element.209), channel_id=1, source_target_pairs={{0,113},{1,114},{2,115},{3,116},{4,117},{5,118},{6,119},{7,120},{8... | collective-permute-start | bytes 98312 | tf_op jit(solution)/shard_map/ppermute | solution.py:111
  63.3 3.8 %collective-permute-start.7 = (f32[4,16,128]{2,1,0:T(8,128)S(1)}, f32[4,16,128]{2,1,0:T(8,128)S(1)}, u32[]{:S(2)}, u32[]{:S(2)}) collective-permute-start(f32[4,16,128]{2,1,0:T(8,128)S(1)} %get-tuple-element.208), channel_id=1, source_target_pairs={{1,112},{2,113},{3,114},{4,115},{5,116},{6,117},{7,118},{8,119},{9... | collective-permute-start | bytes 98312 | tf_op jit(solution)/shard_map/ppermute | solution.py:113
  67.2 1.3 %collective-permute-done.7 = f32[4,16,128]{2,1,0:T(8,128)S(1)} collective-permute-done((f32[4,16,128]{2,1,0:T(8,128)S(1)}, f32[4,16,128]{2,1,0:T(8,128)S(1)}, u32[]{:S(2)}, u32[]{:S(2)}) %collective-permute-start.7) | collective-permute-done | bytes 32800 | tf_op jit(solution)/shard_map/ppermute | solution.py:113
  75.4 1.3 %multiply_add_fusion = f32[8,2,4,64,128]{4,3,2,1,0:T(8,128)S(1)} fusion(f32[4,64,128]{2,1,0:T(8,128)S(1)} %slice.2417, f32[8,2]{1,0:T(8,128)S(1)} %mul.3330, f32[4,64,128]{2,1,0:T(8,128)S(1)} %slice.2415, f32[8,2]{1,0:T(8,128)S(1)} %mul.3326, f32[4,64,128]{2,1,0:T(8,128)S(1)} %slice.2413, f32[8,2]{1,0:T(8,128)S(1)} %mul.3322, f32[4,64,128]{2,1,0:T(8,128)S(1)} %slice-done, ...), kind=kLoop, calls=%fused_computation.1 | loop fusion | flops 7864320 | bytes 3146240 | tf_op jit(solution)/shard_map/add | solution.py:171
  76.8 32.3 %all_to_all.5 = f32[8,2,4,64,128]{4,3,2,1,0:T(8,128)S(1)} all-to-all(f32[8,2,4,64,128]{4,3,2,1,0:T(8,128)S(1)} %multiply_add_fusion), channel_id=1, replica_groups=mesh['slab'=8,'tile'=16] {'slab'}, dimensions={0} | all-to-all | bytes 4194304 | tf_op jit(solution)/shard_map/all_to_all | solution.py:172
  109.1 0.8 reduce_sum.9
  (238 shorter events, 17.4 us)
Async XLA Ops:
  1.5 9.6 %copy-start.49 = (s32[8]{0:T(128)S(1)}, s32[8]{0:T(128)}, u32[]{:S(2)}) copy-start(s32[8]{0:T(128)} %param.7) | copy-start | bytes 100
  1.5 19.3 %copy-start = (f32[8,4,64,128]{3,2,1,0:T(8,128)S(1)}, f32[8,4,64,128]{3,2,1,0:T(8,128)}, u32[]{:S(2)}) copy-start(f32[8,4,64,128]{3,2,1,0:T(8,128)} %param.5) | copy-start | bytes 3145732
  1.5 19.3 %copy-start.1 = (f32[2,8,64,128]{3,2,1,0:T(8,128)S(1)}, f32[2,8,64,128]{3,2,1,0:T(8,128)}, u32[]{:S(2)}) copy-start(f32[2,8,64,128]{3,2,1,0:T(8,128)} %param.4) | copy-start | bytes 1572868
  1.5 19.3 %copy-start.12 = (f32[64,128]{1,0:T(8,128)S(1)}, f32[64,128]{1,0:T(8,128)}, u32[]{:S(2)}) copy-start(f32[64,128]{1,0:T(8,128)} %param.6) | copy-start | bytes 98308
  2.9 16.2 %collective-permute-start = (f32[49,32,128]{2,1,0:T(8,128)}, f32[49,32,128]{2,1,0:T(8,128)S(1)}, u32[]{:S(2)}, u32[]{:S(2)}) collective-permute-start(f32[49,32,128]{2,1,0:T(8,128)} %get-tuple-element.138), channel_id=1, source_target_pairs={{0,1},{1,2},{2,3},{3,4},{4,5},{5,6},{6,7},{7,8},{8,9},{9,10},{10,1... | collective-permute-start | bytes 2408456 | tf_op jit(solution)/shard_map/ppermute | solution.py:95
  4.8 16.1 %collective-permute-start.1 = (f32[49,32,128]{2,1,0:T(8,128)}, f32[49,32,128]{2,1,0:T(8,128)S(1)}, u32[]{:S(2)}, u32[]{:S(2)}) collective-permute-start(f32[49,32,128]{2,1,0:T(8,128)} %get-tuple-element.139), channel_id=1, source_target_pairs={{1,0},{2,1},{3,2},{4,3},{5,4},{6,5},{7,6},{8,7},{9,8},{10,9},{11,1... | collective-permute-start | bytes 2408456 | tf_op jit(solution)/shard_map/ppermute | solution.py:96
  21.4 32.2 %copy-start.31 = (f32[80,128]{1,0:T(8,128)}, f32[80,128]{1,0:T(8,128)S(1)}, u32[]{:S(2)}) copy-start(f32[80,128]{1,0:T(8,128)S(1)} %get-tuple-element.146) | copy-start | bytes 122884
  21.5 32.4 %copy-start.35 = (f32[80,128]{1,0:T(8,128)}, f32[80,128]{1,0:T(8,128)S(1)}, u32[]{:S(2)}) copy-start(f32[80,128]{1,0:T(8,128)S(1)} %get-tuple-element.147) | copy-start | bytes 122884
  21.5 32.8 %copy-start.29 = (f32[80,128]{1,0:T(8,128)}, f32[80,128]{1,0:T(8,128)S(1)}, u32[]{:S(2)}) copy-start(f32[80,128]{1,0:T(8,128)S(1)} %get-tuple-element.144) | copy-start | bytes 122884
  21.5 33.0 %copy-start.39 = (f32[80,128]{1,0:T(8,128)}, f32[80,128]{1,0:T(8,128)S(1)}, u32[]{:S(2)}) copy-start(f32[80,128]{1,0:T(8,128)S(1)} %get-tuple-element.145) | copy-start | bytes 122884
  21.5 33.4 %copy-start.27 = (f32[80,128]{1,0:T(8,128)}, f32[80,128]{1,0:T(8,128)S(1)}, u32[]{:S(2)}) copy-start(f32[80,128]{1,0:T(8,128)S(1)} %get-tuple-element.142) | copy-start | bytes 122884
  21.5 33.6 %copy-start.37 = (f32[80,128]{1,0:T(8,128)}, f32[80,128]{1,0:T(8,128)S(1)}, u32[]{:S(2)}) copy-start(f32[80,128]{1,0:T(8,128)S(1)} %get-tuple-element.143) | copy-start | bytes 122884
  21.5 34.0 %copy-start.25 = (f32[80,128]{1,0:T(8,128)}, f32[80,128]{1,0:T(8,128)S(1)}, u32[]{:S(2)}) copy-start(f32[80,128]{1,0:T(8,128)S(1)} %get-tuple-element.141) | copy-start | bytes 122884
  21.5 34.3 %copy-start.33 = (f32[80,128]{1,0:T(8,128)}, f32[80,128]{1,0:T(8,128)S(1)}, u32[]{:S(2)}) copy-start(f32[80,128]{1,0:T(8,128)S(1)} %get-tuple-element.140) | copy-start | bytes 122884
  21.6 29.2 %copy-start.47 = (f32[96,128]{1,0:T(8,128)}, f32[96,128]{1,0:T(8,128)S(1)}, u32[]{:S(2)}) copy-start(f32[96,128]{1,0:T(8,128)S(1)} %get-tuple-element.162) | copy-start | bytes 147460
  21.6 29.4 %copy-start.45 = (f32[96,128]{1,0:T(8,128)}, f32[96,128]{1,0:T(8,128)S(1)}, u32[]{:S(2)}) copy-start(f32[96,128]{1,0:T(8,128)S(1)} %get-tuple-element.163) | copy-start | bytes 147460
  21.6 29.7 %copy-start.41 = (f32[96,128]{1,0:T(8,128)}, f32[96,128]{1,0:T(8,128)S(1)}, u32[]{:S(2)}) copy-start(f32[96,128]{1,0:T(8,128)S(1)} %get-tuple-element.160) | copy-start | bytes 147460
  21.6 30.1 %copy-start.43 = (f32[96,128]{1,0:T(8,128)}, f32[96,128]{1,0:T(8,128)S(1)}, u32[]{:S(2)}) copy-start(f32[96,128]{1,0:T(8,128)S(1)} %get-tuple-element.161) | copy-start | bytes 147460
  21.6 30.5 %copy-start.19 = (f32[96,128]{1,0:T(8,128)}, f32[96,128]{1,0:T(8,128)S(1)}, u32[]{:S(2)}) copy-start(f32[96,128]{1,0:T(8,128)S(1)} %get-tuple-element.158) | copy-start | bytes 147460
  21.6 30.8 %copy-start.23 = (f32[96,128]{1,0:T(8,128)}, f32[96,128]{1,0:T(8,128)S(1)}, u32[]{:S(2)}) copy-start(f32[96,128]{1,0:T(8,128)S(1)} %get-tuple-element.159) | copy-start | bytes 147460
  21.7 31.1 %copy-start.17 = (f32[96,128]{1,0:T(8,128)}, f32[96,128]{1,0:T(8,128)S(1)}, u32[]{:S(2)}) copy-start(f32[96,128]{1,0:T(8,128)S(1)} %get-tuple-element.157) | copy-start | bytes 147460
  21.7 31.4 %copy-start.21 = (f32[96,128]{1,0:T(8,128)}, f32[96,128]{1,0:T(8,128)S(1)}, u32[]{:S(2)}) copy-start(f32[96,128]{1,0:T(8,128)S(1)} %get-tuple-element.156) | copy-start | bytes 147460
  25.9 13.3 %collective-permute-start.2 = (f32[4,32,128]{2,1,0:T(8,128)S(1)}, f32[4,32,128]{2,1,0:T(8,128)S(1)}, u32[]{:S(2)}, u32[]{:S(2)}) collective-permute-start(f32[4,32,128]{2,1,0:T(8,128)S(1)} %get-tuple-element.211), channel_id=1, source_target_pairs={{0,17},{1,18},{2,19},{3,20},{4,21},{5,22},{6,23},{7,24},{8,25},{9,... | collective-permute-start | bytes 196616 | tf_op jit(solution)/shard_map/ppermute | solution.py:111
  35.4 7.2 %collective-permute-start.3 = (f32[4,64,128]{2,1,0:T(8,128)S(1)}, f32[4,64,128]{2,1,0:T(8,128)S(1)}, u32[]{:S(2)}, u32[]{:S(2)}) collective-permute-start(f32[4,64,128]{2,1,0:T(8,128)S(1)} %slice.2336), channel_id=1, source_target_pairs={{112,0},{0,16},{16,32},{32,48},{48,64},{64,80},{80,96},{96,112},{1... | collective-permute-start | bytes 393224 | tf_op jit(solution)/shard_map/ppermute | solution.py:18
  37.1 8.9 %collective-permute-start.4 = (f32[4,32,128]{2,1,0:T(8,128)S(1)}, f32[4,32,128]{2,1,0:T(8,128)S(1)}, u32[]{:S(2)}, u32[]{:S(2)}) collective-permute-start(f32[4,32,128]{2,1,0:T(8,128)S(1)} %get-tuple-element.210), channel_id=1, source_target_pairs={{1,16},{2,17},{3,18},{4,19},{5,20},{6,21},{7,22},{8,23},{9,24},{10... | collective-permute-start | bytes 196616 | tf_op jit(solution)/shard_map/ppermute | solution.py:113
  46.0 9.8 %copy-start.14 = (f32[4,128,128]{2,1,0:T(8,128)}, f32[4,128,128]{2,1,0:T(8,128)S(1)}, u32[]{:S(2)}) copy-start(f32[4,128,128]{2,1,0:T(8,128)S(1)} %constant_dynamic-update-slice_fusion) | copy-start | bytes 786436
  55.4 13.1 %copy-start.46 = (f32[96,128]{1,0:T(8,128)S(1)}, f32[96,128]{1,0:T(8,128)}, u32[]{:S(2)}) copy-start(f32[96,128]{1,0:T(8,128)} %copy-done.45) | copy-start | bytes 147460
  55.5 13.1 %copy-start.48 = (f32[96,128]{1,0:T(8,128)S(1)}, f32[96,128]{1,0:T(8,128)}, u32[]{:S(2)}) copy-start(f32[96,128]{1,0:T(8,128)} %copy-done.47) | copy-start | bytes 147460
  55.8 13.1 %copy-start.42 = (f32[96,128]{1,0:T(8,128)S(1)}, f32[96,128]{1,0:T(8,128)}, u32[]{:S(2)}) copy-start(f32[96,128]{1,0:T(8,128)} %copy-done.41) | copy-start | bytes 147460
  56.1 10.9 %collective-permute-start.5 = (f32[4,16,128]{2,1,0:T(8,128)S(1)}, f32[4,16,128]{2,1,0:T(8,128)S(1)}, u32[]{:S(2)}, u32[]{:S(2)}) collective-permute-start(f32[4,16,128]{2,1,0:T(8,128)S(1)} %get-tuple-element.209), channel_id=1, source_target_pairs={{0,113},{1,114},{2,115},{3,116},{4,117},{5,118},{6,119},{7,120},{8... | collective-permute-start | bytes 98312 | tf_op jit(solution)/shard_map/ppermute | solution.py:111
  62.2 5.0 %collective-permute-start.6 = (f32[4,64,128]{2,1,0:T(8,128)S(1)}, f32[4,64,128]{2,1,0:T(8,128)S(1)}, u32[]{:S(2)}, u32[]{:S(2)}) collective-permute-start(f32[4,64,128]{2,1,0:T(8,128)S(1)} %slice.2394), channel_id=1, source_target_pairs={{16,0},{32,16},{48,32},{64,48},{80,64},{96,80},{112,96},{0,112},{1... | collective-permute-start | bytes 393224 | tf_op jit(solution)/shard_map/ppermute | solution.py:18
  63.3 5.3 %collective-permute-start.7 = (f32[4,16,128]{2,1,0:T(8,128)S(1)}, f32[4,16,128]{2,1,0:T(8,128)S(1)}, u32[]{:S(2)}, u32[]{:S(2)}) collective-permute-start(f32[4,16,128]{2,1,0:T(8,128)S(1)} %get-tuple-element.208), channel_id=1, source_target_pairs={{1,112},{2,113},{3,114},{4,115},{5,116},{6,117},{7,118},{8,119},{9... | collective-permute-start | bytes 98312 | tf_op jit(solution)/shard_map/ppermute | solution.py:113
  (27 other events, 44.2 us)

commit v7 on v5

--- a/solution.py
+++ b/solution.py
@@ -84,12 +84,9 @@
         return lax.slice_in_dim(field, have - want, have + rows + want, axis=field.ndim - 2)
 
     tail = 2 * steps
-    fwd_need = [0] * steps
-    fwd_need[-1] = 2 * steps - 1
-    for m in range(steps - 2, -1, -1):
-        fwd_need[m] = max(2 * m + 1, fwd_need[m + 1] + 2)
-    fwd_need = [max(need, 2 * m + 2) for m, need in enumerate(fwd_need)]
-    far = band(fwd_need[0])
+    fwd_need = [2 * (steps - 1 - m) for m in range(steps)]
+    reach = [band(2 * m + 1) for m in range(steps)]
+    far = max(band(fwd_need[0] + 2), band(2 * steps))
     assert far <= rows
 
     before = lax.ppermute(packed[:, rows - far :], "tile", [(i, i + 1) for i in range(tiles - 1)])
@@ -140,7 +137,18 @@
         if sweep + 1 < SWEEPS:
             start = slab_start(cut(state, have, 0), 1, far)
             have = far
-    response = record
+    centre = [cut(state_m, held_m, 0) for state_m, held_m in record]
+    down = jnp.concatenate([q[:, rows - d :].reshape(-1, columns) for q, d in zip(centre, reach)], axis=0)
+    up = jnp.concatenate([q[:, :d].reshape(-1, columns) for q, d in zip(centre, reach)], axis=0)
+    from_before = lax.ppermute(down, "tile", [(i, i + 1) for i in range(tiles - 1)])
+    from_after = lax.ppermute(up, "tile", [(i + 1, i) for i in range(tiles - 1)])
+    response, at = [], 0
+    for q, d in zip(centre, reach):
+        size = count_f * d
+        head = from_before[at : at + size].reshape(count_f, d, columns)
+        foot = from_after[at : at + size].reshape(count_f, d, columns)
+        response.append((jnp.concatenate([head, q, foot], axis=1), d))
+        at += size
     adj_bands = [
         [band(2 * m + 2) for m in range(steps)],
         [band(2 * m + 2) for m in range(steps)],

time: 111 us -> 114 us (1.027)
  starting transfers between devices: 31 us -> 35.3 us
  waiting for transfers between devices: 18 us -> 20.1 us
  other arithmetic: 21.5 us -> 20.1 us
  local copies, waits for them, and re-layouts: 3.91 us -> 2.6 us
    ppermute x2, starting transfers between devices: 15.6 us -> 3.84 us  [slab_start(): lax.ppermute(own[:, rows - depth:], both, [(j * tiles + t, onward(j, t +...]
    ppermute x2, starting transfers between devices: 5.84 us -> 14.7 us  [slab_start(): lax.ppermute(own[:, :depth], both, [(j * tiles + t + 1, onward(j, t)) for...]
    ppermute x0 -> x2, waiting for transfers between devices: none -> 7.27 us  [the longest x1 6.25 us: on_device(): lax.ppermute(down, 'tile', [(i, i + 1) for i in range(tiles - 1)])]
    ppermute x0 -> x2, starting transfers between devices: none -> 7.23 us  [the longest x1 5.13 us: on_device(): lax.ppermute(up, 'tile', [(i + 1, i) for i in range(tiles - 1)])]
    ppermute x2, waiting for transfers between devices: 0.01 us -> 6.22 us  [slab_start(): lax.ppermute(own[:, rows - depth:], both, [(j * tiles + t, onward(j, t +...]
    ppermute x1, waiting for transfers between devices: 7.98 us -> 3.51 us  [on_device(): lax.ppermute(packed[:, rows - far:], 'tile', [(i, i + 1) for i in range(t...]
    ppermute x2, waiting for transfers between devices: 4.33 us -> 0.01 us  [passed_along(): return lax.ppermute(block, axis, route)]
    ppermute x2, waiting for transfers between devices: 3.9 us -> 1.31 us  [slab_start(): lax.ppermute(own[:, :depth], both, [(j * tiles + t + 1, onward(j, t)) for...]
  transfers between devices with their start and end apart: 8 -> 10, of which waited for: 6 -> 6; matrix products, arithmetic and copies ran while one was open for 1% -> 0% of each run, Pallas kernels for 0% -> 0%
where the time goes in v7:
time: 114 us; the launch traced here: 113 us
  starting transfers between devices  35.3 us (31%)
  blocking collectives  32.1 us (28%)
  other arithmetic  20.1 us (18%)
  waiting for transfers between devices  20.1 us (18%)
  local copies, waits for them, and re-layouts  2.6 us (2%)
  matrix products  1.77 us (2%)
  between operations  1.2 us (1%)
    all_to_all x1, blocking collectives, on_device(): lax.all_to_all(terms.reshape(slabs, 2 * H // slabs, count_f, rows, column...  32.1 us
    ppermute x2, starting transfers between devices, slab_start(): lax.ppermute(own[:, :depth], both, [(j * tiles + t + 1, onward(j, t)) for...  14.7 us
    mul x28, other arithmetic, adjoint_rate(): flux_y = pad_grid(speed_y * state)  7.56 us
    ppermute x1, waiting for transfers between devices, on_device(): lax.ppermute(down, 'tile', [(i, i + 1) for i in range(tiles - 1)])  6.25 us
    ppermute x2, waiting for transfers between devices, slab_start(): lax.ppermute(own[:, rows - depth:], both, [(j * tiles + t, onward(j, t +...  6.22 us
    ppermute x1, starting transfers between devices, on_device(): lax.ppermute(packed[:, :far], 'tile', [(i + 1, i) for i in range(tiles -...  6.05 us
    ppermute x1, starting transfers between devices, on_device(): lax.ppermute(up, 'tile', [(i + 1, i) for i in range(tiles - 1)])  5.13 us
    ppermute x2, starting transfers between devices, slab_start(): lax.ppermute(own[:, rows - depth:], both, [(j * tiles + t, onward(j, t +...  3.84 us
  transfers between devices with their start and end apart: 10, of which 6 were waited for; matrix products, arithmetic and copies ran while one was open for 0% of the time, Pallas kernels for 0%

profile of v7, /device:TPU:16, one launch (start us, length us, event | category | flops | bytes accessed | tf_op | source)
XLA Modules:
  0.0 113.2 jit_solution(11541384913180485759)
XLA Ops:
  0.0 1.3 %pad_maximum_fusion.3 = (f32[49,16,128]{2,1,0:T(8,128)S(1)}, f32[49,16,128]{2,1,0:T(8,128)S(1)}) fusion(f32[1,64,128]{2,1,0:T(8,128)} %bitcast.203, f32[32,64,128]{2,1,0:T(8,128)} %bitcast.173, f32[16,64,128]{2,1,0:T(8,128)} %bitcast.186), kind=kLoop, calls=%fused_computation.367 | loop fusion | flops 401408 | bytes 2408448 | tf_op jit(solution)/shard_map/slice | solution.py:92
  1.3 1.9 %collective-permute-start = (f32[49,16,128]{2,1,0:T(8,128)S(1)}, f32[49,16,128]{2,1,0:T(8,128)S(1)}, u32[]{:S(2)}, u32[]{:S(2)}) collective-permute-start(f32[49,16,128]{2,1,0:T(8,128)S(1)} %get-tuple-element.132), channel_id=1, source_target_pairs={{0,1},{1,2},{2,3},{3,4},{4,5},{5,6},{6,7},{7,8},{8,9},{9,10},{10,1... | collective-permute-start | bytes 1204232 | tf_op jit(solution)/shard_map/ppermute | solution.py:92
  3.3 6.0 %collective-permute-start.1 = (f32[49,16,128]{2,1,0:T(8,128)S(1)}, f32[49,16,128]{2,1,0:T(8,128)S(1)}, u32[]{:S(2)}, u32[]{:S(2)}) collective-permute-start(f32[49,16,128]{2,1,0:T(8,128)S(1)} %get-tuple-element.133), channel_id=1, source_target_pairs={{1,0},{2,1},{3,2},{4,3},{5,4},{6,5},{7,6},{8,7},{9,8},{10,9},{11,1... | collective-permute-start | bytes 1204232 | tf_op jit(solution)/shard_map/ppermute | solution.py:93
  9.4 3.5 %collective-permute-done = f32[49,16,128]{2,1,0:T(8,128)S(1)} collective-permute-done((f32[49,16,128]{2,1,0:T(8,128)S(1)}, f32[49,16,128]{2,1,0:T(8,128)S(1)}, u32[]{:S(2)}, u32[]{:S(2)}) %collective-permute-start) | collective-permute-done | bytes 401440 | tf_op jit(solution)/shard_map/ppermute | solution.py:92
  12.9 1.8 %collective-permute-done.1 = f32[49,16,128]{2,1,0:T(8,128)S(1)} collective-permute-done((f32[49,16,128]{2,1,0:T(8,128)S(1)}, f32[49,16,128]{2,1,0:T(8,128)S(1)}, u32[]{:S(2)}, u32[]{:S(2)}) %collective-permute-start.1) | collective-permute-done | bytes 401440 | tf_op jit(solution)/shard_map/ppermute | solution.py:93
  16.2 0.3 fusion.229
  19.4 7.2 %collective-permute-start.4 = (f32[4,16,128]{2,1,0:T(8,128)S(1)}, f32[4,16,128]{2,1,0:T(8,128)S(1)}, u32[]{:S(2)}, u32[]{:S(2)}) collective-permute-start(f32[4,16,128]{2,1,0:T(8,128)S(1)} %get-tuple-element.220), channel_id=1, source_target_pairs={{1,16},{2,17},{3,18},{4,19},{5,20},{6,21},{7,22},{8,23},{9,24},{10... | collective-permute-start | bytes 98312 | tf_op jit(solution)/shard_map/ppermute | solution.py:110
  26.6 1.9 %collective-permute-start.3 = (f32[4,16,128]{2,1,0:T(8,128)S(1)}, f32[4,16,128]{2,1,0:T(8,128)S(1)}, u32[]{:S(2)}, u32[]{:S(2)}) collective-permute-start(f32[4,16,128]{2,1,0:T(8,128)S(1)} %get-tuple-element.221), channel_id=1, source_target_pairs={{0,17},{1,18},{2,19},{3,20},{4,21},{5,22},{6,23},{7,24},{8,25},{9,... | collective-permute-start | bytes 98312 | tf_op jit(solution)/shard_map/ppermute | solution.py:108
  28.5 1.6 %collective-permute-start.2 = (f32[4,64,128]{2,1,0:T(8,128)S(1)}, f32[4,64,128]{2,1,0:T(8,128)S(1)}, u32[]{:S(2)}, u32[]{:S(2)}) collective-permute-start(f32[4,64,128]{2,1,0:T(8,128)S(1)} %slice.2242), channel_id=1, source_target_pairs={{112,0},{0,16},{16,32},{32,48},{48,64},{64,80},{80,96},{96,112},{1... | collective-permute-start | bytes 393224 | tf_op jit(solution)/shard_map/ppermute | solution.py:18
  30.2 6.2 %collective-permute-done.3 = f32[4,16,128]{2,1,0:T(8,128)S(1)} collective-permute-done((f32[4,16,128]{2,1,0:T(8,128)S(1)}, f32[4,16,128]{2,1,0:T(8,128)S(1)}, u32[]{:S(2)}, u32[]{:S(2)}) %collective-permute-start.3) | collective-permute-done | bytes 32800 | tf_op jit(solution)/shard_map/ppermute | solution.py:108
  36.4 0.3 fusion.228
  37.0 0.3 fusion.227
  37.6 0.3 fusion.226
  40.5 5.1 %collective-permute-start.6 = (f32[384,128]{1,0:T(8,128)S(1)}, f32[384,128]{1,0:T(8,128)S(1)}, u32[]{:S(2)}, u32[]{:S(2)}) collective-permute-start(f32[384,128]{1,0:T(8,128)S(1)} %constant_dynamic-update-slice_fusion.11), channel_id=1, source_target_pairs={{1,0},{2,1},{3,2},{4,3},{5,4},{6,5},{7,6},{8,7},{9,8},{10,9},{11,1... | collective-permute-start | bytes 589832 | tf_op jit(solution)/shard_map/ppermute | solution.py:144
  45.6 2.1 %collective-permute-start.5 = (f32[384,128]{1,0:T(8,128)S(1)}, f32[384,128]{1,0:T(8,128)S(1)}, u32[]{:S(2)}, u32[]{:S(2)}) collective-permute-start(f32[384,128]{1,0:T(8,128)S(1)} %constant_dynamic-update-slice_fusion.3), channel_id=1, source_target_pairs={{0,1},{1,2},{2,3},{3,4},{4,5},{5,6},{6,7},{7,8},{8,9},{9,10},{10,1... | collective-permute-start | bytes 589832 | tf_op jit(solution)/shard_map/ppermute | solution.py:143
  47.7 1.0 collective-permute-done.6
  48.8 6.3 %collective-permute-done.5 = f32[384,128]{1,0:T(8,128)S(1)} collective-permute-done((f32[384,128]{1,0:T(8,128)S(1)}, f32[384,128]{1,0:T(8,128)S(1)}, u32[]{:S(2)}, u32[]{:S(2)}) %collective-permute-start.5) | collective-permute-done | bytes 196640 | tf_op jit(solution)/shard_map/ppermute | solution.py:143
  55.5 0.3 broadcast_multiply_fusion.18
  55.8 0.3 broadcast_multiply_fusion.11
  56.5 0.3 broadcast_multiply_fusion.3
  60.1 1.9 %collective-permute-start.7 = (f32[4,16,128]{2,1,0:T(8,128)S(1)}, f32[4,16,128]{2,1,0:T(8,128)S(1)}, u32[]{:S(2)}, u32[]{:S(2)}) collective-permute-start(f32[4,16,128]{2,1,0:T(8,128)S(1)} %get-tuple-element.211), channel_id=1, source_target_pairs={{0,113},{1,114},{2,115},{3,116},{4,117},{5,118},{6,119},{7,120},{8... | collective-permute-start | bytes 98312 | tf_op jit(solution)/shard_map/ppermute | solution.py:108
  62.3 7.5 %collective-permute-start.9 = (f32[4,16,128]{2,1,0:T(8,128)S(1)}, f32[4,16,128]{2,1,0:T(8,128)S(1)}, u32[]{:S(2)}, u32[]{:S(2)}) collective-permute-start(f32[4,16,128]{2,1,0:T(8,128)S(1)} %get-tuple-element.210), channel_id=1, source_target_pairs={{1,112},{2,113},{3,114},{4,115},{5,116},{6,117},{7,118},{8,119},{9... | collective-permute-start | bytes 98312 | tf_op jit(solution)/shard_map/ppermute | solution.py:110
  69.8 1.3 %collective-permute-done.9 = f32[4,16,128]{2,1,0:T(8,128)S(1)} collective-permute-done((f32[4,16,128]{2,1,0:T(8,128)S(1)}, f32[4,16,128]{2,1,0:T(8,128)S(1)}, u32[]{:S(2)}, u32[]{:S(2)}) %collective-permute-start.9) | collective-permute-done | bytes 32800 | tf_op jit(solution)/shard_map/ppermute | solution.py:110
  71.5 0.3 broadcast_multiply_fusion.17
  72.2 0.3 broadcast_multiply_fusion.9
  72.9 0.3 broadcast_multiply_fusion.1
  73.6 0.3 fusion.148
  76.5 1.6 %stack.41 = f32[8,32768]{1,0:T(8,128)S(1)} concatenate(f32[1,32768]{1,0:T(1,128)S(1)} %bitcast.251, f32[1,32768]{1,0:T(1,128)S(1)} %bitcast.250, f32[1,32768]{1,0:T(1,128)S(1)} %bitcast.256, f32[1,32768]{1,0:T(1,128)S(1)} %bitcast.255, f32[1,32768]{1,0:T(1,128)S(1)} %bitcast.217, f32[1,32768]{1,0:T(1,128)S(1)} %bitcast.254, f32[1,32768]{1,0:T(1,128)S(1)} %bitcast.253, ...), dimensions={0} | concatenate | bytes 2097152 | tf_op jit(solution)/shard_map/stack | solution.py:177
  78.1 1.8 %fusion.520 = f32[8,2,4,64,128]{4,0,3,2,1:T(8,128)S(1)} fusion(f32[4,64,128,8,1]{2,3,1,0,4:T(8,128)S(1)} %bitcast.216, f32[8,1,8]{2,0,1:T(8,128)S(1)} %get-tuple-element.226, f32[8,1,8]{2,0,1:T(8,128)S(1)} %get-tuple-element.225), kind=kOutput, calls=%fused_computation.1137 | convolution fusion | flops 50331904 | bytes 3146240 | tf_op jit(solution)/shard_map/dot_general | solution.py:181
  79.9 0.4 copy.5
  80.3 32.1 %all_to_all.5 = f32[8,2,4,64,128]{4,3,2,1,0:T(8,128)S(1)} all-to-all(f32[8,2,4,64,128]{4,3,2,1,0:T(8,128)S(1)} %copy.5), channel_id=1, replica_groups=mesh['slab'=8,'tile'=16] {'slab'}, dimensions={0} | all-to-all | bytes 4194304 | tf_op jit(solution)/shard_map/all_to_all | solution.py:182
  112.4 0.8 reduce_sum.9
  (162 shorter events, 15.3 us)
Async XLA Ops:
  0.0 14.7 %copy-start.2 = (f32[64,128]{1,0:T(8,128)S(1)}, f32[64,128]{1,0:T(8,128)}, u32[]{:S(2)}) copy-start(f32[64,128]{1,0:T(8,128)} %param.6) | copy-start | bytes 98308
  0.0 14.7 %copy-start = (f32[8,4,64,128]{3,2,1,0:T(8,128)S(1)}, f32[8,4,64,128]{3,2,1,0:T(8,128)}, u32[]{:S(2)}) copy-start(f32[8,4,64,128]{3,2,1,0:T(8,128)} %param.5) | copy-start | bytes 3145732
  0.0 14.7 %copy-start.1 = (f32[2,8,64,128]{3,2,1,0:T(8,128)S(1)}, f32[2,8,64,128]{3,2,1,0:T(8,128)}, u32[]{:S(2)}) copy-start(f32[2,8,64,128]{3,2,1,0:T(8,128)} %param.4) | copy-start | bytes 1572868
  1.3 11.6 %collective-permute-start = (f32[49,16,128]{2,1,0:T(8,128)S(1)}, f32[49,16,128]{2,1,0:T(8,128)S(1)}, u32[]{:S(2)}, u32[]{:S(2)}) collective-permute-start(f32[49,16,128]{2,1,0:T(8,128)S(1)} %get-tuple-element.132), channel_id=1, source_target_pairs={{0,1},{1,2},{2,3},{3,4},{4,5},{5,6},{6,7},{7,8},{8,9},{9,10},{10,1... | collective-permute-start | bytes 1204232 | tf_op jit(solution)/shard_map/ppermute | solution.py:92
  3.3 11.5 %collective-permute-start.1 = (f32[49,16,128]{2,1,0:T(8,128)S(1)}, f32[49,16,128]{2,1,0:T(8,128)S(1)}, u32[]{:S(2)}, u32[]{:S(2)}) collective-permute-start(f32[49,16,128]{2,1,0:T(8,128)S(1)} %get-tuple-element.133), channel_id=1, source_target_pairs={{1,0},{2,1},{3,2},{4,3},{5,4},{6,5},{7,6},{8,7},{9,8},{10,9},{11,1... | collective-permute-start | bytes 1204232 | tf_op jit(solution)/shard_map/ppermute | solution.py:93
  19.4 17.0 %collective-permute-start.4 = (f32[4,16,128]{2,1,0:T(8,128)S(1)}, f32[4,16,128]{2,1,0:T(8,128)S(1)}, u32[]{:S(2)}, u32[]{:S(2)}) collective-permute-start(f32[4,16,128]{2,1,0:T(8,128)S(1)} %get-tuple-element.220), channel_id=1, source_target_pairs={{1,16},{2,17},{3,18},{4,19},{5,20},{6,21},{7,22},{8,23},{9,24},{10... | collective-permute-start | bytes 98312 | tf_op jit(solution)/shard_map/ppermute | solution.py:110
  26.6 9.8 %collective-permute-start.3 = (f32[4,16,128]{2,1,0:T(8,128)S(1)}, f32[4,16,128]{2,1,0:T(8,128)S(1)}, u32[]{:S(2)}, u32[]{:S(2)}) collective-permute-start(f32[4,16,128]{2,1,0:T(8,128)S(1)} %get-tuple-element.221), channel_id=1, source_target_pairs={{0,17},{1,18},{2,19},{3,20},{4,21},{5,22},{6,23},{7,24},{8,25},{9,... | collective-permute-start | bytes 98312 | tf_op jit(solution)/shard_map/ppermute | solution.py:108
  28.5 7.9 %collective-permute-start.2 = (f32[4,64,128]{2,1,0:T(8,128)S(1)}, f32[4,64,128]{2,1,0:T(8,128)S(1)}, u32[]{:S(2)}, u32[]{:S(2)}) collective-permute-start(f32[4,64,128]{2,1,0:T(8,128)S(1)} %slice.2242), channel_id=1, source_target_pairs={{112,0},{0,16},{16,32},{32,48},{48,64},{64,80},{80,96},{96,112},{1... | collective-permute-start | bytes 393224 | tf_op jit(solution)/shard_map/ppermute | solution.py:18
  40.5 8.3 %collective-permute-start.6 = (f32[384,128]{1,0:T(8,128)S(1)}, f32[384,128]{1,0:T(8,128)S(1)}, u32[]{:S(2)}, u32[]{:S(2)}) collective-permute-start(f32[384,128]{1,0:T(8,128)S(1)} %constant_dynamic-update-slice_fusion.11), channel_id=1, source_target_pairs={{1,0},{2,1},{3,2},{4,3},{5,4},{6,5},{7,6},{8,7},{9,8},{10,9},{11,1... | collective-permute-start | bytes 589832 | tf_op jit(solution)/shard_map/ppermute | solution.py:144
  45.6 9.4 %collective-permute-start.5 = (f32[384,128]{1,0:T(8,128)S(1)}, f32[384,128]{1,0:T(8,128)S(1)}, u32[]{:S(2)}, u32[]{:S(2)}) collective-permute-start(f32[384,128]{1,0:T(8,128)S(1)} %constant_dynamic-update-slice_fusion.3), channel_id=1, source_target_pairs={{0,1},{1,2},{2,3},{3,4},{4,5},{5,6},{6,7},{7,8},{8,9},{9,10},{10,1... | collective-permute-start | bytes 589832 | tf_op jit(solution)/shard_map/ppermute | solution.py:143
  59.2 2.9 %copy-start.4 = (s32[8]{0:T(128)S(1)}, s32[8]{0:T(128)}, u32[]{:S(2)}) copy-start(s32[8]{0:T(128)} %param.7) | copy-start | bytes 100
  60.1 9.7 %collective-permute-start.7 = (f32[4,16,128]{2,1,0:T(8,128)S(1)}, f32[4,16,128]{2,1,0:T(8,128)S(1)}, u32[]{:S(2)}, u32[]{:S(2)}) collective-permute-start(f32[4,16,128]{2,1,0:T(8,128)S(1)} %get-tuple-element.211), channel_id=1, source_target_pairs={{0,113},{1,114},{2,115},{3,116},{4,117},{5,118},{6,119},{7,120},{8... | collective-permute-start | bytes 98312 | tf_op jit(solution)/shard_map/ppermute | solution.py:108
  62.0 7.8 %collective-permute-start.8 = (f32[4,64,128]{2,1,0:T(8,128)S(1)}, f32[4,64,128]{2,1,0:T(8,128)S(1)}, u32[]{:S(2)}, u32[]{:S(2)}) collective-permute-start(f32[4,64,128]{2,1,0:T(8,128)S(1)} %slice.2309), channel_id=1, source_target_pairs={{16,0},{32,16},{48,32},{64,48},{80,64},{96,80},{112,96},{0,112},{1... | collective-permute-start | bytes 393224 | tf_op jit(solution)/shard_map/ppermute | solution.py:18
  62.3 8.8 %collective-permute-start.9 = (f32[4,16,128]{2,1,0:T(8,128)S(1)}, f32[4,16,128]{2,1,0:T(8,128)S(1)}, u32[]{:S(2)}, u32[]{:S(2)}) collective-permute-start(f32[4,16,128]{2,1,0:T(8,128)S(1)} %get-tuple-element.210), channel_id=1, source_target_pairs={{1,112},{2,113},{3,114},{4,115},{5,116},{6,117},{7,118},{8,119},{9... | collective-permute-start | bytes 98312 | tf_op jit(solution)/shard_map/ppermute | solution.py:110
  73.9 0.9 copy-start.3
  75.5 1.0 slice-start

commit v8 on v5

--- a/solution.py
+++ b/solution.py
@@ -92,9 +92,18 @@
     far = band(fwd_need[0])
     assert far <= rows
 
-    before = lax.ppermute(packed[:, rows - far :], "tile", [(i, i + 1) for i in range(tiles - 1)])
-    after = lax.ppermute(packed[:, :far], "tile", [(i + 1, i) for i in range(tiles - 1)])
-    wide = jnp.concatenate([before, packed, after], axis=1)
+    near = band(2 * steps)
+    tile_down = [(i, i + 1) for i in range(tiles - 1)]
+    tile_up = [(i + 1, i) for i in range(tiles - 1)]
+    before = lax.ppermute(packed[:, rows - near :], "tile", tile_down)
+    after = lax.ppermute(packed[:, :near], "tile", tile_up)
+    (far_down, far_up), (before, after) = lax.optimization_barrier(
+        ((packed[:, rows - far : rows - near], packed[:, near:far]), (before, after))
+    )
+    before_far = lax.ppermute(far_down, "tile", tile_down)
+    after_far = lax.ppermute(far_up, "tile", tile_up)
+    narrow = jnp.concatenate([before, packed, after], axis=1)
+    wide = jnp.concatenate([before_far, before, packed, after, after_far], axis=1)
 
     def fields(block, have):
         ext = rows + 2 * have
@@ -104,7 +113,7 @@
         mask = ((row >= 0) & (row < tiles * rows)).astype(jnp.float32)[:, None]
         return flow, drive, block[-1], mask, have
 
-    sweep_fields = [fields(wide, far)] * 2
+    sweep_fields = [fields(narrow, near), fields(wide, far)]
     def slab_start(own, shift, depth):
         onward = lambda j, t: ((j + shift) % slabs) * tiles + t
         both = ("slab", "tile")
@@ -145,7 +154,7 @@
         [band(2 * m + 2) for m in range(steps)],
         [band(2 * m + 2) for m in range(steps)],
     ]
-    flow, drive, damp, mask, held = sweep_fields[1]
+    flow, drive, damp, mask, held = sweep_fields[0]
     have = adj_bands[0][steps - 1]
     start = jnp.zeros((count_f, rows + 2 * have, columns), jnp.float32)
     for sweep in range(SWEEPS):

time: 111 us -> 114 us (1.027)
  starting transfers between devices: 31 us -> 38 us
  waiting for transfers between devices: 18 us -> 13.6 us
    ppermute x2 -> x4, starting transfers between devices: 7.95 us -> 16.1 us  [the longest x1 6.04 us: on_device(): after = lax.ppermute(packed[:, :near], 'tile', tile_up)]
    ppermute x2, waiting for transfers between devices: 4.33 us -> 1.4 us  [passed_along(): return lax.ppermute(block, axis, route)]
    ppermute x2, starting transfers between devices: 15.6 us -> 13.5 us  [slab_start(): lax.ppermute(own[:, rows - depth:], both, [(j * tiles + t, onward(j, t +...]
    ppermute x2, waiting for transfers between devices: 3.9 us -> 2.04 us  [slab_start(): lax.ppermute(own[:, :depth], both, [(j * tiles + t + 1, onward(j, t)) for...]
    ppermute x2, starting transfers between devices: 1.63 us -> 3.06 us  [passed_along(): return lax.ppermute(block, axis, route)]
    ppermute x2 -> x4, waiting for transfers between devices: 9.79 us -> 10.2 us  [the longest x1 3.85 us: on_device(): before_far = lax.ppermute(far_down, 'tile', tile_down)]
  transfers between devices with their start and end apart: 8 -> 10, of which waited for: 6 -> 6; matrix products, arithmetic and copies ran while one was open for 1% -> 1% of each run, Pallas kernels for 0% -> 0%
where the time goes in v8:
time: 114 us; the launch traced here: 113 us
  starting transfers between devices  38 us (33%)
  blocking collectives  32.9 us (29%)
  other arithmetic  21.7 us (19%)
  waiting for transfers between devices  13.6 us (12%)
  local copies, waits for them, and re-layouts  3.88 us (3%)
  matrix products  1.77 us (2%)
    all_to_all x1, blocking collectives, on_device(): lax.all_to_all(terms.reshape(slabs, 2 * H // slabs, count_f, rows, column...  32.9 us
    ppermute x2, starting transfers between devices, slab_start(): lax.ppermute(own[:, rows - depth:], both, [(j * tiles + t, onward(j, t +...  13.5 us
    mul x28, other arithmetic, adjoint_rate(): flux_y = pad_grid(speed_y * state)  7.64 us
    ppermute x1, starting transfers between devices, on_device(): after = lax.ppermute(packed[:, :near], 'tile', tile_up)  6.04 us
    ppermute x1, starting transfers between devices, on_device(): after_far = lax.ppermute(far_up, 'tile', tile_up)  5.5 us
    ppermute x2, starting transfers between devices, slab_start(): lax.ppermute(own[:, :depth], both, [(j * tiles + t + 1, onward(j, t)) for...  5.32 us
    add x14, other arithmetic, on_device(): state + first  4.11 us
    add x15, other arithmetic, on_device(): state = state + 0.5 * (first + second)  3.98 us
  transfers between devices with their start and end apart: 10, of which 6 were waited for; matrix products, arithmetic and copies ran while one was open for 1% of the time, Pallas kernels for 0%

profile of v8, /device:TPU:16, one launch (start us, length us, event | category | flops | bytes accessed | tf_op | source)
XLA Modules:
  0.0 112.9 jit_solution(17781990052433828550)
XLA Ops:
  0.0 1.7 %pad_maximum_fusion.1 = f32[49,64,128]{2,1,0:T(8,128)S(1)} fusion(f32[1,64,128]{2,1,0:T(8,128)} %bitcast.167, f32[32,64,128]{2,1,0:T(8,128)} %bitcast.138, f32[16,64,128]{2,1,0:T(8,128)} %bitcast.151), kind=kLoop, calls=%fused_computation.1 | loop fusion | flops 802816 | bytes 3211264 | tf_op jit(solution)/shard_map/concatenate | solution.py:75
  1.7 1.0 fusion.581
  2.7 1.9 %collective-permute-start = (f32[49,16,128]{2,1,0:T(8,128)}, f32[49,16,128]{2,1,0:T(8,128)S(1)}, u32[]{:S(2)}, u32[]{:S(2)}) collective-permute-start(f32[49,16,128]{2,1,0:T(8,128)} %get-tuple-element.140), channel_id=1, source_target_pairs={{0,1},{1,2},{2,3},{3,4},{4,5},{5,6},{6,7},{7,8},{8,9},{9,10},{10,1... | collective-permute-start | bytes 1204232 | tf_op jit(solution)/shard_map/ppermute | solution.py:98
  4.6 6.0 %collective-permute-start.1 = (f32[49,16,128]{2,1,0:T(8,128)}, f32[49,16,128]{2,1,0:T(8,128)S(1)}, u32[]{:S(2)}, u32[]{:S(2)}) collective-permute-start(f32[49,16,128]{2,1,0:T(8,128)} %get-tuple-element.139), channel_id=1, source_target_pairs={{1,0},{2,1},{3,2},{4,3},{5,4},{6,5},{7,6},{8,7},{9,8},{10,9},{11,1... | collective-permute-start | bytes 1204232 | tf_op jit(solution)/shard_map/ppermute | solution.py:99
  10.9 3.6 %collective-permute-done = f32[49,16,128]{2,1,0:T(8,128)S(1)} collective-permute-done((f32[49,16,128]{2,1,0:T(8,128)}, f32[49,16,128]{2,1,0:T(8,128)S(1)}, u32[]{:S(2)}, u32[]{:S(2)}) %collective-permute-start) | collective-permute-done | bytes 401440 | tf_op jit(solution)/shard_map/ppermute | solution.py:98
  14.5 1.9 %collective-permute-done.1 = f32[49,16,128]{2,1,0:T(8,128)S(1)} collective-permute-done((f32[49,16,128]{2,1,0:T(8,128)}, f32[49,16,128]{2,1,0:T(8,128)S(1)}, u32[]{:S(2)}, u32[]{:S(2)}) %collective-permute-start.1) | collective-permute-done | bytes 401440 | tf_op jit(solution)/shard_map/ppermute | solution.py:99
  21.1 6.1 %collective-permute-start.2 = (f32[4,32,128]{2,1,0:T(8,128)S(1)}, f32[4,32,128]{2,1,0:T(8,128)S(1)}, u32[]{:S(2)}, u32[]{:S(2)}) collective-permute-start(f32[4,32,128]{2,1,0:T(8,128)S(1)} %get-tuple-element.214), channel_id=1, source_target_pairs={{0,17},{1,18},{2,19},{3,20},{4,21},{5,22},{6,23},{7,24},{8,25},{9,... | collective-permute-start | bytes 196616 | tf_op jit(solution)/shard_map/ppermute | solution.py:120
  27.2 1.6 %collective-permute-start.3 = (f32[4,64,128]{2,1,0:T(8,128)S(1)}, f32[4,64,128]{2,1,0:T(8,128)S(1)}, u32[]{:S(2)}, u32[]{:S(2)}) collective-permute-start(f32[4,64,128]{2,1,0:T(8,128)S(1)} %slice.2235), channel_id=1, source_target_pairs={{112,0},{0,16},{16,32},{32,48},{48,64},{64,80},{80,96},{96,112},{1... | collective-permute-start | bytes 393224 | tf_op jit(solution)/shard_map/ppermute | solution.py:18
  28.7 3.1 %collective-permute-start.4 = (f32[4,32,128]{2,1,0:T(8,128)S(1)}, f32[4,32,128]{2,1,0:T(8,128)S(1)}, u32[]{:S(2)}, u32[]{:S(2)}) collective-permute-start(f32[4,32,128]{2,1,0:T(8,128)S(1)} %get-tuple-element.213), channel_id=1, source_target_pairs={{1,16},{2,17},{3,18},{4,19},{5,20},{6,21},{7,22},{8,23},{9,24},{10... | collective-permute-start | bytes 196616 | tf_op jit(solution)/shard_map/ppermute | solution.py:122
  31.9 2.6 %collective-permute-start.5 = (f32[49,16,128]{2,1,0:T(8,128)S(1)}, f32[49,16,128]{2,1,0:T(8,128)S(1)}, u32[]{:S(2)}, u32[]{:S(2)}) collective-permute-start(f32[49,16,128]{2,1,0:T(8,128)S(1)} %get-tuple-element.11), channel_id=1, source_target_pairs={{0,1},{1,2},{2,3},{3,4},{4,5},{5,6},{6,7},{7,8},{8,9},{9,10},{10,1... | collective-permute-start | bytes 1204232 | tf_op jit(solution)/shard_map/ppermute | solution.py:103
  34.5 5.5 %collective-permute-start.6 = (f32[49,16,128]{2,1,0:T(8,128)S(1)}, f32[49,16,128]{2,1,0:T(8,128)S(1)}, u32[]{:S(2)}, u32[]{:S(2)}) collective-permute-start(f32[49,16,128]{2,1,0:T(8,128)S(1)} %get-tuple-element.12), channel_id=1, source_target_pairs={{1,0},{2,1},{3,2},{4,3},{5,4},{6,5},{7,6},{8,7},{9,8},{10,9},{11,1... | collective-permute-start | bytes 1204232 | tf_op jit(solution)/shard_map/ppermute | solution.py:104
  40.2 3.9 %collective-permute-done.5 = f32[49,16,128]{2,1,0:T(8,128)S(1)} collective-permute-done((f32[49,16,128]{2,1,0:T(8,128)S(1)}, f32[49,16,128]{2,1,0:T(8,128)S(1)}, u32[]{:S(2)}, u32[]{:S(2)}) %collective-permute-start.5) | collective-permute-done | bytes 401440 | tf_op jit(solution)/shard_map/ppermute | solution.py:103
  44.4 0.9 collective-permute-done.6
  45.5 0.4 fusion.2
  45.9 0.3 multiply_add_fusion.4
  46.2 0.4 fusion.1
  46.6 0.3 multiply_add_fusion.2
  46.9 0.4 fusion
  47.3 0.3 multiply_add_fusion
  47.7 0.3 fusion.5
  48.3 0.3 fusion.4
  49.0 0.3 fusion.3
  55.3 7.4 %collective-permute-start.7 = (f32[4,16,128]{2,1,0:T(8,128)S(1)}, f32[4,16,128]{2,1,0:T(8,128)S(1)}, u32[]{:S(2)}, u32[]{:S(2)}) collective-permute-start(f32[4,16,128]{2,1,0:T(8,128)S(1)} %get-tuple-element.212), channel_id=1, source_target_pairs={{0,113},{1,114},{2,115},{3,116},{4,117},{5,118},{6,119},{7,120},{8... | collective-permute-start | bytes 98312 | tf_op jit(solution)/shard_map/ppermute | solution.py:120
  62.7 1.5 %collective-permute-start.8 = (f32[4,64,128]{2,1,0:T(8,128)S(1)}, f32[4,64,128]{2,1,0:T(8,128)S(1)}, u32[]{:S(2)}, u32[]{:S(2)}) collective-permute-start(f32[4,64,128]{2,1,0:T(8,128)S(1)} %slice.2300), channel_id=1, source_target_pairs={{16,0},{32,16},{48,32},{64,48},{80,64},{96,80},{112,96},{0,112},{1... | collective-permute-start | bytes 393224 | tf_op jit(solution)/shard_map/ppermute | solution.py:18
  64.4 2.2 %collective-permute-start.9 = (f32[4,16,128]{2,1,0:T(8,128)S(1)}, f32[4,16,128]{2,1,0:T(8,128)S(1)}, u32[]{:S(2)}, u32[]{:S(2)}) collective-permute-start(f32[4,16,128]{2,1,0:T(8,128)S(1)} %get-tuple-element.211), channel_id=1, source_target_pairs={{1,112},{2,113},{3,114},{4,115},{5,116},{6,117},{7,118},{8,119},{9... | collective-permute-start | bytes 98312 | tf_op jit(solution)/shard_map/ppermute | solution.py:122
  66.6 1.4 %collective-permute-done.8 = f32[4,64,128]{2,1,0:T(8,128)S(1)} collective-permute-done((f32[4,64,128]{2,1,0:T(8,128)S(1)}, f32[4,64,128]{2,1,0:T(8,128)S(1)}, u32[]{:S(2)}, u32[]{:S(2)}) %collective-permute-start.8) | collective-permute-done | bytes 131104 | tf_op jit(solution)/shard_map/ppermute | solution.py:18
  68.0 2.0 %collective-permute-done.9 = f32[4,16,128]{2,1,0:T(8,128)S(1)} collective-permute-done((f32[4,16,128]{2,1,0:T(8,128)S(1)}, f32[4,16,128]{2,1,0:T(8,128)S(1)}, u32[]{:S(2)}, u32[]{:S(2)}) %collective-permute-start.9) | collective-permute-done | bytes 32800 | tf_op jit(solution)/shard_map/ppermute | solution.py:122
  75.4 1.6 %stack.41 = f32[8,32768]{1,0:T(8,128)S(1)} concatenate(f32[1,32768]{1,0:T(1,128)S(1)} %bitcast.185, f32[1,32768]{1,0:T(1,128)S(1)} %bitcast.184, f32[1,32768]{1,0:T(1,128)S(1)} %bitcast.186, f32[1,32768]{1,0:T(1,128)S(1)} %bitcast.187, f32[1,32768]{1,0:T(1,128)S(1)} %bitcast.183, f32[1,32768]{1,0:T(1,128)S(1)} %bitcast.188, f32[1,32768]{1,0:T(1,128)S(1)} %bitcast.189, ...), dimensions={0} | concatenate | bytes 2097152 | tf_op jit(solution)/shard_map/stack | solution.py:178
  77.0 1.8 %fusion.537 = f32[8,2,4,64,128]{4,0,3,2,1:T(8,128)S(1)} fusion(f32[4,64,128,8,1]{2,3,1,0,4:T(8,128)S(1)} %bitcast.180, f32[8,1,8]{2,0,1:T(8,128)S(1)} %get-tuple-element.217, f32[8,1,8]{2,0,1:T(8,128)S(1)} %get-tuple-element.216), kind=kOutput, calls=%fused_computation.1131 | convolution fusion | flops 50331904 | bytes 3146240 | tf_op jit(solution)/shard_map/dot_general | solution.py:182
  78.8 0.4 copy.5
  79.2 32.9 %all_to_all.5 = f32[8,2,4,64,128]{4,3,2,1,0:T(8,128)S(1)} all-to-all(f32[8,2,4,64,128]{4,3,2,1,0:T(8,128)S(1)} %copy.5), channel_id=1, replica_groups=mesh['slab'=8,'tile'=16] {'slab'}, dimensions={0} | all-to-all | bytes 4194304 | tf_op jit(solution)/shard_map/all_to_all | solution.py:183
  112.1 0.8 reduce_sum.9
  (150 shorter events, 17.0 us)
Async XLA Ops:
  0.0 16.4 %copy-start = (f32[8,4,64,128]{3,2,1,0:T(8,128)S(1)}, f32[8,4,64,128]{3,2,1,0:T(8,128)}, u32[]{:S(2)}) copy-start(f32[8,4,64,128]{3,2,1,0:T(8,128)} %param.5) | copy-start | bytes 3145732
  0.0 16.4 %copy-start.1 = (f32[2,8,64,128]{3,2,1,0:T(8,128)S(1)}, f32[2,8,64,128]{3,2,1,0:T(8,128)}, u32[]{:S(2)}) copy-start(f32[2,8,64,128]{3,2,1,0:T(8,128)} %param.4) | copy-start | bytes 1572868
  0.0 16.4 %copy-start.2 = (f32[64,128]{1,0:T(8,128)S(1)}, f32[64,128]{1,0:T(8,128)}, u32[]{:S(2)}) copy-start(f32[64,128]{1,0:T(8,128)} %param.6) | copy-start | bytes 98308
  2.7 11.8 %collective-permute-start = (f32[49,16,128]{2,1,0:T(8,128)}, f32[49,16,128]{2,1,0:T(8,128)S(1)}, u32[]{:S(2)}, u32[]{:S(2)}) collective-permute-start(f32[49,16,128]{2,1,0:T(8,128)} %get-tuple-element.140), channel_id=1, source_target_pairs={{0,1},{1,2},{2,3},{3,4},{4,5},{5,6},{6,7},{7,8},{8,9},{9,10},{10,1... | collective-permute-start | bytes 1204232 | tf_op jit(solution)/shard_map/ppermute | solution.py:98
  4.6 11.8 %collective-permute-start.1 = (f32[49,16,128]{2,1,0:T(8,128)}, f32[49,16,128]{2,1,0:T(8,128)S(1)}, u32[]{:S(2)}, u32[]{:S(2)}) collective-permute-start(f32[49,16,128]{2,1,0:T(8,128)} %get-tuple-element.139), channel_id=1, source_target_pairs={{1,0},{2,1},{3,2},{4,3},{5,4},{6,5},{7,6},{8,7},{9,8},{10,9},{11,1... | collective-permute-start | bytes 1204232 | tf_op jit(solution)/shard_map/ppermute | solution.py:99
  21.1 19.1 %collective-permute-start.2 = (f32[4,32,128]{2,1,0:T(8,128)S(1)}, f32[4,32,128]{2,1,0:T(8,128)S(1)}, u32[]{:S(2)}, u32[]{:S(2)}) collective-permute-start(f32[4,32,128]{2,1,0:T(8,128)S(1)} %get-tuple-element.214), channel_id=1, source_target_pairs={{0,17},{1,18},{2,19},{3,20},{4,21},{5,22},{6,23},{7,24},{8,25},{9,... | collective-permute-start | bytes 196616 | tf_op jit(solution)/shard_map/ppermute | solution.py:120
  27.2 13.0 %collective-permute-start.3 = (f32[4,64,128]{2,1,0:T(8,128)S(1)}, f32[4,64,128]{2,1,0:T(8,128)S(1)}, u32[]{:S(2)}, u32[]{:S(2)}) collective-permute-start(f32[4,64,128]{2,1,0:T(8,128)S(1)} %slice.2235), channel_id=1, source_target_pairs={{112,0},{0,16},{16,32},{32,48},{48,64},{64,80},{80,96},{96,112},{1... | collective-permute-start | bytes 393224 | tf_op jit(solution)/shard_map/ppermute | solution.py:18
  28.7 11.4 %collective-permute-start.4 = (f32[4,32,128]{2,1,0:T(8,128)S(1)}, f32[4,32,128]{2,1,0:T(8,128)S(1)}, u32[]{:S(2)}, u32[]{:S(2)}) collective-permute-start(f32[4,32,128]{2,1,0:T(8,128)S(1)} %get-tuple-element.213), channel_id=1, source_target_pairs={{1,16},{2,17},{3,18},{4,19},{5,20},{6,21},{7,22},{8,23},{9,24},{10... | collective-permute-start | bytes 196616 | tf_op jit(solution)/shard_map/ppermute | solution.py:122
  31.9 12.2 %collective-permute-start.5 = (f32[49,16,128]{2,1,0:T(8,128)S(1)}, f32[49,16,128]{2,1,0:T(8,128)S(1)}, u32[]{:S(2)}, u32[]{:S(2)}) collective-permute-start(f32[49,16,128]{2,1,0:T(8,128)S(1)} %get-tuple-element.11), channel_id=1, source_target_pairs={{0,1},{1,2},{2,3},{3,4},{4,5},{5,6},{6,7},{7,8},{8,9},{9,10},{10,1... | collective-permute-start | bytes 1204232 | tf_op jit(solution)/shard_map/ppermute | solution.py:103
  34.5 10.7 %collective-permute-start.6 = (f32[49,16,128]{2,1,0:T(8,128)S(1)}, f32[49,16,128]{2,1,0:T(8,128)S(1)}, u32[]{:S(2)}, u32[]{:S(2)}) collective-permute-start(f32[49,16,128]{2,1,0:T(8,128)S(1)} %get-tuple-element.12), channel_id=1, source_target_pairs={{1,0},{2,1},{3,2},{4,3},{5,4},{6,5},{7,6},{8,7},{9,8},{10,9},{11,1... | collective-permute-start | bytes 1204232 | tf_op jit(solution)/shard_map/ppermute | solution.py:104
  54.1 10.1 %copy-start.4 = (s32[8]{0:T(128)S(1)}, s32[8]{0:T(128)}, u32[]{:S(2)}) copy-start(s32[8]{0:T(128)} %param.7) | copy-start | bytes 100
  55.3 11.3 %collective-permute-start.7 = (f32[4,16,128]{2,1,0:T(8,128)S(1)}, f32[4,16,128]{2,1,0:T(8,128)S(1)}, u32[]{:S(2)}, u32[]{:S(2)}) collective-permute-start(f32[4,16,128]{2,1,0:T(8,128)S(1)} %get-tuple-element.212), channel_id=1, source_target_pairs={{0,113},{1,114},{2,115},{3,116},{4,117},{5,118},{6,119},{7,120},{8... | collective-permute-start | bytes 98312 | tf_op jit(solution)/shard_map/ppermute | solution.py:120
  62.7 5.3 %collective-permute-start.8 = (f32[4,64,128]{2,1,0:T(8,128)S(1)}, f32[4,64,128]{2,1,0:T(8,128)S(1)}, u32[]{:S(2)}, u32[]{:S(2)}) collective-permute-start(f32[4,64,128]{2,1,0:T(8,128)S(1)} %slice.2300), channel_id=1, source_target_pairs={{16,0},{32,16},{48,32},{64,48},{80,64},{96,80},{112,96},{0,112},{1... | collective-permute-start | bytes 393224 | tf_op jit(solution)/shard_map/ppermute | solution.py:18
  64.4 5.7 %collective-permute-start.9 = (f32[4,16,128]{2,1,0:T(8,128)S(1)}, f32[4,16,128]{2,1,0:T(8,128)S(1)}, u32[]{:S(2)}, u32[]{:S(2)}) collective-permute-start(f32[4,16,128]{2,1,0:T(8,128)S(1)} %get-tuple-element.211), channel_id=1, source_target_pairs={{1,112},{2,113},{3,114},{4,115},{5,116},{6,117},{7,118},{8,119},{9... | collective-permute-start | bytes 98312 | tf_op jit(solution)/shard_map/ppermute | solution.py:122
  72.8 1.3 %copy-start.3 = (f32[4,96,128]{2,1,0:T(8,128)}, f32[4,96,128]{2,1,0:T(8,128)S(1)}, u32[]{:S(2)}) copy-start(f32[4,96,128]{2,1,0:T(8,128)S(1)} %fusion.154) | copy-start | bytes 589828
  74.1 1.3 %slice-start = ((f32[4,96,128]{2,1,0:T(8,128)}), f32[4,64,128]{2,1,0:T(8,128)S(1)}, s32[]{:S(2)}) async-start(f32[4,96,128]{2,1,0:T(8,128)} %copy-done.3), calls=%async_computation.1 | async-start | bytes 262144 | tf_op jit(solution)/shard_map/slice | solution.py:84

commit v9 on v8

--- a/solution.py
+++ b/solution.py
@@ -4,6 +4,7 @@
 import jax.numpy as jnp
 from jax import lax
 from jax.sharding import PartitionSpec as P
+
 
 SWEEPS = 2
 H = 8
@@ -16,13 +17,6 @@
     devices = range(lax.axis_size(axis))
     route = [((i - distance) % len(devices), i) for i in devices]
     return lax.ppermute(block, axis, route)
-
-
-def with_neighbours(block, axis, dim):
-    count = lax.axis_size(axis)
-    before = lax.ppermute(block, axis, [(i, i + 1) for i in range(count - 1)])
-    after = lax.ppermute(block, axis, [(i + 1, i) for i in range(count - 1)])
-    return jnp.concatenate([before, block, after], axis=dim)
 
 
 def pad_grid(field):
@@ -65,7 +59,7 @@
     return table.reshape(2 * chosen.shape[0], phase.shape[0])
 
 
-def on_device(base_flow, forcing, damping, harmonics):
+def whole(base_flow, forcing, damping, harmonics):
     steps = forcing.shape[0]
     count_f, rows, columns = (forcing.shape[1], forcing.shape[2], forcing.shape[3])
     slabs = lax.axis_size("slab")
@@ -114,6 +108,7 @@
         return flow, drive, block[-1], mask, have
 
     sweep_fields = [fields(narrow, near), fields(wide, far)]
+
     def slab_start(own, shift, depth):
         onward = lambda j, t: ((j + shift) % slabs) * tiles + t
         both = ("slab", "tile")
@@ -175,18 +170,16 @@
         if sweep + 1 < SWEEPS:
             start = slab_start(cut(state, have, 0), -1, tail)
             have = tail
-    adjoint = jnp.stack(record, axis=0)
     phase = lax.axis_index("slab") * steps + jnp.arange(steps, dtype=jnp.int32)
-    flat = adjoint.reshape(steps, count_f * rows * columns)
     table = coefficient_table(harmonics, phase, periods)
-    terms = jnp.dot(table, flat, precision=lax.Precision.HIGHEST)
+    terms = sum(table[:, m, None, None, None] * record[m][None] for m in range(steps))
     parts = lax.all_to_all(terms.reshape(slabs, 2 * H // slabs, count_f, rows, columns), "slab", 0, 0, tiled=True)
     return jnp.sum(parts, axis=0, keepdims=True)
 
 
 def solution(mesh):
     return jax.shard_map(
-        on_device,
+        whole,
         mesh=mesh,
         in_specs=(
             P(None, "slab", "tile", None),

time: 114 us -> 113 us (level)
  matrix products: 1.77 us -> 0 us
    dot_general x1 -> x0, matrix products: 1.77 us -> none  [on_device(): terms = jnp.dot(table, flat, precision=lax.Precision.HIGHEST)]
    another operation x2 -> x1, local copies, waits for them, and re-layouts: 1.63 us -> 0.01 us  [the longest x1 1.62 us: on_device(): adjoint = jnp.stack(record, axis=0)]
    add x30 -> x32, other arithmetic: 8.1 us -> 9.44 us  [the longest x14 4.11 us: whole(): state + first]
  transfers between devices with their start and end apart: 10 -> 10, of which waited for: 6 -> 6; matrix products, arithmetic and copies ran while one was open for 1% -> 2% of each run, Pallas kernels for 0% -> 0%
where the time goes in v9:
time: 113 us; the launch traced here: 111 us
  starting transfers between devices  38.3 us (34%)
  blocking collectives  32.9 us (29%)
  other arithmetic  22.7 us (20%)
  waiting for transfers between devices  13.2 us (12%)
  local copies, waits for them, and re-layouts  3 us (3%)
  between operations  1.16 us (1%)
    all_to_all x1, blocking collectives, whole(): lax.all_to_all(terms.reshape(slabs, 2 * H // slabs, count_f, rows, column...  32.9 us
    ppermute x2, starting transfers between devices, slab_start(): lax.ppermute(own[:, rows - depth:], both, [(j * tiles + t, onward(j, t +...  13.9 us
    mul x28, other arithmetic, adjoint_rate(): flux_y = pad_grid(speed_y * state)  7.48 us
    ppermute x1, starting transfers between devices, whole(): after = lax.ppermute(packed[:, :near], 'tile', tile_up)  6.05 us
    ppermute x2, starting transfers between devices, slab_start(): lax.ppermute(own[:, :depth], both, [(j * tiles + t + 1, onward(j, t)) for...  5.19 us
    ppermute x1, starting transfers between devices, whole(): after_far = lax.ppermute(far_up, 'tile', tile_up)  5.18 us
    add x14, other arithmetic, whole(): state + first  4.11 us
    add x16, other arithmetic, whole(): state = state + 0.5 * (first + second)  4.01 us
  transfers between devices with their start and end apart: 10, of which 6 were waited for; matrix products, arithmetic and copies ran while one was open for 2% of the time, Pallas kernels for 0%

profile of v9, /device:TPU:16, one launch (start us, length us, event | category | flops | bytes accessed | tf_op | source)
XLA Modules:
  0.0 111.2 jit_solution(12126906516234594300)
XLA Ops:
  0.0 1.5 %pad_maximum_fusion.1 = f32[49,64,128]{2,1,0:T(8,128)S(1)} fusion(f32[1,64,128]{2,1,0:T(8,128)} %bitcast.149, f32[32,64,128]{2,1,0:T(8,128)} %bitcast.120, f32[16,64,128]{2,1,0:T(8,128)} %bitcast.133), kind=kLoop, calls=%fused_computation.2 | loop fusion | flops 802816 | bytes 3211264 | tf_op jit(solution)/shard_map/concatenate | solution.py:69
  1.6 1.1 fusion.573
  2.7 1.9 %collective-permute-start = (f32[49,16,128]{2,1,0:T(8,128)}, f32[49,16,128]{2,1,0:T(8,128)S(1)}, u32[]{:S(2)}, u32[]{:S(2)}) collective-permute-start(f32[49,16,128]{2,1,0:T(8,128)} %get-tuple-element.148), channel_id=1, source_target_pairs={{0,1},{1,2},{2,3},{3,4},{4,5},{5,6},{6,7},{7,8},{8,9},{9,10},{10,1... | collective-permute-start | bytes 1204232 | tf_op jit(solution)/shard_map/ppermute | solution.py:92
  4.6 6.0 %collective-permute-start.1 = (f32[49,16,128]{2,1,0:T(8,128)S(1)}, f32[49,16,128]{2,1,0:T(8,128)S(1)}, u32[]{:S(2)}, u32[]{:S(2)}) collective-permute-start(f32[49,16,128]{2,1,0:T(8,128)S(1)} %get-tuple-element.147), channel_id=1, source_target_pairs={{1,0},{2,1},{3,2},{4,3},{5,4},{6,5},{7,6},{8,7},{9,8},{10,9},{11,1... | collective-permute-start | bytes 1204232 | tf_op jit(solution)/shard_map/ppermute | solution.py:93
  11.0 3.4 %collective-permute-done = f32[49,16,128]{2,1,0:T(8,128)S(1)} collective-permute-done((f32[49,16,128]{2,1,0:T(8,128)}, f32[49,16,128]{2,1,0:T(8,128)S(1)}, u32[]{:S(2)}, u32[]{:S(2)}) %collective-permute-start) | collective-permute-done | bytes 401440 | tf_op jit(solution)/shard_map/ppermute | solution.py:92
  14.5 1.6 %collective-permute-done.1 = f32[49,16,128]{2,1,0:T(8,128)S(1)} collective-permute-done((f32[49,16,128]{2,1,0:T(8,128)S(1)}, f32[49,16,128]{2,1,0:T(8,128)S(1)}, u32[]{:S(2)}, u32[]{:S(2)}) %collective-permute-start.1) | collective-permute-done | bytes 401440 | tf_op jit(solution)/shard_map/ppermute | solution.py:93
  20.7 6.2 %collective-permute-start.2 = (f32[4,32,128]{2,1,0:T(8,128)S(1)}, f32[4,32,128]{2,1,0:T(8,128)S(1)}, u32[]{:S(2)}, u32[]{:S(2)}) collective-permute-start(f32[4,32,128]{2,1,0:T(8,128)S(1)} %get-tuple-element.222), channel_id=1, source_target_pairs={{0,17},{1,18},{2,19},{3,20},{4,21},{5,22},{6,23},{7,24},{8,25},{9,... | collective-permute-start | bytes 196616 | tf_op jit(solution)/shard_map/ppermute | solution.py:115
  26.9 1.6 %collective-permute-start.3 = (f32[4,64,128]{2,1,0:T(8,128)S(1)}, f32[4,64,128]{2,1,0:T(8,128)S(1)}, u32[]{:S(2)}, u32[]{:S(2)}) collective-permute-start(f32[4,64,128]{2,1,0:T(8,128)S(1)} %slice.2268), channel_id=1, source_target_pairs={{112,0},{0,16},{16,32},{32,48},{48,64},{64,80},{80,96},{96,112},{1... | collective-permute-start | bytes 393224 | tf_op jit(solution)/shard_map/ppermute | solution.py:19
  28.5 3.0 %collective-permute-start.4 = (f32[4,32,128]{2,1,0:T(8,128)S(1)}, f32[4,32,128]{2,1,0:T(8,128)S(1)}, u32[]{:S(2)}, u32[]{:S(2)}) collective-permute-start(f32[4,32,128]{2,1,0:T(8,128)S(1)} %get-tuple-element.221), channel_id=1, source_target_pairs={{1,16},{2,17},{3,18},{4,19},{5,20},{6,21},{7,22},{8,23},{9,24},{10... | collective-permute-start | bytes 196616 | tf_op jit(solution)/shard_map/ppermute | solution.py:117
  31.5 3.0 %collective-permute-start.5 = (f32[49,16,128]{2,1,0:T(8,128)S(1)}, f32[49,16,128]{2,1,0:T(8,128)S(1)}, u32[]{:S(2)}, u32[]{:S(2)}) collective-permute-start(f32[49,16,128]{2,1,0:T(8,128)S(1)} %copy-done.5), channel_id=1, source_target_pairs={{0,1},{1,2},{2,3},{3,4},{4,5},{5,6},{6,7},{7,8},{8,9},{9,10},{10,1... | collective-permute-start | bytes 1204232 | tf_op jit(solution)/shard_map/ppermute | solution.py:97
  34.5 5.2 %collective-permute-start.6 = (f32[49,16,128]{2,1,0:T(8,128)S(1)}, f32[49,16,128]{2,1,0:T(8,128)S(1)}, u32[]{:S(2)}, u32[]{:S(2)}) collective-permute-start(f32[49,16,128]{2,1,0:T(8,128)S(1)} %copy-done.4), channel_id=1, source_target_pairs={{1,0},{2,1},{3,2},{4,3},{5,4},{6,5},{7,6},{8,7},{9,8},{10,9},{11,1... | collective-permute-start | bytes 1204232 | tf_op jit(solution)/shard_map/ppermute | solution.py:98
  39.9 3.9 %collective-permute-done.5 = f32[49,16,128]{2,1,0:T(8,128)S(1)} collective-permute-done((f32[49,16,128]{2,1,0:T(8,128)S(1)}, f32[49,16,128]{2,1,0:T(8,128)S(1)}, u32[]{:S(2)}, u32[]{:S(2)}) %collective-permute-start.5) | collective-permute-done | bytes 401440 | tf_op jit(solution)/shard_map/ppermute | solution.py:97
  44.1 0.8 collective-permute-done.6
  45.2 0.4 fusion.2
  45.5 0.3 multiply_add_fusion.5
  45.9 0.4 fusion.1
  46.3 0.3 multiply_add_fusion.3
  46.6 0.4 fusion
  47.0 0.3 multiply_add_fusion.1
  47.3 0.3 fusion.5
  48.0 0.3 fusion.4
  48.6 0.3 fusion.3
  49.5 0.3 add_subtract_fusion.3
  50.7 0.3 broadcast_multiply_fusion.11
  54.8 7.7 %collective-permute-start.7 = (f32[4,16,128]{2,1,0:T(8,128)S(1)}, f32[4,16,128]{2,1,0:T(8,128)S(1)}, u32[]{:S(2)}, u32[]{:S(2)}) collective-permute-start(f32[4,16,128]{2,1,0:T(8,128)S(1)} %get-tuple-element.220), channel_id=1, source_target_pairs={{0,113},{1,114},{2,115},{3,116},{4,117},{5,118},{6,119},{7,120},{8... | collective-permute-start | bytes 98312 | tf_op jit(solution)/shard_map/ppermute | solution.py:115
  62.5 1.5 %collective-permute-start.8 = (f32[4,64,128]{2,1,0:T(8,128)S(1)}, f32[4,64,128]{2,1,0:T(8,128)S(1)}, u32[]{:S(2)}, u32[]{:S(2)}) collective-permute-start(f32[4,64,128]{2,1,0:T(8,128)S(1)} %slice.2333), channel_id=1, source_target_pairs={{16,0},{32,16},{48,32},{64,48},{80,64},{96,80},{112,96},{0,112},{1... | collective-permute-start | bytes 393224 | tf_op jit(solution)/shard_map/ppermute | solution.py:19
  65.0 2.2 %collective-permute-start.9 = (f32[4,16,128]{2,1,0:T(8,128)S(1)}, f32[4,16,128]{2,1,0:T(8,128)S(1)}, u32[]{:S(2)}, u32[]{:S(2)}) collective-permute-start(f32[4,16,128]{2,1,0:T(8,128)S(1)} %get-tuple-element.219), channel_id=1, source_target_pairs={{1,112},{2,113},{3,114},{4,115},{5,116},{6,117},{7,118},{8,119},{9... | collective-permute-start | bytes 98312 | tf_op jit(solution)/shard_map/ppermute | solution.py:117
  67.2 0.6 collective-permute-done.8
  67.8 2.9 %collective-permute-done.9 = f32[4,16,128]{2,1,0:T(8,128)S(1)} collective-permute-done((f32[4,16,128]{2,1,0:T(8,128)S(1)}, f32[4,16,128]{2,1,0:T(8,128)S(1)}, u32[]{:S(2)}, u32[]{:S(2)}) %collective-permute-start.9) | collective-permute-done | bytes 32800 | tf_op jit(solution)/shard_map/ppermute | solution.py:117
  76.2 1.3 %multiply_add_fusion = f32[8,2,4,64,128]{4,3,2,1,0:T(8,128)S(1)} fusion(f32[4,64,128]{2,1,0:T(8,128)S(1)} %slice.2356, f32[8,2]{1,0:T(8,128)S(1)} %mul.3331, f32[4,64,128]{2,1,0:T(8,128)S(1)} %slice.2354, f32[8,2]{1,0:T(8,128)S(1)} %mul.3327, f32[4,64,128]{2,1,0:T(8,128)S(1)} %slice.2352, f32[8,2]{1,0:T(8,128)S(1)} %mul.3323, f32[4,64,128]{2,1,0:T(8,128)S(1)} %slice-done, ...), kind=kLoop, calls=%fused_computation.1 | loop fusion | flops 7864320 | bytes 3146240 | tf_op jit(solution)/shard_map/add | solution.py:175
  77.5 32.9 %all_to_all.5 = f32[8,2,4,64,128]{4,3,2,1,0:T(8,128)S(1)} all-to-all(f32[8,2,4,64,128]{4,3,2,1,0:T(8,128)S(1)} %multiply_add_fusion), channel_id=1, replica_groups=mesh['slab'=8,'tile'=16] {'slab'}, dimensions={0} | all-to-all | bytes 4194304 | tf_op jit(solution)/shard_map/all_to_all | solution.py:176
  110.3 0.8 reduce_sum.9
  (163 shorter events, 17.2 us)
Async XLA Ops:
  1.6 9.3 %copy-start.6 = (s32[8]{0:T(128)S(1)}, s32[8]{0:T(128)}, u32[]{:S(2)}) copy-start(s32[8]{0:T(128)} %param.7) | copy-start | bytes 100
  1.6 14.5 %copy-start = (f32[8,4,64,128]{3,2,1,0:T(8,128)S(1)}, f32[8,4,64,128]{3,2,1,0:T(8,128)}, u32[]{:S(2)}) copy-start(f32[8,4,64,128]{3,2,1,0:T(8,128)} %param.5) | copy-start | bytes 3145732
  1.6 14.5 %copy-start.1 = (f32[2,8,64,128]{3,2,1,0:T(8,128)S(1)}, f32[2,8,64,128]{3,2,1,0:T(8,128)}, u32[]{:S(2)}) copy-start(f32[2,8,64,128]{3,2,1,0:T(8,128)} %param.4) | copy-start | bytes 1572868
  1.6 14.5 %copy-start.2 = (f32[64,128]{1,0:T(8,128)S(1)}, f32[64,128]{1,0:T(8,128)}, u32[]{:S(2)}) copy-start(f32[64,128]{1,0:T(8,128)} %param.6) | copy-start | bytes 98308
  2.7 11.8 %collective-permute-start = (f32[49,16,128]{2,1,0:T(8,128)}, f32[49,16,128]{2,1,0:T(8,128)S(1)}, u32[]{:S(2)}, u32[]{:S(2)}) collective-permute-start(f32[49,16,128]{2,1,0:T(8,128)} %get-tuple-element.148), channel_id=1, source_target_pairs={{0,1},{1,2},{2,3},{3,4},{4,5},{5,6},{6,7},{7,8},{8,9},{9,10},{10,1... | collective-permute-start | bytes 1204232 | tf_op jit(solution)/shard_map/ppermute | solution.py:92
  4.6 11.5 %collective-permute-start.1 = (f32[49,16,128]{2,1,0:T(8,128)S(1)}, f32[49,16,128]{2,1,0:T(8,128)S(1)}, u32[]{:S(2)}, u32[]{:S(2)}) collective-permute-start(f32[49,16,128]{2,1,0:T(8,128)S(1)} %get-tuple-element.147), channel_id=1, source_target_pairs={{1,0},{2,1},{3,2},{4,3},{5,4},{6,5},{7,6},{8,7},{9,8},{10,9},{11,1... | collective-permute-start | bytes 1204232 | tf_op jit(solution)/shard_map/ppermute | solution.py:93
  20.2 11.4 %copy-start.5 = (f32[49,16,128]{2,1,0:T(8,128)S(1)}, f32[49,16,128]{2,1,0:T(8,128)}, u32[]{:S(2)}) copy-start(f32[49,16,128]{2,1,0:T(8,128)} %get-tuple-element.11) | copy-start | bytes 1204228
  20.2 14.3 %copy-start.4 = (f32[49,16,128]{2,1,0:T(8,128)S(1)}, f32[49,16,128]{2,1,0:T(8,128)}, u32[]{:S(2)}) copy-start(f32[49,16,128]{2,1,0:T(8,128)} %get-tuple-element.12) | copy-start | bytes 1204228
  20.7 19.1 %collective-permute-start.2 = (f32[4,32,128]{2,1,0:T(8,128)S(1)}, f32[4,32,128]{2,1,0:T(8,128)S(1)}, u32[]{:S(2)}, u32[]{:S(2)}) collective-permute-start(f32[4,32,128]{2,1,0:T(8,128)S(1)} %get-tuple-element.222), channel_id=1, source_target_pairs={{0,17},{1,18},{2,19},{3,20},{4,21},{5,22},{6,23},{7,24},{8,25},{9,... | collective-permute-start | bytes 196616 | tf_op jit(solution)/shard_map/ppermute | solution.py:115
  26.9 12.9 %collective-permute-start.3 = (f32[4,64,128]{2,1,0:T(8,128)S(1)}, f32[4,64,128]{2,1,0:T(8,128)S(1)}, u32[]{:S(2)}, u32[]{:S(2)}) collective-permute-start(f32[4,64,128]{2,1,0:T(8,128)S(1)} %slice.2268), channel_id=1, source_target_pairs={{112,0},{0,16},{16,32},{32,48},{48,64},{64,80},{80,96},{96,112},{1... | collective-permute-start | bytes 393224 | tf_op jit(solution)/shard_map/ppermute | solution.py:19
  28.5 11.4 %collective-permute-start.4 = (f32[4,32,128]{2,1,0:T(8,128)S(1)}, f32[4,32,128]{2,1,0:T(8,128)S(1)}, u32[]{:S(2)}, u32[]{:S(2)}) collective-permute-start(f32[4,32,128]{2,1,0:T(8,128)S(1)} %get-tuple-element.221), channel_id=1, source_target_pairs={{1,16},{2,17},{3,18},{4,19},{5,20},{6,21},{7,22},{8,23},{9,24},{10... | collective-permute-start | bytes 196616 | tf_op jit(solution)/shard_map/ppermute | solution.py:117
  31.5 12.3 %collective-permute-start.5 = (f32[49,16,128]{2,1,0:T(8,128)S(1)}, f32[49,16,128]{2,1,0:T(8,128)S(1)}, u32[]{:S(2)}, u32[]{:S(2)}) collective-permute-start(f32[49,16,128]{2,1,0:T(8,128)S(1)} %copy-done.5), channel_id=1, source_target_pairs={{0,1},{1,2},{2,3},{3,4},{4,5},{5,6},{6,7},{7,8},{8,9},{9,10},{10,1... | collective-permute-start | bytes 1204232 | tf_op jit(solution)/shard_map/ppermute | solution.py:97
  34.5 10.4 %collective-permute-start.6 = (f32[49,16,128]{2,1,0:T(8,128)S(1)}, f32[49,16,128]{2,1,0:T(8,128)S(1)}, u32[]{:S(2)}, u32[]{:S(2)}) collective-permute-start(f32[49,16,128]{2,1,0:T(8,128)S(1)} %copy-done.4), channel_id=1, source_target_pairs={{1,0},{2,1},{3,2},{4,3},{5,4},{6,5},{7,6},{8,7},{9,8},{10,9},{11,1... | collective-permute-start | bytes 1204232 | tf_op jit(solution)/shard_map/ppermute | solution.py:98
  54.8 12.4 %collective-permute-start.7 = (f32[4,16,128]{2,1,0:T(8,128)S(1)}, f32[4,16,128]{2,1,0:T(8,128)S(1)}, u32[]{:S(2)}, u32[]{:S(2)}) collective-permute-start(f32[4,16,128]{2,1,0:T(8,128)S(1)} %get-tuple-element.220), channel_id=1, source_target_pairs={{0,113},{1,114},{2,115},{3,116},{4,117},{5,118},{6,119},{7,120},{8... | collective-permute-start | bytes 98312 | tf_op jit(solution)/shard_map/ppermute | solution.py:115
  62.5 5.3 %collective-permute-start.8 = (f32[4,64,128]{2,1,0:T(8,128)S(1)}, f32[4,64,128]{2,1,0:T(8,128)S(1)}, u32[]{:S(2)}, u32[]{:S(2)}) collective-permute-start(f32[4,64,128]{2,1,0:T(8,128)S(1)} %slice.2333), channel_id=1, source_target_pairs={{16,0},{32,16},{48,32},{64,48},{80,64},{96,80},{112,96},{0,112},{1... | collective-permute-start | bytes 393224 | tf_op jit(solution)/shard_map/ppermute | solution.py:19
  65.0 5.7 %collective-permute-start.9 = (f32[4,16,128]{2,1,0:T(8,128)S(1)}, f32[4,16,128]{2,1,0:T(8,128)S(1)}, u32[]{:S(2)}, u32[]{:S(2)}) collective-permute-start(f32[4,16,128]{2,1,0:T(8,128)S(1)} %get-tuple-element.219), channel_id=1, source_target_pairs={{1,112},{2,113},{3,114},{4,115},{5,116},{6,117},{7,118},{8,119},{9... | collective-permute-start | bytes 98312 | tf_op jit(solution)/shard_map/ppermute | solution.py:117
  73.4 1.3 %copy-start.3 = (f32[4,96,128]{2,1,0:T(8,128)}, f32[4,96,128]{2,1,0:T(8,128)S(1)}, u32[]{:S(2)}) copy-start(f32[4,96,128]{2,1,0:T(8,128)S(1)} %fusion.154) | copy-start | bytes 589828
  75.2 0.9 slice-start

commit v10 on v9

--- a/solution.py
+++ b/solution.py
@@ -89,10 +89,21 @@
     near = band(2 * steps)
     tile_down = [(i, i + 1) for i in range(tiles - 1)]
     tile_up = [(i + 1, i) for i in range(tiles - 1)]
-    before = lax.ppermute(packed[:, rows - near :], "tile", tile_down)
-    after = lax.ppermute(packed[:, :near], "tile", tile_up)
+
+    def rows_of(lo, hi):
+        return jnp.concatenate(
+            [
+                base_flow[:, :, lo:hi].reshape(2 * steps, hi - lo, columns),
+                forcing[:, :, lo:hi].reshape(steps * count_f, hi - lo, columns),
+                damping[None, lo:hi],
+            ],
+            axis=0,
+        )
+
+    before = lax.ppermute(rows_of(rows - near, rows), "tile", tile_down)
+    after = lax.ppermute(rows_of(0, near), "tile", tile_up)
     (far_down, far_up), (before, after) = lax.optimization_barrier(
-        ((packed[:, rows - far : rows - near], packed[:, near:far]), (before, after))
+        ((rows_of(rows - far, rows - near), rows_of(near, far)), (before, after))
     )
     before_far = lax.ppermute(far_down, "tile", tile_down)
     after_far = lax.ppermute(far_up, "tile", tile_up)

time: 113 us -> 110 us (0.973)
  waiting for transfers between devices: 13.2 us -> 11.2 us
    ppermute x2, starting transfers between devices: 13.9 us -> 11.5 us  [slab_start(): lax.ppermute(own[:, rows - depth:], both, [(j * tiles + t, onward(j, t +...]
    ppermute x2, starting transfers between devices: 5.19 us -> 7.44 us  [slab_start(): lax.ppermute(own[:, :depth], both, [(j * tiles + t + 1, onward(j, t)) for...]
    ppermute x2, waiting for transfers between devices: 2.87 us -> 1.31 us  [slab_start(): lax.ppermute(own[:, :depth], both, [(j * tiles + t + 1, onward(j, t)) for...]
  transfers between devices with their start and end apart: 10 -> 10, of which waited for: 6 -> 5; matrix products, arithmetic and copies ran while one was open for 2% -> 2% of each run, Pallas kernels for 0% -> 0%
where the time goes in v10:
time: 110 us; the launch traced here: 109 us
  starting transfers between devices  38.1 us (35%)
  blocking collectives  32.8 us (30%)
  other arithmetic  22.8 us (21%)
  waiting for transfers between devices  11.2 us (10%)
  local copies, waits for them, and re-layouts  3.14 us (3%)
  between operations  1.16 us (1%)
    all_to_all x1, blocking collectives, whole(): lax.all_to_all(terms.reshape(slabs, 2 * H // slabs, count_f, rows, column...  32.8 us
    ppermute x2, starting transfers between devices, slab_start(): lax.ppermute(own[:, rows - depth:], both, [(j * tiles + t, onward(j, t +...  11.5 us
    mul x28, other arithmetic, adjoint_rate(): flux_y = pad_grid(speed_y * state)  7.48 us
    ppermute x2, starting transfers between devices, slab_start(): lax.ppermute(own[:, :depth], both, [(j * tiles + t + 1, onward(j, t)) for...  7.44 us
    ppermute x1, starting transfers between devices, whole(): after_far = lax.ppermute(far_up, 'tile', tile_up)  6.11 us
    ppermute x1, starting transfers between devices, whole(): after = lax.ppermute(rows_of(0, near), 'tile', tile_up)  6.03 us
    add x14, other arithmetic, whole(): state + first  4.1 us
    add x16, other arithmetic, whole(): state = state + 0.5 * (first + second)  4.01 us
  transfers between devices with their start and end apart: 10, of which 5 were waited for; matrix products, arithmetic and copies ran while one was open for 2% of the time, Pallas kernels for 0%

profile of v10, /device:TPU:16, one launch (start us, length us, event | category | flops | bytes accessed | tf_op | source)
XLA Modules:
  0.0 109.1 jit_solution(2426301216489471806)
XLA Ops:
  0.0 1.4 %fusion.573 = (f32[8,4,16,128]{3,2,1,0:T(8,128)S(1)}, f32[8,4,16,128]{3,2,1,0:T(8,128)S(1)}, f32[8,4,16,128]{3,2,1,0:T(8,128)S(1)}, f32[8,4,16,128]{3,2,1,0:T(8,128)S(1)}) fusion(f32[8,4,64,128]{3,2,1,0:T(8,128)} %param.5), kind=kLoop, calls=%fused_computation.1164 | loop fusion | bytes 2097152 | tf_op jit(solution)/shard_map/slice | solution.py:97
  1.5 0.8 pad_maximum_fusion.3
  2.3 1.9 %collective-permute-start = (f32[49,16,128]{2,1,0:T(8,128)}, f32[49,16,128]{2,1,0:T(8,128)S(1)}, u32[]{:S(2)}, u32[]{:S(2)}) collective-permute-start(f32[49,16,128]{2,1,0:T(8,128)} %pad_maximum_fusion.3), channel_id=1, source_target_pairs={{0,1},{1,2},{2,3},{3,4},{4,5},{5,6},{6,7},{7,8},{8,9},{9,10},{10,1... | collective-permute-start | bytes 1204232 | tf_op jit(solution)/shard_map/ppermute | solution.py:103
  4.2 0.8 pad_maximum_fusion.4
  5.0 6.0 %collective-permute-start.1 = (f32[49,16,128]{2,1,0:T(8,128)}, f32[49,16,128]{2,1,0:T(8,128)S(1)}, u32[]{:S(2)}, u32[]{:S(2)}) collective-permute-start(f32[49,16,128]{2,1,0:T(8,128)} %pad_maximum_fusion.4), channel_id=1, source_target_pairs={{1,0},{2,1},{3,2},{4,3},{5,4},{6,5},{7,6},{8,7},{9,8},{10,9},{11,1... | collective-permute-start | bytes 1204232 | tf_op jit(solution)/shard_map/ppermute | solution.py:104
  11.5 2.6 %collective-permute-done = f32[49,16,128]{2,1,0:T(8,128)S(1)} collective-permute-done((f32[49,16,128]{2,1,0:T(8,128)}, f32[49,16,128]{2,1,0:T(8,128)S(1)}, u32[]{:S(2)}, u32[]{:S(2)}) %collective-permute-start) | collective-permute-done | bytes 401440 | tf_op jit(solution)/shard_map/ppermute | solution.py:103
  14.1 2.6 %collective-permute-done.1 = f32[49,16,128]{2,1,0:T(8,128)S(1)} collective-permute-done((f32[49,16,128]{2,1,0:T(8,128)}, f32[49,16,128]{2,1,0:T(8,128)S(1)}, u32[]{:S(2)}, u32[]{:S(2)}) %collective-permute-start.1) | collective-permute-done | bytes 401440 | tf_op jit(solution)/shard_map/ppermute | solution.py:104
  21.3 6.2 %collective-permute-start.2 = (f32[4,32,128]{2,1,0:T(8,128)S(1)}, f32[4,32,128]{2,1,0:T(8,128)S(1)}, u32[]{:S(2)}, u32[]{:S(2)}) collective-permute-start(f32[4,32,128]{2,1,0:T(8,128)S(1)} %get-tuple-element.226), channel_id=1, source_target_pairs={{0,17},{1,18},{2,19},{3,20},{4,21},{5,22},{6,23},{7,24},{8,25},{9,... | collective-permute-start | bytes 196616 | tf_op jit(solution)/shard_map/ppermute | solution.py:126
  27.5 1.6 %collective-permute-start.3 = (f32[4,64,128]{2,1,0:T(8,128)S(1)}, f32[4,64,128]{2,1,0:T(8,128)S(1)}, u32[]{:S(2)}, u32[]{:S(2)}) collective-permute-start(f32[4,64,128]{2,1,0:T(8,128)S(1)} %slice.2296), channel_id=1, source_target_pairs={{112,0},{0,16},{16,32},{32,48},{48,64},{64,80},{80,96},{96,112},{1... | collective-permute-start | bytes 393224 | tf_op jit(solution)/shard_map/ppermute | solution.py:19
  29.0 3.1 %collective-permute-start.4 = (f32[4,32,128]{2,1,0:T(8,128)S(1)}, f32[4,32,128]{2,1,0:T(8,128)S(1)}, u32[]{:S(2)}, u32[]{:S(2)}) collective-permute-start(f32[4,32,128]{2,1,0:T(8,128)S(1)} %get-tuple-element.225), channel_id=1, source_target_pairs={{1,16},{2,17},{3,18},{4,19},{5,20},{6,21},{7,22},{8,23},{9,24},{10... | collective-permute-start | bytes 196616 | tf_op jit(solution)/shard_map/ppermute | solution.py:128
  32.1 2.0 %collective-permute-start.5 = (f32[49,16,128]{2,1,0:T(8,128)S(1)}, f32[49,16,128]{2,1,0:T(8,128)S(1)}, u32[]{:S(2)}, u32[]{:S(2)}) collective-permute-start(f32[49,16,128]{2,1,0:T(8,128)S(1)} %get-tuple-element.11), channel_id=1, source_target_pairs={{0,1},{1,2},{2,3},{3,4},{4,5},{5,6},{6,7},{7,8},{8,9},{9,10},{10,1... | collective-permute-start | bytes 1204232 | tf_op jit(solution)/shard_map/ppermute | solution.py:108
  34.2 6.1 %collective-permute-start.6 = (f32[49,16,128]{2,1,0:T(8,128)S(1)}, f32[49,16,128]{2,1,0:T(8,128)S(1)}, u32[]{:S(2)}, u32[]{:S(2)}) collective-permute-start(f32[49,16,128]{2,1,0:T(8,128)S(1)} %get-tuple-element.12), channel_id=1, source_target_pairs={{1,0},{2,1},{3,2},{4,3},{5,4},{6,5},{7,6},{8,7},{9,8},{10,9},{11,1... | collective-permute-start | bytes 1204232 | tf_op jit(solution)/shard_map/ppermute | solution.py:109
  40.5 3.3 %collective-permute-done.5 = f32[49,16,128]{2,1,0:T(8,128)S(1)} collective-permute-done((f32[49,16,128]{2,1,0:T(8,128)S(1)}, f32[49,16,128]{2,1,0:T(8,128)S(1)}, u32[]{:S(2)}, u32[]{:S(2)}) %collective-permute-start.5) | collective-permute-done | bytes 401440 | tf_op jit(solution)/shard_map/ppermute | solution.py:108
  44.2 1.3 %collective-permute-done.6 = f32[49,16,128]{2,1,0:T(8,128)S(1)} collective-permute-done((f32[49,16,128]{2,1,0:T(8,128)S(1)}, f32[49,16,128]{2,1,0:T(8,128)S(1)}, u32[]{:S(2)}, u32[]{:S(2)}) %collective-permute-start.6) | collective-permute-done | bytes 401440 | tf_op jit(solution)/shard_map/ppermute | solution.py:109
  45.7 0.4 fusion.2
  46.1 0.3 multiply_add_fusion.5
  46.4 0.4 fusion.1
  46.8 0.3 multiply_add_fusion.3
  47.1 0.4 fusion
  47.5 0.3 multiply_add_fusion.1
  47.9 0.3 fusion.5
  48.5 0.3 fusion.4
  49.1 0.3 fusion.3
  50.0 0.3 add_subtract_fusion.3
  51.2 0.3 broadcast_multiply_fusion.11
  55.4 5.3 %collective-permute-start.7 = (f32[4,16,128]{2,1,0:T(8,128)S(1)}, f32[4,16,128]{2,1,0:T(8,128)S(1)}, u32[]{:S(2)}, u32[]{:S(2)}) collective-permute-start(f32[4,16,128]{2,1,0:T(8,128)S(1)} %get-tuple-element.224), channel_id=1, source_target_pairs={{0,113},{1,114},{2,115},{3,116},{4,117},{5,118},{6,119},{7,120},{8... | collective-permute-start | bytes 98312 | tf_op jit(solution)/shard_map/ppermute | solution.py:126
  60.7 1.5 %collective-permute-start.8 = (f32[4,64,128]{2,1,0:T(8,128)S(1)}, f32[4,64,128]{2,1,0:T(8,128)S(1)}, u32[]{:S(2)}, u32[]{:S(2)}) collective-permute-start(f32[4,64,128]{2,1,0:T(8,128)S(1)} %slice.2361), channel_id=1, source_target_pairs={{16,0},{32,16},{48,32},{64,48},{80,64},{96,80},{112,96},{0,112},{1... | collective-permute-start | bytes 393224 | tf_op jit(solution)/shard_map/ppermute | solution.py:19
  63.2 4.4 %collective-permute-start.9 = (f32[4,16,128]{2,1,0:T(8,128)S(1)}, f32[4,16,128]{2,1,0:T(8,128)S(1)}, u32[]{:S(2)}, u32[]{:S(2)}) collective-permute-start(f32[4,16,128]{2,1,0:T(8,128)S(1)} %get-tuple-element.223), channel_id=1, source_target_pairs={{1,112},{2,113},{3,114},{4,115},{5,116},{6,117},{7,118},{8,119},{9... | collective-permute-start | bytes 98312 | tf_op jit(solution)/shard_map/ppermute | solution.py:128
  67.6 1.3 %collective-permute-done.9 = f32[4,16,128]{2,1,0:T(8,128)S(1)} collective-permute-done((f32[4,16,128]{2,1,0:T(8,128)S(1)}, f32[4,16,128]{2,1,0:T(8,128)S(1)}, u32[]{:S(2)}, u32[]{:S(2)}) %collective-permute-start.9) | collective-permute-done | bytes 32800 | tf_op jit(solution)/shard_map/ppermute | solution.py:128
  74.2 1.3 %multiply_add_fusion = f32[8,2,4,64,128]{4,3,2,1,0:T(8,128)S(1)} fusion(f32[4,64,128]{2,1,0:T(8,128)S(1)} %slice.2384, f32[8,2]{1,0:T(8,128)S(1)} %mul.3331, f32[4,64,128]{2,1,0:T(8,128)S(1)} %slice.2382, f32[8,2]{1,0:T(8,128)S(1)} %mul.3327, f32[4,64,128]{2,1,0:T(8,128)S(1)} %slice.2380, f32[8,2]{1,0:T(8,128)S(1)} %mul.3323, f32[4,64,128]{2,1,0:T(8,128)S(1)} %slice-done, ...), kind=kLoop, calls=%fused_computation.1 | loop fusion | flops 7864320 | bytes 3146240 | tf_op jit(solution)/shard_map/add | solution.py:186
  75.5 32.8 %all_to_all.5 = f32[8,2,4,64,128]{4,3,2,1,0:T(8,128)S(1)} all-to-all(f32[8,2,4,64,128]{4,3,2,1,0:T(8,128)S(1)} %multiply_add_fusion), channel_id=1, replica_groups=mesh['slab'=8,'tile'=16] {'slab'}, dimensions={0} | all-to-all | bytes 4194304 | tf_op jit(solution)/shard_map/all_to_all | solution.py:187
  108.3 0.8 reduce_sum.9
  (164 shorter events, 17.2 us)
Async XLA Ops:
  0.0 1.4 %copy-start.1 = (f32[2,8,64,128]{3,2,1,0:T(8,128)S(1)}, f32[2,8,64,128]{3,2,1,0:T(8,128)}, u32[]{:S(2)}) copy-start(f32[2,8,64,128]{3,2,1,0:T(8,128)} %param.4) | copy-start | bytes 1572868
  0.0 1.4 %copy-start.2 = (f32[64,128]{1,0:T(8,128)S(1)}, f32[64,128]{1,0:T(8,128)}, u32[]{:S(2)}) copy-start(f32[64,128]{1,0:T(8,128)} %param.6) | copy-start | bytes 98308
  0.0 11.3 %copy-start.4 = (s32[8]{0:T(128)S(1)}, s32[8]{0:T(128)}, u32[]{:S(2)}) copy-start(s32[8]{0:T(128)} %param.7) | copy-start | bytes 100
  1.4 15.3 %copy-start = (f32[8,4,64,128]{3,2,1,0:T(8,128)S(1)}, f32[8,4,64,128]{3,2,1,0:T(8,128)}, u32[]{:S(2)}) copy-start(f32[8,4,64,128]{3,2,1,0:T(8,128)} %param.5) | copy-start | bytes 3145732
  2.3 11.8 %collective-permute-start = (f32[49,16,128]{2,1,0:T(8,128)}, f32[49,16,128]{2,1,0:T(8,128)S(1)}, u32[]{:S(2)}, u32[]{:S(2)}) collective-permute-start(f32[49,16,128]{2,1,0:T(8,128)} %pad_maximum_fusion.3), channel_id=1, source_target_pairs={{0,1},{1,2},{2,3},{3,4},{4,5},{5,6},{6,7},{7,8},{8,9},{9,10},{10,1... | collective-permute-start | bytes 1204232 | tf_op jit(solution)/shard_map/ppermute | solution.py:103
  5.0 11.7 %collective-permute-start.1 = (f32[49,16,128]{2,1,0:T(8,128)}, f32[49,16,128]{2,1,0:T(8,128)S(1)}, u32[]{:S(2)}, u32[]{:S(2)}) collective-permute-start(f32[49,16,128]{2,1,0:T(8,128)} %pad_maximum_fusion.4), channel_id=1, source_target_pairs={{1,0},{2,1},{3,2},{4,3},{5,4},{6,5},{7,6},{8,7},{9,8},{10,9},{11,1... | collective-permute-start | bytes 1204232 | tf_op jit(solution)/shard_map/ppermute | solution.py:104
  21.3 19.1 %collective-permute-start.2 = (f32[4,32,128]{2,1,0:T(8,128)S(1)}, f32[4,32,128]{2,1,0:T(8,128)S(1)}, u32[]{:S(2)}, u32[]{:S(2)}) collective-permute-start(f32[4,32,128]{2,1,0:T(8,128)S(1)} %get-tuple-element.226), channel_id=1, source_target_pairs={{0,17},{1,18},{2,19},{3,20},{4,21},{5,22},{6,23},{7,24},{8,25},{9,... | collective-permute-start | bytes 196616 | tf_op jit(solution)/shard_map/ppermute | solution.py:126
  27.5 13.0 %collective-permute-start.3 = (f32[4,64,128]{2,1,0:T(8,128)S(1)}, f32[4,64,128]{2,1,0:T(8,128)S(1)}, u32[]{:S(2)}, u32[]{:S(2)}) collective-permute-start(f32[4,64,128]{2,1,0:T(8,128)S(1)} %slice.2296), channel_id=1, source_target_pairs={{112,0},{0,16},{16,32},{32,48},{48,64},{64,80},{80,96},{96,112},{1... | collective-permute-start | bytes 393224 | tf_op jit(solution)/shard_map/ppermute | solution.py:19
  29.0 11.4 %collective-permute-start.4 = (f32[4,32,128]{2,1,0:T(8,128)S(1)}, f32[4,32,128]{2,1,0:T(8,128)S(1)}, u32[]{:S(2)}, u32[]{:S(2)}) collective-permute-start(f32[4,32,128]{2,1,0:T(8,128)S(1)} %get-tuple-element.225), channel_id=1, source_target_pairs={{1,16},{2,17},{3,18},{4,19},{5,20},{6,21},{7,22},{8,23},{9,24},{10... | collective-permute-start | bytes 196616 | tf_op jit(solution)/shard_map/ppermute | solution.py:128
  32.1 11.7 %collective-permute-start.5 = (f32[49,16,128]{2,1,0:T(8,128)S(1)}, f32[49,16,128]{2,1,0:T(8,128)S(1)}, u32[]{:S(2)}, u32[]{:S(2)}) collective-permute-start(f32[49,16,128]{2,1,0:T(8,128)S(1)} %get-tuple-element.11), channel_id=1, source_target_pairs={{0,1},{1,2},{2,3},{3,4},{4,5},{5,6},{6,7},{7,8},{8,9},{9,10},{10,1... | collective-permute-start | bytes 1204232 | tf_op jit(solution)/shard_map/ppermute | solution.py:108
  34.2 11.3 %collective-permute-start.6 = (f32[49,16,128]{2,1,0:T(8,128)S(1)}, f32[49,16,128]{2,1,0:T(8,128)S(1)}, u32[]{:S(2)}, u32[]{:S(2)}) collective-permute-start(f32[49,16,128]{2,1,0:T(8,128)S(1)} %get-tuple-element.12), channel_id=1, source_target_pairs={{1,0},{2,1},{3,2},{4,3},{5,4},{6,5},{7,6},{8,7},{9,8},{10,9},{11,1... | collective-permute-start | bytes 1204232 | tf_op jit(solution)/shard_map/ppermute | solution.py:109
  55.4 12.2 %collective-permute-start.7 = (f32[4,16,128]{2,1,0:T(8,128)S(1)}, f32[4,16,128]{2,1,0:T(8,128)S(1)}, u32[]{:S(2)}, u32[]{:S(2)}) collective-permute-start(f32[4,16,128]{2,1,0:T(8,128)S(1)} %get-tuple-element.224), channel_id=1, source_target_pairs={{0,113},{1,114},{2,115},{3,116},{4,117},{5,118},{6,119},{7,120},{8... | collective-permute-start | bytes 98312 | tf_op jit(solution)/shard_map/ppermute | solution.py:126
  60.7 6.9 %collective-permute-start.8 = (f32[4,64,128]{2,1,0:T(8,128)S(1)}, f32[4,64,128]{2,1,0:T(8,128)S(1)}, u32[]{:S(2)}, u32[]{:S(2)}) collective-permute-start(f32[4,64,128]{2,1,0:T(8,128)S(1)} %slice.2361), channel_id=1, source_target_pairs={{16,0},{32,16},{48,32},{64,48},{80,64},{96,80},{112,96},{0,112},{1... | collective-permute-start | bytes 393224 | tf_op jit(solution)/shard_map/ppermute | solution.py:19
  63.2 5.7 %collective-permute-start.9 = (f32[4,16,128]{2,1,0:T(8,128)S(1)}, f32[4,16,128]{2,1,0:T(8,128)S(1)}, u32[]{:S(2)}, u32[]{:S(2)}) collective-permute-start(f32[4,16,128]{2,1,0:T(8,128)S(1)} %get-tuple-element.223), channel_id=1, source_target_pairs={{1,112},{2,113},{3,114},{4,115},{5,116},{6,117},{7,118},{8,119},{9... | collective-permute-start | bytes 98312 | tf_op jit(solution)/shard_map/ppermute | solution.py:128
  71.6 1.3 %copy-start.3 = (f32[4,96,128]{2,1,0:T(8,128)}, f32[4,96,128]{2,1,0:T(8,128)S(1)}, u32[]{:S(2)}) copy-start(f32[4,96,128]{2,1,0:T(8,128)S(1)} %fusion.154) | copy-start | bytes 589828
  73.2 1.0 slice-start
